TPU v7x, 1024 devices: a whole 4x8x16 slice. The times are simulated.
1024 devices in a mesh: grp: 2 (over y_lo), gx: 16 (over z), yz: 32 (over x, y_hi, core).
Axes of the slice: x: 4, y: 8 (y_hi: 4, y_lo: 2; y = y_hi * 2 + y_lo), z: 16, core: 2. Of those that a mesh axis runs over, the one named last changes fastest.
Arguments:
- rhs: float32 [48, 128, 8, 512], P('gx', 'yz', 'grp'), may hold values from -5 to 5
- coeff: float32 [48, 128, 8], P('gx', 'yz', 'grp'), may hold values from 0.5 to 2
- flags: int32 [48, 128, 8], P('gx', 'yz', 'grp'), may hold values 0 or 1
- basis: float32 [8, 8], replicated, may hold values from -1 to 1, as said below
- eigenvalues: float32 [8], replicated, may hold values from 0.2 to 4
Outputs:
- solution: float32 [48, 128, 8, 512], P('gx', 'yz', 'grp')
Inputs may be any that keep to these rules, and one draw needn't show every extreme that they name: basis is orthogonal: its transpose is its inverse.
All inputs are finite; a program needn't handle non-finite values. No bound on the sum of `flags` on one device may be relied on, other than what follows from the above.
Results may differ from a plain program's by a relative error of at most 0.0003.
Values sent between devices are 32-bit elements; how exact they have to be, the bound alone decides.
No kernel may reach another device: no remote copies, remote signals or barrier semaphores. Data moves between devices by JAX's collectives and lax.ppermute only.
A program may use at most 64 MiB of HBM per device.

v0:
```python
import jax
import jax.numpy as jnp
import numpy as np
from jax import lax
from jax.sharding import PartitionSpec as P

DEG1 = 8
ITERS = 2
CHEB = 4


PENALTY = 2.0
COARSE_PENALTY = 1.0
DAMPING = 0.5
CHEB_LOW = 0.1
CHEB_HIGH = 2.0
GLL_POINTS = (
    -1.0,
    -0.8717401485096066,
    -0.5917001814331423,
    -0.2092992179024789,
    0.2092992179024789,
    0.5917001814331423,
    0.8717401485096066,
    1.0,
)
HIGHEST = lax.Precision.HIGHEST


def with_halo(cells, sides, width):
    for axis, dim in sides:
        count = lax.axis_size(axis)
        ends = count - 1
        head = lax.slice_in_dim(cells, 0, width, axis=dim)
        tail = lax.slice_in_dim(cells, cells.shape[dim] - width, cells.shape[dim], axis=dim)
        cells = jnp.concatenate(
            [
                lax.ppermute(tail, axis, [(i, (i + 1) % count) for i in range(ends)]),
                cells,
                lax.ppermute(head, axis, [((i + 1) % count, i) for i in range(ends)]),
            ],
            axis=dim,
        )
    return cells


def build_tables(basis, eigenvalues):
    eigen_table = (
        basis[:, None, None, :, None, None]
        * basis[None, :, None, None, :, None]
        * basis[None, None, :, None, None, :]
    ).reshape(DEG1**3, DEG1**3)
    spectrum = (
        eigenvalues[:, None, None] + eigenvalues[None, :, None] + eigenvalues[None, None, :]
    ).reshape(-1)
    points = jnp.array(np.array(GLL_POINTS), jnp.float32)
    linear = jnp.stack([(1.0 - points) * 0.5, (1.0 + points) * 0.5])
    restrict_table = (
        linear.T[:, None, None, :, None, None]
        * linear.T[None, :, None, None, :, None]
        * linear.T[None, None, :, None, None, :]
    ).reshape(DEG1**3, 8)
    return (eigen_table, spectrum, restrict_table)


def eigen_apply(values, eigen_table, scale):
    flat = values.reshape(-1, eigen_table.shape[0])
    inside = jnp.dot(flat, eigen_table, precision=HIGHEST, preferred_element_type=jnp.float32)
    scaled = inside * scale.reshape(flat.shape)
    back = lax.dot_general(
        scaled,
        eigen_table,
        (((1,), (1,)), ((), ())),
        precision=HIGHEST,
        preferred_element_type=jnp.float32,
    )
    return back.reshape(values.shape)


def boundary_coefs(flag_values, starts, totals, penalty):
    result_list = []
    for dimension in range(3):
        position = starts[dimension] + lax.broadcasted_iota(jnp.int32, flag_values.shape, dimension)
        lower_coef = penalty * jnp.where(position > 0, 1.0, flag_values)
        upper_coef = penalty * jnp.where(position < totals[dimension] - 1, 1.0, flag_values)
        result_list.append((lower_coef[..., None, None, None], upper_coef[..., None, None, None]))
    return result_list


def neighbour_traces(padded, points):
    lower_list, upper_list = ([], [])
    for dimension in range(3):
        interior = [slice(1, -1)] * 3
        before_index = list(interior)
        before_index[dimension] = slice(0, -2)
        after_index = list(interior)
        after_index[dimension] = slice(2, None)
        lower_list.append(
            lax.slice_in_dim(padded[tuple(before_index)], points - 1, points, axis=3 + dimension)
        )
        upper_list.append(lax.slice_in_dim(padded[tuple(after_index)], 0, 1, axis=3 + dimension))
    return (lower_list, upper_list)


def face_term(field, lower_list, upper_list, coefs, penalty):
    summed = jnp.zeros_like(field)
    points = field.shape[3]
    for dimension in range(3):
        node_axis = 3 + dimension
        low_face = lax.slice_in_dim(field, 0, 1, axis=node_axis)
        high_face = lax.slice_in_dim(field, points - 1, points, axis=node_axis)
        lower_coef, upper_coef = coefs[dimension]
        low_term = lower_coef * low_face - penalty * lower_list[dimension]
        high_term = upper_coef * high_face - penalty * upper_list[dimension]
        low_pad = [(0, 0)] * 6
        low_pad[node_axis] = (0, points - 1)
        high_pad = [(0, 0)] * 6
        high_pad[node_axis] = (points - 1, 0)
        summed = summed + jnp.pad(low_term, low_pad) + jnp.pad(high_term, high_pad)
    return summed


def coarse_block(corners, coarse_coeff):
    weight = coarse_coeff[..., None, None, None]
    return weight * (
        3.5 * corners - jnp.flip(corners, 3) - jnp.flip(corners, 4) - jnp.flip(corners, 5)
    )


def chebyshev(coarse_rhs, coarse_coeff, apply_coarse):
    center = 0.5 * (CHEB_HIGH + CHEB_LOW)
    half_width = 0.5 * (CHEB_HIGH - CHEB_LOW)
    sigma_value = center / half_width
    rho_now = 1.0 / sigma_value
    inverse_diag = (1.0 / (coarse_coeff * 3.5 + 3.0 * COARSE_PENALTY))[..., None]
    remain = coarse_rhs
    update = inverse_diag * remain / center
    result = update
    for sweep_num in range(CHEB - 1):
        remain = remain - apply_coarse(update)
        rho_next = 1.0 / (2.0 * sigma_value - rho_now)
        update = rho_next * rho_now * update + 2.0 * rho_next / half_width * (inverse_diag * remain)
        result = result + update
        rho_now = rho_next
    return result


def body(rhs, coeff, flags, basis, eigenvalues):
    eigen_table, spectrum, restrict_table = build_tables(basis, eigenvalues)
    shape_three = rhs.shape[:3]
    node_count = rhs.shape[3]
    flag_values = flags.astype(jnp.float32)
    starts = (
        lax.axis_index("gx") * shape_three[0],
        lax.axis_index("yz") * shape_three[1],
        lax.axis_index("grp") * shape_three[2],
    )
    totals = (
        shape_three[0] * lax.axis_size("gx"),
        shape_three[1] * lax.axis_size("yz"),
        shape_three[2] * lax.axis_size("grp"),
    )
    fine_coefs = boundary_coefs(flag_values, starts, totals, PENALTY)
    block_scale = coeff[..., None] * spectrum
    inverse_scale = 1.0 / block_scale

    def apply_fine(solution):
        field = solution.reshape(shape_three + (DEG1, DEG1, DEG1))
        padded = with_halo(solution, (("gx", 0), ("yz", 1), ("grp", 2)), 1)
        padded = padded.reshape(padded.shape[:3] + (DEG1, DEG1, DEG1))
        lower_list, upper_list = neighbour_traces(padded, DEG1)
        faces = face_term(field, lower_list, upper_list, fine_coefs, PENALTY).reshape(
            solution.shape
        )
        return eigen_apply(solution, eigen_table, block_scale) + faces

    solution = jnp.zeros_like(rhs)
    for iteration in range(ITERS):
        residual = rhs if iteration == 0 else rhs - apply_fine(solution)
        smoothed = eigen_apply(residual, eigen_table, inverse_scale)
        coarse_rhs = jnp.dot(
            residual.reshape(-1, node_count),
            restrict_table,
            precision=HIGHEST,
            preferred_element_type=jnp.float32,
        ).reshape(shape_three + (8,))
        own_coefs = boundary_coefs(flag_values, starts, totals, COARSE_PENALTY)

        def apply_own(values):
            corners = values.reshape(values.shape[:3] + (2, 2, 2))
            padded = with_halo(corners, (("gx", 0), ("yz", 1), ("grp", 2)), 1)
            lower_list, upper_list = neighbour_traces(padded, 2)
            faces = face_term(corners, lower_list, upper_list, own_coefs, COARSE_PENALTY)
            return (coarse_block(corners, coeff) + faces).reshape(values.shape)

        coarse_sol = chebyshev(coarse_rhs, coeff, apply_own)
        lifted = lax.dot_general(
            coarse_sol.reshape(-1, 8),
            restrict_table,
            (((1,), (1,)), ((), ())),
            precision=HIGHEST,
            preferred_element_type=jnp.float32,
        ).reshape(rhs.shape)
        solution = solution + DAMPING * (smoothed + lifted)
    return solution


def solution(mesh):
    in_specs = (P("gx", "yz", "grp", None), P("gx", "yz", "grp"), P("gx", "yz", "grp"), P(), P())
    out_specs = P("gx", "yz", "grp", None)
    return jax.shard_map(body, mesh=mesh, in_specs=in_specs, out_specs=out_specs, check_vma=False)
```

profile of v0, /device:TPU:772, one launch (start us, length us, event | category | flops | bytes accessed | tf_op | source)
XLA Modules:
  0.0 262.4 jit_solution(10630246044815315283)
XLA Ops:
  10.8 8.7 %broadcast_multiply_fusion = f32[8,8,8,8,8,8]{5,4,3,2,1,0:T(8,128)} fusion(f32[8,8]{1,0:T(8,128)} %param.9, f32[8,8,8,8]{3,2,1,0:T(8,128)S(1)} %broadcast_multiply_fusion.2), kind=kLoop, calls=%fused_computation | loop fusion | flops 262144 | bytes 1065216 | tf_op jit(solution)/shard_map/mul | solution.py:49
  20.6 12.6 %mul.684 = f32[512,512]{1,0:T(8,128)S(1)} reshape(f32[8,8,8,8,8,8]{5,4,3,2,1,0:T(8,128)} %broadcast_multiply_fusion) | data formatting | bytes 2097152 | tf_op jit(solution)/shard_map/mul | solution.py:49
  33.5 5.0 %collective-permute-start.3 = (f32[5,1,4,2,2,2]{2,5,4,3,1,0:T(2,128)S(1)}, f32[5,1,4,2,2,2]{2,5,4,3,1,0:T(2,128)S(1)}, u32[]{:S(2)}, u32[]{:S(2)}) collective-permute-start(f32[5,1,4,2,2,2]{2,5,4,3,1,0:T(2,128)S(1)} %get-tuple-element.86), channel_id=1, source_target_pairs={{1,0},{2,1},{3,2},{4,3},{5,4},{6,5},{7,6},{8,7},{9,8},{10,9},{11,1... | collective-permute-start | bytes 1928 | tf_op jit(solution)/shard_map/ppermute | solution.py:40
  40.5 6.1 %collective-permute-done.2 = f32[5,1,4,2,2,2]{2,5,4,3,1,0:T(2,128)S(1)} collective-permute-done((f32[5,1,4,2,2,2]{2,5,4,3,1,0:T(2,128)S(1)}, f32[5,1,4,2,2,2]{2,5,4,3,1,0:T(2,128)S(1)}, u32[]{:S(2)}, u32[]{:S(2)}) %collective-permute-start.2) | collective-permute-done | bytes 672 | tf_op jit(solution)/shard_map/ppermute | solution.py:38
  51.9 4.4 %collective-permute-done.5 = f32[5,6,1,2,2,2]{2,5,4,3,1,0:T(2,128)S(1)} collective-permute-done((f32[5,6,1,2,2,2]{2,5,4,3,1,0:T(2,128)S(1)}, f32[5,6,1,2,2,2]{2,5,4,3,1,0:T(2,128)S(1)}, u32[]{:S(2)}, u32[]{:S(2)}) %collective-permute-start.5) | collective-permute-done | bytes 992 | tf_op jit(solution)/shard_map/ppermute | solution.py:40
  57.0 4.8 %collective-permute-start.7 = (f32[1,4,4,2,2,2]{2,5,4,3,1,0:T(2,128)S(1)}, f32[1,4,4,2,2,2]{2,5,4,3,1,0:T(2,128)S(1)}, u32[]{:S(2)}, u32[]{:S(2)}) collective-permute-start(f32[1,4,4,2,2,2]{2,5,4,3,1,0:T(2,128)S(1)} %bitcast.114), channel_id=1, source_target_pairs={{32,0},{64,32},{96,64},{128,96},{160,128},{192,160},{224,192},{256... | collective-permute-start | bytes 1544 | tf_op jit(solution)/shard_map/ppermute | solution.py:40
  64.7 12.6 %reshape.282 = f32[512,512,1,1]{1,0,2,3:T(8,128)S(1)} reshape(f32[8,8,8,8,8,8]{5,4,3,2,1,0:T(8,128)} %broadcast_multiply_fusion) | data formatting | bytes 2097152 | tf_op jit(solution)/shard_map/mul | solution.py:49
  81.9 5.6 %collective-permute-done.8 = f32[5,1,4,2,2,2]{2,5,4,3,1,0:T(2,128)S(1)} collective-permute-done((f32[5,1,4,2,2,2]{2,5,4,3,1,0:T(2,128)S(1)}, f32[5,1,4,2,2,2]{2,5,4,3,1,0:T(2,128)S(1)}, u32[]{:S(2)}, u32[]{:S(2)}) %collective-permute-start.8) | collective-permute-done | bytes 672 | tf_op jit(solution)/shard_map/ppermute | solution.py:38
  91.7 4.4 %collective-permute-done.11 = f32[5,6,1,2,2,2]{2,5,4,3,1,0:T(2,128)S(1)} collective-permute-done((f32[5,6,1,2,2,2]{2,5,4,3,1,0:T(2,128)S(1)}, f32[5,6,1,2,2,2]{2,5,4,3,1,0:T(2,128)S(1)}, u32[]{:S(2)}, u32[]{:S(2)}) %collective-permute-start.11) | collective-permute-done | bytes 992 | tf_op jit(solution)/shard_map/ppermute | solution.py:40
  96.9 5.1 %collective-permute-start.13 = (f32[1,4,4,2,2,2]{2,5,4,3,1,0:T(2,128)S(1)}, f32[1,4,4,2,2,2]{2,5,4,3,1,0:T(2,128)S(1)}, u32[]{:S(2)}, u32[]{:S(2)}) collective-permute-start(f32[1,4,4,2,2,2]{2,5,4,3,1,0:T(2,128)S(1)} %bitcast.111), channel_id=1, source_target_pairs={{32,0},{64,32},{96,64},{128,96},{160,128},{192,160},{224,192},{256... | collective-permute-start | bytes 1544 | tf_op jit(solution)/shard_map/ppermute | solution.py:40
  113.4 5.6 %collective-permute-done.14 = f32[5,1,4,2,2,2]{2,5,4,3,1,0:T(2,128)S(1)} collective-permute-done((f32[5,1,4,2,2,2]{2,5,4,3,1,0:T(2,128)S(1)}, f32[5,1,4,2,2,2]{2,5,4,3,1,0:T(2,128)S(1)}, u32[]{:S(2)}, u32[]{:S(2)}) %collective-permute-start.14) | collective-permute-done | bytes 672 | tf_op jit(solution)/shard_map/ppermute | solution.py:38
  123.2 4.4 %collective-permute-done.17 = f32[5,6,1,2,2,2]{2,5,4,3,1,0:T(2,128)S(1)} collective-permute-done((f32[5,6,1,2,2,2]{2,5,4,3,1,0:T(2,128)S(1)}, f32[5,6,1,2,2,2]{2,5,4,3,1,0:T(2,128)S(1)}, u32[]{:S(2)}, u32[]{:S(2)}) %collective-permute-start.17) | collective-permute-done | bytes 992 | tf_op jit(solution)/shard_map/ppermute | solution.py:40
  141.8 5.9 %collective-permute-done.20 = f32[5,1,4,512]{3,2,1,0:T(4,128)S(1)} collective-permute-done((f32[5,1,4,512]{3,2,1,0:T(4,128)S(1)}, f32[5,1,4,512]{3,2,1,0:T(4,128)S(1)}, u32[]{:S(2)}, u32[]{:S(2)}) %collective-permute-start.20) | collective-permute-done | bytes 40992 | tf_op jit(solution)/shard_map/ppermute | solution.py:38
  149.1 5.8 %collective-permute-start.22 = (f32[5,6,1,512]{3,2,1,0:T(1,128)S(1)}, f32[5,6,1,512]{3,2,1,0:T(1,128)}, u32[]{:S(2)}, u32[]{:S(2)}) collective-permute-start(f32[5,6,1,512]{3,2,1,0:T(1,128)S(1)} %get-tuple-element.33), channel_id=1, source_target_pairs={{0,512},{1,513},{2,514},{3,515},{4,516},{5,517},{6,518},{7,519},{8... | collective-permute-start | bytes 184328 | tf_op jit(solution)/shard_map/ppermute | solution.py:38
  157.5 4.8 %reshape.273 = f32[5,6,6,8,8,8]{5,4,3,2,1,0:T(8,128)} reshape(f32[5,6,6,512]{3,2,1,0:T(8,128)S(1)} %pad_maximum_fusion) | data formatting | bytes 737280 | tf_op jit(solution)/shard_map/reshape | solution.py:170
  176.8 3.9 %collective-permute-start.24 = (f32[1,4,4,2,2,2]{2,5,4,3,1,0:T(2,128)S(1)}, f32[1,4,4,2,2,2]{2,5,4,3,1,0:T(2,128)S(1)}, u32[]{:S(2)}, u32[]{:S(2)}) collective-permute-start(f32[1,4,4,2,2,2]{2,5,4,3,1,0:T(2,128)S(1)} %bitcast.120), channel_id=1, source_target_pairs={{0,32},{32,64},{64,96},{96,128},{128,160},{160,192},{192,224},{224... | collective-permute-start | bytes 1544 | tf_op jit(solution)/shard_map/ppermute | solution.py:38
  188.0 5.6 %collective-permute-done.26 = f32[5,1,4,2,2,2]{2,5,4,3,1,0:T(2,128)S(1)} collective-permute-done((f32[5,1,4,2,2,2]{2,5,4,3,1,0:T(2,128)S(1)}, f32[5,1,4,2,2,2]{2,5,4,3,1,0:T(2,128)S(1)}, u32[]{:S(2)}, u32[]{:S(2)}) %collective-permute-start.26) | collective-permute-done | bytes 672 | tf_op jit(solution)/shard_map/ppermute | solution.py:38
  193.9 4.0 %collective-permute-start.28 = (f32[5,6,1,2,2,2]{2,5,4,3,1,0:T(2,128)S(1)}, f32[5,6,1,2,2,2]{2,5,4,3,1,0:T(2,128)S(1)}, u32[]{:S(2)}, u32[]{:S(2)}) collective-permute-start(f32[5,6,1,2,2,2]{2,5,4,3,1,0:T(2,128)S(1)} %get-tuple-element.47), channel_id=1, source_target_pairs={{0,512},{1,513},{2,514},{3,515},{4,516},{5,517},{6,518},{7,519},{8... | collective-permute-start | bytes 2888 | tf_op jit(solution)/shard_map/ppermute | solution.py:38
  200.3 4.4 %collective-permute-done.29 = f32[5,6,1,2,2,2]{2,5,4,3,1,0:T(2,128)S(1)} collective-permute-done((f32[5,6,1,2,2,2]{2,5,4,3,1,0:T(2,128)S(1)}, f32[5,6,1,2,2,2]{2,5,4,3,1,0:T(2,128)S(1)}, u32[]{:S(2)}, u32[]{:S(2)}) %collective-permute-start.29) | collective-permute-done | bytes 992 | tf_op jit(solution)/shard_map/ppermute | solution.py:40
  207.4 3.9 %collective-permute-start.30 = (f32[1,4,4,2,2,2]{2,5,4,3,1,0:T(2,128)S(1)}, f32[1,4,4,2,2,2]{2,5,4,3,1,0:T(2,128)S(1)}, u32[]{:S(2)}, u32[]{:S(2)}) collective-permute-start(f32[1,4,4,2,2,2]{2,5,4,3,1,0:T(2,128)S(1)} %bitcast.115), channel_id=1, source_target_pairs={{0,32},{32,64},{64,96},{96,128},{128,160},{160,192},{192,224},{224... | collective-permute-start | bytes 1544 | tf_op jit(solution)/shard_map/ppermute | solution.py:38
  218.6 5.6 %collective-permute-done.32 = f32[5,1,4,2,2,2]{2,5,4,3,1,0:T(2,128)S(1)} collective-permute-done((f32[5,1,4,2,2,2]{2,5,4,3,1,0:T(2,128)S(1)}, f32[5,1,4,2,2,2]{2,5,4,3,1,0:T(2,128)S(1)}, u32[]{:S(2)}, u32[]{:S(2)}) %collective-permute-start.32) | collective-permute-done | bytes 672 | tf_op jit(solution)/shard_map/ppermute | solution.py:38
  228.5 4.4 %collective-permute-done.35 = f32[5,6,1,2,2,2]{2,5,4,3,1,0:T(2,128)S(1)} collective-permute-done((f32[5,6,1,2,2,2]{2,5,4,3,1,0:T(2,128)S(1)}, f32[5,6,1,2,2,2]{2,5,4,3,1,0:T(2,128)S(1)}, u32[]{:S(2)}, u32[]{:S(2)}) %collective-permute-start.35) | collective-permute-done | bytes 992 | tf_op jit(solution)/shard_map/ppermute | solution.py:40
  246.8 5.6 %collective-permute-done.38 = f32[5,1,4,2,2,2]{2,5,4,3,1,0:T(2,128)S(1)} collective-permute-done((f32[5,1,4,2,2,2]{2,5,4,3,1,0:T(2,128)S(1)}, f32[5,1,4,2,2,2]{2,5,4,3,1,0:T(2,128)S(1)}, u32[]{:S(2)}, u32[]{:S(2)}) %collective-permute-start.38) | collective-permute-done | bytes 672 | tf_op jit(solution)/shard_map/ppermute | solution.py:38
  256.6 4.4 %collective-permute-done.41 = f32[5,6,1,2,2,2]{2,5,4,3,1,0:T(2,128)S(1)} collective-permute-done((f32[5,6,1,2,2,2]{2,5,4,3,1,0:T(2,128)S(1)}, f32[5,6,1,2,2,2]{2,5,4,3,1,0:T(2,128)S(1)}, u32[]{:S(2)}, u32[]{:S(2)}) %collective-permute-start.41) | collective-permute-done | bytes 992 | tf_op jit(solution)/shard_map/ppermute | solution.py:40
  (223 shorter events, 123.7 us)
Async XLA Ops:
  3.9 29.5 %collective-permute-start.1 = (f32[1,4,4,2,2,2]{2,5,4,3,1,0:T(2,128)S(1)}, f32[1,4,4,2,2,2]{2,5,4,3,1,0:T(2,128)S(1)}, u32[]{:S(2)}, u32[]{:S(2)}) collective-permute-start(f32[1,4,4,2,2,2]{2,5,4,3,1,0:T(2,128)S(1)} %bitcast.109), channel_id=1, source_target_pairs={{32,0},{64,32},{96,64},{128,96},{160,128},{192,160},{224,192},{256... | collective-permute-start | bytes 1544 | tf_op jit(solution)/shard_map/ppermute | solution.py:40
  7.6 25.8 %collective-permute-start = (f32[1,4,4,2,2,2]{2,5,4,3,1,0:T(2,128)S(1)}, f32[1,4,4,2,2,2]{2,5,4,3,1,0:T(2,128)S(1)}, u32[]{:S(2)}, u32[]{:S(2)}) collective-permute-start(f32[1,4,4,2,2,2]{2,5,4,3,1,0:T(2,128)S(1)} %bitcast.110), channel_id=1, source_target_pairs={{0,32},{32,64},{64,96},{96,128},{128,160},{160,192},{192,224},{224... | collective-permute-start | bytes 1544 | tf_op jit(solution)/shard_map/ppermute | solution.py:38
  33.5 7.0 %collective-permute-start.3 = (f32[5,1,4,2,2,2]{2,5,4,3,1,0:T(2,128)S(1)}, f32[5,1,4,2,2,2]{2,5,4,3,1,0:T(2,128)S(1)}, u32[]{:S(2)}, u32[]{:S(2)}) collective-permute-start(f32[5,1,4,2,2,2]{2,5,4,3,1,0:T(2,128)S(1)} %get-tuple-element.86), channel_id=1, source_target_pairs={{1,0},{2,1},{3,2},{4,3},{5,4},{6,5},{7,6},{8,7},{9,8},{10,9},{11,1... | collective-permute-start | bytes 1928 | tf_op jit(solution)/shard_map/ppermute | solution.py:40
  38.5 8.1 %collective-permute-start.2 = (f32[5,1,4,2,2,2]{2,5,4,3,1,0:T(2,128)S(1)}, f32[5,1,4,2,2,2]{2,5,4,3,1,0:T(2,128)S(1)}, u32[]{:S(2)}, u32[]{:S(2)}) collective-permute-start(f32[5,1,4,2,2,2]{2,5,4,3,1,0:T(2,128)S(1)} %get-tuple-element.85), channel_id=1, source_target_pairs={{0,1},{1,2},{2,3},{3,4},{4,5},{5,6},{6,7},{7,8},{8,9},{9,10},{10,1... | collective-permute-start | bytes 1928 | tf_op jit(solution)/shard_map/ppermute | solution.py:38
  57.0 20.4 %collective-permute-start.7 = (f32[1,4,4,2,2,2]{2,5,4,3,1,0:T(2,128)S(1)}, f32[1,4,4,2,2,2]{2,5,4,3,1,0:T(2,128)S(1)}, u32[]{:S(2)}, u32[]{:S(2)}) collective-permute-start(f32[1,4,4,2,2,2]{2,5,4,3,1,0:T(2,128)S(1)} %bitcast.114), channel_id=1, source_target_pairs={{32,0},{64,32},{96,64},{128,96},{160,128},{192,160},{224,192},{256... | collective-permute-start | bytes 1544 | tf_op jit(solution)/shard_map/ppermute | solution.py:40
  62.0 15.5 %collective-permute-start.6 = (f32[1,4,4,2,2,2]{2,5,4,3,1,0:T(2,128)S(1)}, f32[1,4,4,2,2,2]{2,5,4,3,1,0:T(2,128)S(1)}, u32[]{:S(2)}, u32[]{:S(2)}) collective-permute-start(f32[1,4,4,2,2,2]{2,5,4,3,1,0:T(2,128)S(1)} %bitcast.117), channel_id=1, source_target_pairs={{0,32},{32,64},{64,96},{96,128},{128,160},{160,192},{192,224},{224... | collective-permute-start | bytes 1544 | tf_op jit(solution)/shard_map/ppermute | solution.py:38
  79.4 8.1 %collective-permute-start.8 = (f32[5,1,4,2,2,2]{2,5,4,3,1,0:T(2,128)S(1)}, f32[5,1,4,2,2,2]{2,5,4,3,1,0:T(2,128)S(1)}, u32[]{:S(2)}, u32[]{:S(2)}) collective-permute-start(f32[5,1,4,2,2,2]{2,5,4,3,1,0:T(2,128)S(1)} %get-tuple-element.81), channel_id=1, source_target_pairs={{0,1},{1,2},{2,3},{3,4},{4,5},{5,6},{6,7},{7,8},{8,9},{9,10},{10,1... | collective-permute-start | bytes 1928 | tf_op jit(solution)/shard_map/ppermute | solution.py:38
  89.3 6.8 %collective-permute-start.11 = (f32[5,6,1,2,2,2]{2,5,4,3,1,0:T(2,128)S(1)}, f32[5,6,1,2,2,2]{2,5,4,3,1,0:T(2,128)S(1)}, u32[]{:S(2)}, u32[]{:S(2)}) collective-permute-start(f32[5,6,1,2,2,2]{2,5,4,3,1,0:T(2,128)S(1)} %get-tuple-element.56), channel_id=1, source_target_pairs={{512,0},{513,1},{514,2},{515,3},{516,4},{517,5},{518,6},{519,7},{5... | collective-permute-start | bytes 2888 | tf_op jit(solution)/shard_map/ppermute | solution.py:40
  96.9 8.9 %collective-permute-start.13 = (f32[1,4,4,2,2,2]{2,5,4,3,1,0:T(2,128)S(1)}, f32[1,4,4,2,2,2]{2,5,4,3,1,0:T(2,128)S(1)}, u32[]{:S(2)}, u32[]{:S(2)}) collective-permute-start(f32[1,4,4,2,2,2]{2,5,4,3,1,0:T(2,128)S(1)} %bitcast.111), channel_id=1, source_target_pairs={{32,0},{64,32},{96,64},{128,96},{160,128},{192,160},{224,192},{256... | collective-permute-start | bytes 1544 | tf_op jit(solution)/shard_map/ppermute | solution.py:40
  102.1 6.8 %collective-permute-start.12 = (f32[1,4,4,2,2,2]{2,5,4,3,1,0:T(2,128)S(1)}, f32[1,4,4,2,2,2]{2,5,4,3,1,0:T(2,128)S(1)}, u32[]{:S(2)}, u32[]{:S(2)}) collective-permute-start(f32[1,4,4,2,2,2]{2,5,4,3,1,0:T(2,128)S(1)} %bitcast.112), channel_id=1, source_target_pairs={{0,32},{32,64},{64,96},{96,128},{128,160},{160,192},{192,224},{224... | collective-permute-start | bytes 1544 | tf_op jit(solution)/shard_map/ppermute | solution.py:38
  110.9 8.1 %collective-permute-start.14 = (f32[5,1,4,2,2,2]{2,5,4,3,1,0:T(2,128)S(1)}, f32[5,1,4,2,2,2]{2,5,4,3,1,0:T(2,128)S(1)}, u32[]{:S(2)}, u32[]{:S(2)}) collective-permute-start(f32[5,1,4,2,2,2]{2,5,4,3,1,0:T(2,128)S(1)} %get-tuple-element.77), channel_id=1, source_target_pairs={{0,1},{1,2},{2,3},{3,4},{4,5},{5,6},{6,7},{7,8},{8,9},{9,10},{10,1... | collective-permute-start | bytes 1928 | tf_op jit(solution)/shard_map/ppermute | solution.py:38
  130.4 7.0 %collective-permute-start.18 = (f32[1,4,4,512]{3,2,1,0:T(4,128)S(1)}, f32[1,4,4,512]{3,2,1,0:T(4,128)S(1)}, u32[]{:S(2)}, u32[]{:S(2)}) collective-permute-start(f32[1,4,4,512]{3,2,1,0:T(4,128)S(1)} %get-tuple-element.61), channel_id=1, source_target_pairs={{0,32},{32,64},{64,96},{96,128},{128,160},{160,192},{192,224},{224... | collective-permute-start | bytes 98312 | tf_op jit(solution)/shard_map/ppermute | solution.py:38
  139.3 8.3 %collective-permute-start.20 = (f32[5,1,4,512]{3,2,1,0:T(4,128)S(1)}, f32[5,1,4,512]{3,2,1,0:T(4,128)S(1)}, u32[]{:S(2)}, u32[]{:S(2)}) collective-permute-start(f32[5,1,4,512]{3,2,1,0:T(4,128)S(1)} %get-tuple-element.35), channel_id=1, source_target_pairs={{0,1},{1,2},{2,3},{3,4},{4,5},{5,6},{6,7},{7,8},{8,9},{9,10},{10,1... | collective-permute-start | bytes 122888 | tf_op jit(solution)/shard_map/ppermute | solution.py:38
  147.8 8.7 %collective-permute-start.23 = (f32[5,6,1,512]{3,2,1,0:T(1,128)S(1)}, f32[5,6,1,512]{3,2,1,0:T(1,128)}, u32[]{:S(2)}, u32[]{:S(2)}) collective-permute-start(f32[5,6,1,512]{3,2,1,0:T(1,128)S(1)} %get-tuple-element.34), channel_id=1, source_target_pairs={{512,0},{513,1},{514,2},{515,3},{516,4},{517,5},{518,6},{519,7},{5... | collective-permute-start | bytes 184328 | tf_op jit(solution)/shard_map/ppermute | solution.py:40
  149.1 7.4 %collective-permute-start.22 = (f32[5,6,1,512]{3,2,1,0:T(1,128)S(1)}, f32[5,6,1,512]{3,2,1,0:T(1,128)}, u32[]{:S(2)}, u32[]{:S(2)}) collective-permute-start(f32[5,6,1,512]{3,2,1,0:T(1,128)S(1)} %get-tuple-element.33), channel_id=1, source_target_pairs={{0,512},{1,513},{2,514},{3,515},{4,516},{5,517},{6,518},{7,519},{8... | collective-permute-start | bytes 184328 | tf_op jit(solution)/shard_map/ppermute | solution.py:38
  176.8 6.8 %collective-permute-start.24 = (f32[1,4,4,2,2,2]{2,5,4,3,1,0:T(2,128)S(1)}, f32[1,4,4,2,2,2]{2,5,4,3,1,0:T(2,128)S(1)}, u32[]{:S(2)}, u32[]{:S(2)}) collective-permute-start(f32[1,4,4,2,2,2]{2,5,4,3,1,0:T(2,128)S(1)} %bitcast.120), channel_id=1, source_target_pairs={{0,32},{32,64},{64,96},{96,128},{128,160},{160,192},{192,224},{224... | collective-permute-start | bytes 1544 | tf_op jit(solution)/shard_map/ppermute | solution.py:38
  185.5 8.1 %collective-permute-start.26 = (f32[5,1,4,2,2,2]{2,5,4,3,1,0:T(2,128)S(1)}, f32[5,1,4,2,2,2]{2,5,4,3,1,0:T(2,128)S(1)}, u32[]{:S(2)}, u32[]{:S(2)}) collective-permute-start(f32[5,1,4,2,2,2]{2,5,4,3,1,0:T(2,128)S(1)} %get-tuple-element.73), channel_id=1, source_target_pairs={{0,1},{1,2},{2,3},{3,4},{4,5},{5,6},{6,7},{7,8},{8,9},{9,10},{10,1... | collective-permute-start | bytes 1928 | tf_op jit(solution)/shard_map/ppermute | solution.py:38
  197.9 6.8 %collective-permute-start.29 = (f32[5,6,1,2,2,2]{2,5,4,3,1,0:T(2,128)S(1)}, f32[5,6,1,2,2,2]{2,5,4,3,1,0:T(2,128)S(1)}, u32[]{:S(2)}, u32[]{:S(2)}) collective-permute-start(f32[5,6,1,2,2,2]{2,5,4,3,1,0:T(2,128)S(1)} %get-tuple-element.48), channel_id=1, source_target_pairs={{512,0},{513,1},{514,2},{515,3},{516,4},{517,5},{518,6},{519,7},{5... | collective-permute-start | bytes 2888 | tf_op jit(solution)/shard_map/ppermute | solution.py:40
  205.4 7.0 %collective-permute-start.31 = (f32[1,4,4,2,2,2]{2,5,4,3,1,0:T(2,128)S(1)}, f32[1,4,4,2,2,2]{2,5,4,3,1,0:T(2,128)S(1)}, u32[]{:S(2)}, u32[]{:S(2)}) collective-permute-start(f32[1,4,4,2,2,2]{2,5,4,3,1,0:T(2,128)S(1)} %bitcast.113), channel_id=1, source_target_pairs={{32,0},{64,32},{96,64},{128,96},{160,128},{192,160},{224,192},{256... | collective-permute-start | bytes 1544 | tf_op jit(solution)/shard_map/ppermute | solution.py:40
  207.4 6.8 %collective-permute-start.30 = (f32[1,4,4,2,2,2]{2,5,4,3,1,0:T(2,128)S(1)}, f32[1,4,4,2,2,2]{2,5,4,3,1,0:T(2,128)S(1)}, u32[]{:S(2)}, u32[]{:S(2)}) collective-permute-start(f32[1,4,4,2,2,2]{2,5,4,3,1,0:T(2,128)S(1)} %bitcast.115), channel_id=1, source_target_pairs={{0,32},{32,64},{64,96},{96,128},{128,160},{160,192},{192,224},{224... | collective-permute-start | bytes 1544 | tf_op jit(solution)/shard_map/ppermute | solution.py:38
  216.2 8.1 %collective-permute-start.32 = (f32[5,1,4,2,2,2]{2,5,4,3,1,0:T(2,128)S(1)}, f32[5,1,4,2,2,2]{2,5,4,3,1,0:T(2,128)S(1)}, u32[]{:S(2)}, u32[]{:S(2)}) collective-permute-start(f32[5,1,4,2,2,2]{2,5,4,3,1,0:T(2,128)S(1)} %get-tuple-element.69), channel_id=1, source_target_pairs={{0,1},{1,2},{2,3},{3,4},{4,5},{5,6},{6,7},{7,8},{8,9},{9,10},{10,1... | collective-permute-start | bytes 1928 | tf_op jit(solution)/shard_map/ppermute | solution.py:38
  233.5 7.4 %collective-permute-start.37 = (f32[1,4,4,2,2,2]{2,5,4,3,1,0:T(2,128)S(1)}, f32[1,4,4,2,2,2]{2,5,4,3,1,0:T(2,128)S(1)}, u32[]{:S(2)}, u32[]{:S(2)}) collective-permute-start(f32[1,4,4,2,2,2]{2,5,4,3,1,0:T(2,128)S(1)} %bitcast.116), channel_id=1, source_target_pairs={{32,0},{64,32},{96,64},{128,96},{160,128},{192,160},{224,192},{256... | collective-permute-start | bytes 1544 | tf_op jit(solution)/shard_map/ppermute | solution.py:40
  235.5 6.8 %collective-permute-start.36 = (f32[1,4,4,2,2,2]{2,5,4,3,1,0:T(2,128)S(1)}, f32[1,4,4,2,2,2]{2,5,4,3,1,0:T(2,128)S(1)}, u32[]{:S(2)}, u32[]{:S(2)}) collective-permute-start(f32[1,4,4,2,2,2]{2,5,4,3,1,0:T(2,128)S(1)} %bitcast.119), channel_id=1, source_target_pairs={{0,32},{32,64},{64,96},{96,128},{128,160},{160,192},{192,224},{224... | collective-permute-start | bytes 1544 | tf_op jit(solution)/shard_map/ppermute | solution.py:38
  244.3 8.1 %collective-permute-start.38 = (f32[5,1,4,2,2,2]{2,5,4,3,1,0:T(2,128)S(1)}, f32[5,1,4,2,2,2]{2,5,4,3,1,0:T(2,128)S(1)}, u32[]{:S(2)}, u32[]{:S(2)}) collective-permute-start(f32[5,1,4,2,2,2]{2,5,4,3,1,0:T(2,128)S(1)} %get-tuple-element.65), channel_id=1, source_target_pairs={{0,1},{1,2},{2,3},{3,4},{4,5},{5,6},{6,7},{7,8},{8,9},{9,10},{10,1... | collective-permute-start | bytes 1928 | tf_op jit(solution)/shard_map/ppermute | solution.py:38
  (32 other events, 295.5 us)
where the time goes:
time: 264 us; the launch traced here: 262 us
  starting transfers between devices  103 us (39%)
  waiting for transfers between devices  85 us (32%)
  local copies, waits for them, and re-layouts  39.6 us (15%)
  other arithmetic  26.1 us (10%)
  matrix products  7.29 us (3%)
    ppermute x21, waiting for transfers between devices, with_halo(): lax.ppermute(tail, axis, [(i, (i + 1) % count) for i in range(ends)])  58.9 us
    ppermute x21, starting transfers between devices, with_halo(): lax.ppermute(tail, axis, [(i, (i + 1) % count) for i in range(ends)])  56.2 us
    ppermute x21, starting transfers between devices, with_halo(): lax.ppermute(head, axis, [((i + 1) % count, i) for i in range(ends)])  47 us
    ppermute x21, waiting for transfers between devices, with_halo(): lax.ppermute(head, axis, [((i + 1) % count, i) for i in range(ends)])  26.2 us
    mul x2, local copies, waits for them, and re-layouts, build_tables(): basis[:, None, None, :, None, None] * basis[None, :, None, None, :, None]  25.2 us
    mul x2, other arithmetic, build_tables(): basis[:, None, None, :, None, None] * basis[None, :, None, None, :, None]  9.6 us
    sub x21, other arithmetic, face_term(): low_term = lower_coef * low_face - penalty * lower_list[dimension]  8.43 us
  transfers between devices with their start and end apart: 42, of which 24 were waited for; matrix products, arithmetic and copies ran while one was open for 17% of the time, Pallas kernels for 0%

commit v1 on v0

--- a/solution.py
+++ b/solution.py
@@ -27,29 +27,55 @@
 HIGHEST = lax.Precision.HIGHEST
 
 
-def with_halo(cells, sides, width):
-    for axis, dim in sides:
+def face_traces(field, points):
+    lower_list, upper_list = ([], [])
+    for dimension, axis in enumerate(("gx", "yz", "grp")):
         count = lax.axis_size(axis)
-        ends = count - 1
-        head = lax.slice_in_dim(cells, 0, width, axis=dim)
-        tail = lax.slice_in_dim(cells, cells.shape[dim] - width, cells.shape[dim], axis=dim)
-        cells = jnp.concatenate(
-            [
-                lax.ppermute(tail, axis, [(i, (i + 1) % count) for i in range(ends)]),
-                cells,
-                lax.ppermute(head, axis, [((i + 1) % count, i) for i in range(ends)]),
-            ],
-            axis=dim,
-        )
-    return cells
+        block = field.shape[dimension]
+        node_axis = 3 + dimension
+        high = lax.slice_in_dim(field, points - 1, points, axis=node_axis)
+        low = lax.slice_in_dim(field, 0, 1, axis=node_axis)
+        top = lax.slice_in_dim(high, block - 1, block, axis=dimension)
+        bottom = lax.slice_in_dim(low, 0, 1, axis=dimension)
+        if count == 2:
+            me = lax.axis_index(axis)
+            got = lax.ppermute(jnp.where(me == 0, top, bottom), axis, [(0, 1), (1, 0)])
+            zero = jnp.zeros_like(got)
+            from_below = jnp.where(me == 1, got, zero)
+            from_above = jnp.where(me == 0, got, zero)
+        else:
+            from_below = lax.ppermute(top, axis, [(i, i + 1) for i in range(count - 1)])
+            from_above = lax.ppermute(bottom, axis, [(i + 1, i) for i in range(count - 1)])
+        lower_list.append(
+            jnp.concatenate([from_below, lax.slice_in_dim(high, 0, block - 1, axis=dimension)], axis=dimension)
+        )
+        upper_list.append(
+            jnp.concatenate([lax.slice_in_dim(low, 1, block, axis=dimension), from_above], axis=dimension)
+        )
+    return (lower_list, upper_list)
+
+
+def _onehot_tables():
+    idx = np.arange(DEG1**3)
+    picks = [idx // (DEG1 * DEG1), (idx // DEG1) % DEG1, idx % DEG1]
+    return np.stack([(p[:, None] == np.arange(DEG1)[None, :]) for p in picks]).astype(np.float32)
+
+
+ONEHOT = _onehot_tables()
 
 
 def build_tables(basis, eigenvalues):
-    eigen_table = (
-        basis[:, None, None, :, None, None]
-        * basis[None, :, None, None, :, None]
-        * basis[None, None, :, None, None, :]
-    ).reshape(DEG1**3, DEG1**3)
+    eigen_table = None
+    for pick in ONEHOT:
+        pick = jnp.asarray(pick)
+        part = lax.dot_general(
+            jnp.dot(pick, basis, precision=HIGHEST, preferred_element_type=jnp.float32),
+            pick,
+            (((1,), (1,)), ((), ())),
+            precision=HIGHEST,
+            preferred_element_type=jnp.float32,
+        )
+        eigen_table = part if eigen_table is None else eigen_table * part
     spectrum = (
         eigenvalues[:, None, None] + eigenvalues[None, :, None] + eigenvalues[None, None, :]
     ).reshape(-1)
@@ -85,21 +111,6 @@
         upper_coef = penalty * jnp.where(position < totals[dimension] - 1, 1.0, flag_values)
         result_list.append((lower_coef[..., None, None, None], upper_coef[..., None, None, None]))
     return result_list
-
-
-def neighbour_traces(padded, points):
-    lower_list, upper_list = ([], [])
-    for dimension in range(3):
-        interior = [slice(1, -1)] * 3
-        before_index = list(interior)
-        before_index[dimension] = slice(0, -2)
-        after_index = list(interior)
-        after_index[dimension] = slice(2, None)
-        lower_list.append(
-            lax.slice_in_dim(padded[tuple(before_index)], points - 1, points, axis=3 + dimension)
-        )
-        upper_list.append(lax.slice_in_dim(padded[tuple(after_index)], 0, 1, axis=3 + dimension))
-    return (lower_list, upper_list)
 
 
 def face_term(field, lower_list, upper_list, coefs, penalty):
@@ -166,9 +177,7 @@
 
     def apply_fine(solution):
         field = solution.reshape(shape_three + (DEG1, DEG1, DEG1))
-        padded = with_halo(solution, (("gx", 0), ("yz", 1), ("grp", 2)), 1)
-        padded = padded.reshape(padded.shape[:3] + (DEG1, DEG1, DEG1))
-        lower_list, upper_list = neighbour_traces(padded, DEG1)
+        lower_list, upper_list = face_traces(field, DEG1)
         faces = face_term(field, lower_list, upper_list, fine_coefs, PENALTY).reshape(
             solution.shape
         )
@@ -188,8 +197,7 @@
 
         def apply_own(values):
             corners = values.reshape(values.shape[:3] + (2, 2, 2))
-            padded = with_halo(corners, (("gx", 0), ("yz", 1), ("grp", 2)), 1)
-            lower_list, upper_list = neighbour_traces(padded, 2)
+            lower_list, upper_list = face_traces(corners, 2)
             faces = face_term(corners, lower_list, upper_list, own_coefs, COARSE_PENALTY)
             return (coarse_block(corners, coeff) + faces).reshape(values.shape)
 

time: 264 us -> 233 us (0.88)
  the two profiles are of different devices: /device:TPU:772 before, /device:TPU:4 now
where the time goes in v1:
time: 233 us; the launch traced here: 231 us
  starting transfers between devices  121 us (52%)
  local copies, waits for them, and re-layouts  56.7 us (24%)
  waiting for transfers between devices  22.3 us (10%)
  other arithmetic  17.8 us (8%)
  matrix products  11.9 us (5%)
    ppermute x14, starting transfers between devices, face_traces(): lax.ppermute(bottom, axis, [(i + 1, i) for i in range(count - 1)])  51 us
    ppermute x14, starting transfers between devices, face_traces(): from_below = lax.ppermute(top, axis, [(i, i + 1) for i in range(count - 1)])  48.9 us
    ppermute x14, waiting for transfers between devices, face_traces(): lax.ppermute(bottom, axis, [(i + 1, i) for i in range(count - 1)])  22.2 us
    ppermute x7, starting transfers between devices, face_traces(): got = lax.ppermute(jnp.where(me == 0, top, bottom), axis, [(0, 1), (1, 0)])  21 us
    unnamed x94, local copies, waits for them, and re-layouts  21 us
    slice x22, local copies, waits for them, and re-layouts, face_traces(): lax.slice_in_dim(high, 0, block - 1, axis=dimension)  8.11 us
  transfers between devices with their start and end apart: 35, of which 5 were waited for; matrix products, arithmetic and copies ran while one was open for 24% of the time, Pallas kernels for 0%

profile of v1, /device:TPU:4, one launch (start us, length us, event | category | flops | bytes accessed | tf_op | source)
XLA Modules:
  0.0 231.2 jit_solution(2893452395470218472)
XLA Ops:
  9.4 6.7 %collective-permute-start.3 = (f32[3,1,4,2,1,2]{2,5,4,3,1,0:T(2,128)S(1)}, f32[3,1,4,2,1,2]{2,5,4,3,1,0:T(2,128)S(1)}, u32[]{:S(2)}, u32[]{:S(2)}) collective-permute-start(f32[3,1,4,2,1,2]{2,5,4,3,1,0:T(2,128)S(1)} %get-tuple-element.134), channel_id=1, source_target_pairs={{1,0},{2,1},{3,2},{4,3},{5,4},{6,5},{7,6},{8,7},{9,8},{10,9},{11,1... | collective-permute-start | bytes 584 | tf_op jit(solution)/shard_map/ppermute | solution.py:48
  16.1 4.3 %collective-permute-start = (f32[1,4,4,1,2,2]{2,5,4,3,1,0:T(2,128)S(1)}, f32[1,4,4,1,2,2]{2,5,4,3,1,0:T(2,128)S(1)}, u32[]{:S(2)}, u32[]{:S(2)}) collective-permute-start(f32[1,4,4,1,2,2]{2,5,4,3,1,0:T(2,128)S(1)} %get-tuple-element.127), channel_id=1, source_target_pairs={{0,32},{32,64},{64,96},{96,128},{128,160},{160,192},{192,224},{224... | collective-permute-start | bytes 776 | tf_op jit(solution)/shard_map/ppermute | solution.py:47
  35.6 6.7 %collective-permute-start.8 = (f32[3,1,4,2,1,2]{2,5,4,3,1,0:T(2,128)S(1)}, f32[3,1,4,2,1,2]{2,5,4,3,1,0:T(2,128)S(1)}, u32[]{:S(2)}, u32[]{:S(2)}) collective-permute-start(f32[3,1,4,2,1,2]{2,5,4,3,1,0:T(2,128)S(1)} %get-tuple-element.118), channel_id=1, source_target_pairs={{1,0},{2,1},{3,2},{4,3},{5,4},{6,5},{7,6},{8,7},{9,8},{10,9},{11,1... | collective-permute-start | bytes 584 | tf_op jit(solution)/shard_map/ppermute | solution.py:48
  42.2 4.9 %collective-permute-start.5 = (f32[1,4,4,1,2,2]{2,5,4,3,1,0:T(2,128)S(1)}, f32[1,4,4,1,2,2]{2,5,4,3,1,0:T(2,128)S(1)}, u32[]{:S(2)}, u32[]{:S(2)}) collective-permute-start(f32[1,4,4,1,2,2]{2,5,4,3,1,0:T(2,128)S(1)} %get-tuple-element.111), channel_id=1, source_target_pairs={{0,32},{32,64},{64,96},{96,128},{128,160},{160,192},{192,224},{224... | collective-permute-start | bytes 776 | tf_op jit(solution)/shard_map/ppermute | solution.py:47
  48.9 4.2 %collective-permute-done.6 = f32[1,4,4,1,2,2]{2,5,4,3,1,0:T(2,128)S(1)} collective-permute-done((f32[1,4,4,1,2,2]{2,5,4,3,1,0:T(2,128)S(1)}, f32[1,4,4,1,2,2]{2,5,4,3,1,0:T(2,128)S(1)}, u32[]{:S(2)}, u32[]{:S(2)}) %collective-permute-start.6) | collective-permute-done | bytes 288 | tf_op jit(solution)/shard_map/ppermute | solution.py:48
  59.2 6.7 %collective-permute-start.13 = (f32[3,1,4,2,1,2]{2,5,4,3,1,0:T(2,128)S(1)}, f32[3,1,4,2,1,2]{2,5,4,3,1,0:T(2,128)S(1)}, u32[]{:S(2)}, u32[]{:S(2)}) collective-permute-start(f32[3,1,4,2,1,2]{2,5,4,3,1,0:T(2,128)S(1)} %get-tuple-element.102), channel_id=1, source_target_pairs={{1,0},{2,1},{3,2},{4,3},{5,4},{6,5},{7,6},{8,7},{9,8},{10,9},{11,1... | collective-permute-start | bytes 584 | tf_op jit(solution)/shard_map/ppermute | solution.py:48
  65.8 5.5 %collective-permute-start.10 = (f32[1,4,4,1,2,2]{2,5,4,3,1,0:T(2,128)S(1)}, f32[1,4,4,1,2,2]{2,5,4,3,1,0:T(2,128)S(1)}, u32[]{:S(2)}, u32[]{:S(2)}) collective-permute-start(f32[1,4,4,1,2,2]{2,5,4,3,1,0:T(2,128)S(1)} %get-tuple-element.95), channel_id=1, source_target_pairs={{0,32},{32,64},{64,96},{96,128},{128,160},{160,192},{192,224},{224... | collective-permute-start | bytes 776 | tf_op jit(solution)/shard_map/ppermute | solution.py:47
  73.3 4.8 %collective-permute-done.11 = f32[1,4,4,1,2,2]{2,5,4,3,1,0:T(2,128)S(1)} collective-permute-done((f32[1,4,4,1,2,2]{2,5,4,3,1,0:T(2,128)S(1)}, f32[1,4,4,1,2,2]{2,5,4,3,1,0:T(2,128)S(1)}, u32[]{:S(2)}, u32[]{:S(2)}) %collective-permute-start.11) | collective-permute-done | bytes 288 | tf_op jit(solution)/shard_map/ppermute | solution.py:48
  95.2 3.7 %copy.235 = f32[3,4,3,8,8,1]{4,3,5,2,1,0:T(8,128)} copy(f32[3,4,3,8,8,1]{5,4,3,2,1,0:T(8,128)} %get-tuple-element.40) | data formatting | bytes 18432 | tf_op jit(solution)/shard_map/slice | solution.py:53
  98.8 4.5 %copy.254 = f32[3,4,4,8,8,1]{4,3,5,2,1,0:T(8,128)} copy(f32[3,4,4,8,8,1]{5,4,3,2,1,0:T(8,128)} %get-tuple-element.38) | data formatting | bytes 24576
  103.3 3.7 %copy.233 = f32[3,4,3,8,8,1]{4,3,5,2,1,0:T(8,128)} copy(f32[3,4,3,8,8,1]{5,4,3,2,1,0:T(8,128)} %get-tuple-element.39) | data formatting | bytes 18432 | tf_op jit(solution)/shard_map/slice | solution.py:50
  126.9 6.4 %collective-permute-start.15 = (f32[1,4,4,1,8,8]{4,3,5,2,1,0:T(1,128)}, f32[1,4,4,1,8,8]{4,3,5,2,1,0:T(1,128)}, u32[]{:S(2)}, u32[]{:S(2)}) collective-permute-start(f32[1,4,4,1,8,8]{4,3,5,2,1,0:T(1,128)} %copy.246), channel_id=1, source_target_pairs={{0,32},{32,64},{64,96},{96,128},{128,160},{160,192},{192,224},{224... | collective-permute-start | bytes 12296 | tf_op jit(solution)/shard_map/ppermute | solution.py:47
  138.7 4.4 %copy.230 = f32[3,4,4,8,1,8]{4,3,5,2,1,0:T(8,128)} copy(f32[3,4,4,8,1,8]{5,3,4,2,1,0:T(8,128)} %maximum_multiply_fusion.3) | data formatting | bytes 24576 | tf_op jit(solution)/shard_map/mul | solution.py:125
  160.9 3.5 %collective-permute-start.24 = (f32[3,4,1,2,2,1]{2,5,4,3,1,0:T(1,128)S(1)}, f32[3,4,1,2,2,1]{2,5,4,3,1,0:T(1,128)S(1)}, u32[]{:S(2)}, u32[]{:S(2)}) collective-permute-start(f32[3,4,1,2,2,1]{2,5,4,3,1,0:T(1,128)S(1)} %broadcast_select_fusion.7), channel_id=1, source_target_pairs={{0,512},{512,0},{1,513},{513,1},{2,514},{514,2},{3,515},{515,3},{4... | collective-permute-start | bytes 584 | tf_op jit(solution)/shard_map/ppermute | solution.py:42
  166.4 6.7 %collective-permute-start.23 = (f32[3,1,4,2,1,2]{2,5,4,3,1,0:T(2,128)S(1)}, f32[3,1,4,2,1,2]{2,5,4,3,1,0:T(2,128)S(1)}, u32[]{:S(2)}, u32[]{:S(2)}) collective-permute-start(f32[3,1,4,2,1,2]{2,5,4,3,1,0:T(2,128)S(1)} %get-tuple-element.86), channel_id=1, source_target_pairs={{1,0},{2,1},{3,2},{4,3},{5,4},{6,5},{7,6},{8,7},{9,8},{10,9},{11,1... | collective-permute-start | bytes 584 | tf_op jit(solution)/shard_map/ppermute | solution.py:48
  173.0 3.5 %collective-permute-start.20 = (f32[1,4,4,1,2,2]{2,5,4,3,1,0:T(2,128)S(1)}, f32[1,4,4,1,2,2]{2,5,4,3,1,0:T(2,128)S(1)}, u32[]{:S(2)}, u32[]{:S(2)}) collective-permute-start(f32[1,4,4,1,2,2]{2,5,4,3,1,0:T(2,128)S(1)} %get-tuple-element.79), channel_id=1, source_target_pairs={{0,32},{32,64},{64,96},{96,128},{128,160},{160,192},{192,224},{224... | collective-permute-start | bytes 776 | tf_op jit(solution)/shard_map/ppermute | solution.py:47
  178.2 4.1 %collective-permute-done.21 = f32[1,4,4,1,2,2]{2,5,4,3,1,0:T(2,128)S(1)} collective-permute-done((f32[1,4,4,1,2,2]{2,5,4,3,1,0:T(2,128)S(1)}, f32[1,4,4,1,2,2]{2,5,4,3,1,0:T(2,128)S(1)}, u32[]{:S(2)}, u32[]{:S(2)}) %collective-permute-start.21) | collective-permute-done | bytes 288 | tf_op jit(solution)/shard_map/ppermute | solution.py:48
  187.6 6.7 %collective-permute-start.28 = (f32[3,1,4,2,1,2]{2,5,4,3,1,0:T(2,128)S(1)}, f32[3,1,4,2,1,2]{2,5,4,3,1,0:T(2,128)S(1)}, u32[]{:S(2)}, u32[]{:S(2)}) collective-permute-start(f32[3,1,4,2,1,2]{2,5,4,3,1,0:T(2,128)S(1)} %get-tuple-element.70), channel_id=1, source_target_pairs={{1,0},{2,1},{3,2},{4,3},{5,4},{6,5},{7,6},{8,7},{9,8},{10,9},{11,1... | collective-permute-start | bytes 584 | tf_op jit(solution)/shard_map/ppermute | solution.py:48
  194.3 5.1 %collective-permute-start.25 = (f32[1,4,4,1,2,2]{2,5,4,3,1,0:T(2,128)S(1)}, f32[1,4,4,1,2,2]{2,5,4,3,1,0:T(2,128)S(1)}, u32[]{:S(2)}, u32[]{:S(2)}) collective-permute-start(f32[1,4,4,1,2,2]{2,5,4,3,1,0:T(2,128)S(1)} %get-tuple-element.63), channel_id=1, source_target_pairs={{0,32},{32,64},{64,96},{96,128},{128,160},{160,192},{192,224},{224... | collective-permute-start | bytes 776 | tf_op jit(solution)/shard_map/ppermute | solution.py:47
  201.0 5.1 %collective-permute-done.26 = f32[1,4,4,1,2,2]{2,5,4,3,1,0:T(2,128)S(1)} collective-permute-done((f32[1,4,4,1,2,2]{2,5,4,3,1,0:T(2,128)S(1)}, f32[1,4,4,1,2,2]{2,5,4,3,1,0:T(2,128)S(1)}, u32[]{:S(2)}, u32[]{:S(2)}) %collective-permute-start.26) | collective-permute-done | bytes 288 | tf_op jit(solution)/shard_map/ppermute | solution.py:48
  207.2 3.5 %collective-permute-start.34 = (f32[3,4,1,2,2,1]{2,5,4,3,1,0:T(1,128)S(1)}, f32[3,4,1,2,2,1]{2,5,4,3,1,0:T(1,128)S(1)}, u32[]{:S(2)}, u32[]{:S(2)}) collective-permute-start(f32[3,4,1,2,2,1]{2,5,4,3,1,0:T(1,128)S(1)} %broadcast_select_fusion.3), channel_id=1, source_target_pairs={{0,512},{512,0},{1,513},{513,1},{2,514},{514,2},{3,515},{515,3},{4... | collective-permute-start | bytes 584 | tf_op jit(solution)/shard_map/ppermute | solution.py:42
  212.6 6.7 %collective-permute-start.33 = (f32[3,1,4,2,1,2]{2,5,4,3,1,0:T(2,128)S(1)}, f32[3,1,4,2,1,2]{2,5,4,3,1,0:T(2,128)S(1)}, u32[]{:S(2)}, u32[]{:S(2)}) collective-permute-start(f32[3,1,4,2,1,2]{2,5,4,3,1,0:T(2,128)S(1)} %get-tuple-element.54), channel_id=1, source_target_pairs={{1,0},{2,1},{3,2},{4,3},{5,4},{6,5},{7,6},{8,7},{9,8},{10,9},{11,1... | collective-permute-start | bytes 584 | tf_op jit(solution)/shard_map/ppermute | solution.py:48
  219.2 5.1 %collective-permute-start.30 = (f32[1,4,4,1,2,2]{2,5,4,3,1,0:T(2,128)S(1)}, f32[1,4,4,1,2,2]{2,5,4,3,1,0:T(2,128)S(1)}, u32[]{:S(2)}, u32[]{:S(2)}) collective-permute-start(f32[1,4,4,1,2,2]{2,5,4,3,1,0:T(2,128)S(1)} %get-tuple-element.47), channel_id=1, source_target_pairs={{0,32},{32,64},{64,96},{96,128},{128,160},{160,192},{192,224},{224... | collective-permute-start | bytes 776 | tf_op jit(solution)/shard_map/ppermute | solution.py:47
  226.0 3.9 %collective-permute-done.31 = f32[1,4,4,1,2,2]{2,5,4,3,1,0:T(2,128)S(1)} collective-permute-done((f32[1,4,4,1,2,2]{2,5,4,3,1,0:T(2,128)S(1)}, f32[1,4,4,1,2,2]{2,5,4,3,1,0:T(2,128)S(1)}, u32[]{:S(2)}, u32[]{:S(2)}) %collective-permute-start.31) | collective-permute-done | bytes 288 | tf_op jit(solution)/shard_map/ppermute | solution.py:48
  (295 shorter events, 109.5 us)
Async XLA Ops:
  4.0 26.2 %collective-permute-start.4 = (f32[3,4,1,2,2,1]{2,5,4,3,1,0:T(1,128)S(1)}, f32[3,4,1,2,2,1]{2,5,4,3,1,0:T(1,128)S(1)}, u32[]{:S(2)}, u32[]{:S(2)}) collective-permute-start(f32[3,4,1,2,2,1]{2,5,4,3,1,0:T(1,128)S(1)} %broadcast_select_fusion.13), channel_id=1, source_target_pairs={{0,512},{512,0},{1,513},{513,1},{2,514},{514,2},{3,515},{515,3},{4... | collective-permute-start | bytes 584 | tf_op jit(solution)/shard_map/ppermute | solution.py:42
  7.5 23.0 %collective-permute-start.2 = (f32[3,1,4,2,1,2]{2,5,4,3,1,0:T(2,128)S(1)}, f32[3,1,4,2,1,2]{2,5,4,3,1,0:T(2,128)S(1)}, u32[]{:S(2)}, u32[]{:S(2)}) collective-permute-start(f32[3,1,4,2,1,2]{2,5,4,3,1,0:T(2,128)S(1)} %get-tuple-element.133), channel_id=1, source_target_pairs={{0,1},{1,2},{2,3},{3,4},{4,5},{5,6},{6,7},{7,8},{8,9},{9,10},{10,1... | collective-permute-start | bytes 584 | tf_op jit(solution)/shard_map/ppermute | solution.py:47
  9.4 21.1 %collective-permute-start.3 = (f32[3,1,4,2,1,2]{2,5,4,3,1,0:T(2,128)S(1)}, f32[3,1,4,2,1,2]{2,5,4,3,1,0:T(2,128)S(1)}, u32[]{:S(2)}, u32[]{:S(2)}) collective-permute-start(f32[3,1,4,2,1,2]{2,5,4,3,1,0:T(2,128)S(1)} %get-tuple-element.134), channel_id=1, source_target_pairs={{1,0},{2,1},{3,2},{4,3},{5,4},{6,5},{7,6},{8,7},{9,8},{10,9},{11,1... | collective-permute-start | bytes 584 | tf_op jit(solution)/shard_map/ppermute | solution.py:48
  16.1 14.4 %collective-permute-start = (f32[1,4,4,1,2,2]{2,5,4,3,1,0:T(2,128)S(1)}, f32[1,4,4,1,2,2]{2,5,4,3,1,0:T(2,128)S(1)}, u32[]{:S(2)}, u32[]{:S(2)}) collective-permute-start(f32[1,4,4,1,2,2]{2,5,4,3,1,0:T(2,128)S(1)} %get-tuple-element.127), channel_id=1, source_target_pairs={{0,32},{32,64},{64,96},{96,128},{128,160},{160,192},{192,224},{224... | collective-permute-start | bytes 776 | tf_op jit(solution)/shard_map/ppermute | solution.py:47
  31.3 17.3 %collective-permute-start.9 = (f32[3,4,1,2,2,1]{2,5,4,3,1,0:T(1,128)S(1)}, f32[3,4,1,2,2,1]{2,5,4,3,1,0:T(1,128)S(1)}, u32[]{:S(2)}, u32[]{:S(2)}) collective-permute-start(f32[3,4,1,2,2,1]{2,5,4,3,1,0:T(1,128)S(1)} %broadcast_select_fusion.11), channel_id=1, source_target_pairs={{0,512},{512,0},{1,513},{513,1},{2,514},{514,2},{3,515},{515,3},{4... | collective-permute-start | bytes 584 | tf_op jit(solution)/shard_map/ppermute | solution.py:42
  33.6 15.1 %collective-permute-start.7 = (f32[3,1,4,2,1,2]{2,5,4,3,1,0:T(2,128)S(1)}, f32[3,1,4,2,1,2]{2,5,4,3,1,0:T(2,128)S(1)}, u32[]{:S(2)}, u32[]{:S(2)}) collective-permute-start(f32[3,1,4,2,1,2]{2,5,4,3,1,0:T(2,128)S(1)} %get-tuple-element.117), channel_id=1, source_target_pairs={{0,1},{1,2},{2,3},{3,4},{4,5},{5,6},{6,7},{7,8},{8,9},{9,10},{10,1... | collective-permute-start | bytes 584 | tf_op jit(solution)/shard_map/ppermute | solution.py:47
  35.6 13.2 %collective-permute-start.8 = (f32[3,1,4,2,1,2]{2,5,4,3,1,0:T(2,128)S(1)}, f32[3,1,4,2,1,2]{2,5,4,3,1,0:T(2,128)S(1)}, u32[]{:S(2)}, u32[]{:S(2)}) collective-permute-start(f32[3,1,4,2,1,2]{2,5,4,3,1,0:T(2,128)S(1)} %get-tuple-element.118), channel_id=1, source_target_pairs={{1,0},{2,1},{3,2},{4,3},{5,4},{6,5},{7,6},{8,7},{9,8},{10,9},{11,1... | collective-permute-start | bytes 584 | tf_op jit(solution)/shard_map/ppermute | solution.py:48
  53.7 19.2 %collective-permute-start.14 = (f32[3,4,1,2,2,1]{2,5,4,3,1,0:T(1,128)S(1)}, f32[3,4,1,2,2,1]{2,5,4,3,1,0:T(1,128)S(1)}, u32[]{:S(2)}, u32[]{:S(2)}) collective-permute-start(f32[3,4,1,2,2,1]{2,5,4,3,1,0:T(1,128)S(1)} %broadcast_select_fusion.9), channel_id=1, source_target_pairs={{0,512},{512,0},{1,513},{513,1},{2,514},{514,2},{3,515},{515,3},{4... | collective-permute-start | bytes 584 | tf_op jit(solution)/shard_map/ppermute | solution.py:42
  57.2 15.9 %collective-permute-start.12 = (f32[3,1,4,2,1,2]{2,5,4,3,1,0:T(2,128)S(1)}, f32[3,1,4,2,1,2]{2,5,4,3,1,0:T(2,128)S(1)}, u32[]{:S(2)}, u32[]{:S(2)}) collective-permute-start(f32[3,1,4,2,1,2]{2,5,4,3,1,0:T(2,128)S(1)} %get-tuple-element.101), channel_id=1, source_target_pairs={{0,1},{1,2},{2,3},{3,4},{4,5},{5,6},{6,7},{7,8},{8,9},{9,10},{10,1... | collective-permute-start | bytes 584 | tf_op jit(solution)/shard_map/ppermute | solution.py:47
  59.2 14.0 %collective-permute-start.13 = (f32[3,1,4,2,1,2]{2,5,4,3,1,0:T(2,128)S(1)}, f32[3,1,4,2,1,2]{2,5,4,3,1,0:T(2,128)S(1)}, u32[]{:S(2)}, u32[]{:S(2)}) collective-permute-start(f32[3,1,4,2,1,2]{2,5,4,3,1,0:T(2,128)S(1)} %get-tuple-element.102), channel_id=1, source_target_pairs={{1,0},{2,1},{3,2},{4,3},{5,4},{6,5},{7,6},{8,7},{9,8},{10,9},{11,1... | collective-permute-start | bytes 584 | tf_op jit(solution)/shard_map/ppermute | solution.py:48
  90.6 43.5 %collective-permute-start.19 = (f32[3,4,1,8,8,1]{5,4,3,2,1,0:T(8,128)}, f32[3,4,1,8,8,1]{5,4,3,2,1,0:T(8,128)}, u32[]{:S(2)}, u32[]{:S(2)}) collective-permute-start(f32[3,4,1,8,8,1]{5,4,3,2,1,0:T(8,128)} %slice_select_fusion), channel_id=1, source_target_pairs={{0,512},{512,0},{1,513},{513,1},{2,514},{514,2},{3,515},{515,3},{4... | collective-permute-start | bytes 9224 | tf_op jit(solution)/shard_map/ppermute | solution.py:42
  110.0 25.2 %collective-permute-start.18 = (f32[3,1,4,8,1,8]{5,4,3,2,1,0:T(1,128)}, f32[3,1,4,8,1,8]{5,4,3,2,1,0:T(1,128)}, u32[]{:S(2)}, u32[]{:S(2)}) collective-permute-start(f32[3,1,4,8,1,8]{5,4,3,2,1,0:T(1,128)} %get-tuple-element.34), channel_id=1, source_target_pairs={{1,0},{2,1},{3,2},{4,3},{5,4},{6,5},{7,6},{8,7},{9,8},{10,9},{11,1... | collective-permute-start | bytes 9224 | tf_op jit(solution)/shard_map/ppermute | solution.py:48
  114.2 28.9 %collective-permute-start.17 = (f32[3,1,4,8,1,8]{5,4,3,2,1,0:T(1,128)}, f32[3,1,4,8,1,8]{5,4,3,2,1,0:T(1,128)}, u32[]{:S(2)}, u32[]{:S(2)}) collective-permute-start(f32[3,1,4,8,1,8]{5,4,3,2,1,0:T(1,128)} %get-tuple-element.33), channel_id=1, source_target_pairs={{0,1},{1,2},{2,3},{3,4},{4,5},{5,6},{6,7},{7,8},{8,9},{9,10},{10,1... | collective-permute-start | bytes 9224 | tf_op jit(solution)/shard_map/ppermute | solution.py:47
  121.7 29.3 %collective-permute-start.16 = (f32[1,4,4,1,8,8]{4,3,5,2,1,0:T(1,128)}, f32[1,4,4,1,8,8]{4,3,5,2,1,0:T(1,128)}, u32[]{:S(2)}, u32[]{:S(2)}) collective-permute-start(f32[1,4,4,1,8,8]{4,3,5,2,1,0:T(1,128)} %copy.250), channel_id=1, source_target_pairs={{32,0},{64,32},{96,64},{128,96},{160,128},{192,160},{224,192},{256... | collective-permute-start | bytes 12296 | tf_op jit(solution)/shard_map/ppermute | solution.py:48
  126.9 25.4 %collective-permute-start.15 = (f32[1,4,4,1,8,8]{4,3,5,2,1,0:T(1,128)}, f32[1,4,4,1,8,8]{4,3,5,2,1,0:T(1,128)}, u32[]{:S(2)}, u32[]{:S(2)}) collective-permute-start(f32[1,4,4,1,8,8]{4,3,5,2,1,0:T(1,128)} %copy.246), channel_id=1, source_target_pairs={{0,32},{32,64},{64,96},{96,128},{128,160},{160,192},{192,224},{224... | collective-permute-start | bytes 12296 | tf_op jit(solution)/shard_map/ppermute | solution.py:47
  160.9 16.9 %collective-permute-start.24 = (f32[3,4,1,2,2,1]{2,5,4,3,1,0:T(1,128)S(1)}, f32[3,4,1,2,2,1]{2,5,4,3,1,0:T(1,128)S(1)}, u32[]{:S(2)}, u32[]{:S(2)}) collective-permute-start(f32[3,4,1,2,2,1]{2,5,4,3,1,0:T(1,128)S(1)} %broadcast_select_fusion.7), channel_id=1, source_target_pairs={{0,512},{512,0},{1,513},{513,1},{2,514},{514,2},{3,515},{515,3},{4... | collective-permute-start | bytes 584 | tf_op jit(solution)/shard_map/ppermute | solution.py:42
  164.4 13.7 %collective-permute-start.22 = (f32[3,1,4,2,1,2]{2,5,4,3,1,0:T(2,128)S(1)}, f32[3,1,4,2,1,2]{2,5,4,3,1,0:T(2,128)S(1)}, u32[]{:S(2)}, u32[]{:S(2)}) collective-permute-start(f32[3,1,4,2,1,2]{2,5,4,3,1,0:T(2,128)S(1)} %get-tuple-element.85), channel_id=1, source_target_pairs={{0,1},{1,2},{2,3},{3,4},{4,5},{5,6},{6,7},{7,8},{8,9},{9,10},{10,1... | collective-permute-start | bytes 584 | tf_op jit(solution)/shard_map/ppermute | solution.py:47
  166.4 11.8 %collective-permute-start.23 = (f32[3,1,4,2,1,2]{2,5,4,3,1,0:T(2,128)S(1)}, f32[3,1,4,2,1,2]{2,5,4,3,1,0:T(2,128)S(1)}, u32[]{:S(2)}, u32[]{:S(2)}) collective-permute-start(f32[3,1,4,2,1,2]{2,5,4,3,1,0:T(2,128)S(1)} %get-tuple-element.86), channel_id=1, source_target_pairs={{1,0},{2,1},{3,2},{4,3},{5,4},{6,5},{7,6},{8,7},{9,8},{10,9},{11,1... | collective-permute-start | bytes 584 | tf_op jit(solution)/shard_map/ppermute | solution.py:48
  183.3 17.4 %collective-permute-start.29 = (f32[3,4,1,2,2,1]{2,5,4,3,1,0:T(1,128)S(1)}, f32[3,4,1,2,2,1]{2,5,4,3,1,0:T(1,128)S(1)}, u32[]{:S(2)}, u32[]{:S(2)}) collective-permute-start(f32[3,4,1,2,2,1]{2,5,4,3,1,0:T(1,128)S(1)} %broadcast_select_fusion.5), channel_id=1, source_target_pairs={{0,512},{512,0},{1,513},{513,1},{2,514},{514,2},{3,515},{515,3},{4... | collective-permute-start | bytes 584 | tf_op jit(solution)/shard_map/ppermute | solution.py:42
  185.7 15.3 %collective-permute-start.27 = (f32[3,1,4,2,1,2]{2,5,4,3,1,0:T(2,128)S(1)}, f32[3,1,4,2,1,2]{2,5,4,3,1,0:T(2,128)S(1)}, u32[]{:S(2)}, u32[]{:S(2)}) collective-permute-start(f32[3,1,4,2,1,2]{2,5,4,3,1,0:T(2,128)S(1)} %get-tuple-element.69), channel_id=1, source_target_pairs={{0,1},{1,2},{2,3},{3,4},{4,5},{5,6},{6,7},{7,8},{8,9},{9,10},{10,1... | collective-permute-start | bytes 584 | tf_op jit(solution)/shard_map/ppermute | solution.py:47
  187.6 13.3 %collective-permute-start.28 = (f32[3,1,4,2,1,2]{2,5,4,3,1,0:T(2,128)S(1)}, f32[3,1,4,2,1,2]{2,5,4,3,1,0:T(2,128)S(1)}, u32[]{:S(2)}, u32[]{:S(2)}) collective-permute-start(f32[3,1,4,2,1,2]{2,5,4,3,1,0:T(2,128)S(1)} %get-tuple-element.70), channel_id=1, source_target_pairs={{1,0},{2,1},{3,2},{4,3},{5,4},{6,5},{7,6},{8,7},{9,8},{10,9},{11,1... | collective-permute-start | bytes 584 | tf_op jit(solution)/shard_map/ppermute | solution.py:48
  207.2 18.5 %collective-permute-start.34 = (f32[3,4,1,2,2,1]{2,5,4,3,1,0:T(1,128)S(1)}, f32[3,4,1,2,2,1]{2,5,4,3,1,0:T(1,128)S(1)}, u32[]{:S(2)}, u32[]{:S(2)}) collective-permute-start(f32[3,4,1,2,2,1]{2,5,4,3,1,0:T(1,128)S(1)} %broadcast_select_fusion.3), channel_id=1, source_target_pairs={{0,512},{512,0},{1,513},{513,1},{2,514},{514,2},{3,515},{515,3},{4... | collective-permute-start | bytes 584 | tf_op jit(solution)/shard_map/ppermute | solution.py:42
  210.7 15.3 %collective-permute-start.32 = (f32[3,1,4,2,1,2]{2,5,4,3,1,0:T(2,128)S(1)}, f32[3,1,4,2,1,2]{2,5,4,3,1,0:T(2,128)S(1)}, u32[]{:S(2)}, u32[]{:S(2)}) collective-permute-start(f32[3,1,4,2,1,2]{2,5,4,3,1,0:T(2,128)S(1)} %get-tuple-element.53), channel_id=1, source_target_pairs={{0,1},{1,2},{2,3},{3,4},{4,5},{5,6},{6,7},{7,8},{8,9},{9,10},{10,1... | collective-permute-start | bytes 584 | tf_op jit(solution)/shard_map/ppermute | solution.py:47
  212.6 13.3 %collective-permute-start.33 = (f32[3,1,4,2,1,2]{2,5,4,3,1,0:T(2,128)S(1)}, f32[3,1,4,2,1,2]{2,5,4,3,1,0:T(2,128)S(1)}, u32[]{:S(2)}, u32[]{:S(2)}) collective-permute-start(f32[3,1,4,2,1,2]{2,5,4,3,1,0:T(2,128)S(1)} %get-tuple-element.54), channel_id=1, source_target_pairs={{1,0},{2,1},{3,2},{4,3},{5,4},{6,5},{7,6},{8,7},{9,8},{10,9},{11,1... | collective-permute-start | bytes 584 | tf_op jit(solution)/shard_map/ppermute | solution.py:48
  (53 other events, 516.6 us)

commit v2 on v1

--- a/solution.py
+++ b/solution.py
@@ -64,6 +64,51 @@
 ONEHOT = _onehot_tables()
 
 
+def face_select():
+    n = lax.broadcasted_iota(jnp.int32, (DEG1**3, 6 * 128), 0)
+    c = lax.broadcasted_iota(jnp.int32, (DEG1**3, 6 * 128), 1)
+    face, spot = c // 128, c % 128
+    dim, side = face // 2, face % 2
+    n0, n1, n2 = n // (DEG1 * DEG1), (n // DEG1) % DEG1, n % DEG1
+    along = jnp.where(dim == 0, n0, jnp.where(dim == 1, n1, n2))
+    rest = jnp.where(dim == 0, n1 * DEG1 + n2, jnp.where(dim == 1, n0 * DEG1 + n2, n0 * DEG1 + n1))
+    return ((along == side * (DEG1 - 1)) & (spot == rest)).astype(jnp.float32)
+
+
+def fine_face_term(flat, shape_three, coefs):
+    select = face_select()
+    faces = jnp.dot(flat, select, precision=HIGHEST, preferred_element_type=jnp.float32)
+    faces = faces.reshape(shape_three + (6, 128))
+    terms = []
+    for dimension, axis in enumerate(("gx", "yz", "grp")):
+        count = lax.axis_size(axis)
+        block = shape_three[dimension]
+        low = faces[..., 2 * dimension, :]
+        high = faces[..., 2 * dimension + 1, :]
+        top = lax.slice_in_dim(high, block - 1, block, axis=dimension)
+        bottom = lax.slice_in_dim(low, 0, 1, axis=dimension)
+        if count == 2:
+            me = lax.axis_index(axis)
+            got = lax.ppermute(jnp.where(me == 0, top, bottom), axis, [(0, 1), (1, 0)])
+            zero = jnp.zeros_like(got)
+            from_below = jnp.where(me == 1, got, zero)
+            from_above = jnp.where(me == 0, got, zero)
+        else:
+            from_below = lax.ppermute(top, axis, [(i, i + 1) for i in range(count - 1)])
+            from_above = lax.ppermute(bottom, axis, [(i + 1, i) for i in range(count - 1)])
+        lower = jnp.concatenate([from_below, lax.slice_in_dim(high, 0, block - 1, axis=dimension)], axis=dimension)
+        upper = jnp.concatenate([lax.slice_in_dim(low, 1, block, axis=dimension), from_above], axis=dimension)
+        lower_coef, upper_coef = coefs[dimension]
+        lower_coef = lower_coef.reshape(shape_three + (1,))
+        upper_coef = upper_coef.reshape(shape_three + (1,))
+        terms.append(lower_coef * low - PENALTY * lower)
+        terms.append(upper_coef * high - PENALTY * upper)
+    terms = jnp.stack(terms, axis=3).reshape(-1, 6 * 128)
+    return lax.dot_general(
+        terms, select, (((1,), (1,)), ((), ())), precision=HIGHEST, preferred_element_type=jnp.float32
+    )
+
+
 def build_tables(basis, eigenvalues):
     eigen_table = None
     for pick in ONEHOT:
@@ -176,9 +221,7 @@
     inverse_scale = 1.0 / block_scale
 
     def apply_fine(solution):
-        field = solution.reshape(shape_three + (DEG1, DEG1, DEG1))
-        lower_list, upper_list = face_traces(field, DEG1)
-        faces = face_term(field, lower_list, upper_list, fine_coefs, PENALTY).reshape(
+        faces = fine_face_term(solution.reshape(-1, node_count), shape_three, fine_coefs).reshape(
             solution.shape
         )
         return eigen_apply(solution, eigen_table, block_scale) + faces

time: 233 us -> 174 us (0.75)
  the two profiles are of different devices: /device:TPU:4 before, /device:TPU:249 now
where the time goes in v2:
time: 174 us; the launch traced here: 173 us
  starting transfers between devices  117 us (67%)
  waiting for transfers between devices  23.5 us (14%)
  matrix products  18.9 us (11%)
  other arithmetic  6.94 us (4%)
  local copies, waits for them, and re-layouts  4.85 us (3%)
    ppermute x12, starting transfers between devices, face_traces(): from_below = lax.ppermute(top, axis, [(i, i + 1) for i in range(count - 1)])  57.6 us
    ppermute x12, starting transfers between devices, face_traces(): lax.ppermute(bottom, axis, [(i + 1, i) for i in range(count - 1)])  23 us
    ppermute x6, starting transfers between devices, face_traces(): got = lax.ppermute(jnp.where(me == 0, top, bottom), axis, [(0, 1), (1, 0)])  16.4 us
    ppermute x12, waiting for transfers between devices, face_traces(): lax.ppermute(bottom, axis, [(i + 1, i) for i in range(count - 1)])  14.7 us
    ppermute x2, starting transfers between devices, fine_face_term(): from_below = lax.ppermute(top, axis, [(i, i + 1) for i in range(count - 1)])  12.9 us
    ppermute x2, waiting for transfers between devices, fine_face_term(): lax.ppermute(bottom, axis, [(i + 1, i) for i in range(count - 1)])  6.26 us
    dot_general x3, matrix products, eigen_apply(): jnp.dot(flat, eigen_table, precision=HIGHEST, preferred_element_type=jnp....  5.47 us
    ppermute x2, starting transfers between devices, fine_face_term(): lax.ppermute(bottom, axis, [(i + 1, i) for i in range(count - 1)])  4.02 us
  transfers between devices with their start and end apart: 35, of which 9 were waited for; matrix products, arithmetic and copies ran while one was open for 9% of the time, Pallas kernels for 0%

profile of v2, /device:TPU:249, one launch (start us, length us, event | category | flops | bytes accessed | tf_op | source)
XLA Modules:
  0.0 172.7 jit_solution(6674652542278211683)
XLA Ops:
  4.0 3.0 %collective-permute-start.4 = (f32[3,4,1,2,2,1]{2,5,4,3,1,0:T(1,128)S(1)}, f32[3,4,1,2,2,1]{2,5,4,3,1,0:T(1,128)S(1)}, u32[]{:S(2)}, u32[]{:S(2)}) collective-permute-start(f32[3,4,1,2,2,1]{2,5,4,3,1,0:T(1,128)S(1)} %broadcast_select_fusion.11), channel_id=1, source_target_pairs={{0,512},{512,0},{1,513},{513,1},{2,514},{514,2},{3,515},{515,3},{4... | collective-permute-start | bytes 584 | tf_op jit(solution)/shard_map/ppermute | solution.py:42
  7.0 5.2 %collective-permute-start = (f32[1,4,4,1,2,2]{2,5,4,3,1,0:T(2,128)S(1)}, f32[1,4,4,1,2,2]{2,5,4,3,1,0:T(2,128)S(1)}, u32[]{:S(2)}, u32[]{:S(2)}) collective-permute-start(f32[1,4,4,1,2,2]{2,5,4,3,1,0:T(2,128)S(1)} %get-tuple-element.118), channel_id=1, source_target_pairs={{0,32},{32,64},{64,96},{96,128},{128,160},{160,192},{192,224},{224... | collective-permute-start | bytes 776 | tf_op jit(solution)/shard_map/ppermute | solution.py:47
  14.1 3.6 %collective-permute-start.2 = (f32[3,1,4,2,1,2]{2,5,4,3,1,0:T(2,128)S(1)}, f32[3,1,4,2,1,2]{2,5,4,3,1,0:T(2,128)S(1)}, u32[]{:S(2)}, u32[]{:S(2)}) collective-permute-start(f32[3,1,4,2,1,2]{2,5,4,3,1,0:T(2,128)S(1)} %get-tuple-element.124), channel_id=1, source_target_pairs={{0,1},{1,2},{2,3},{3,4},{4,5},{5,6},{6,7},{7,8},{8,9},{9,10},{10,1... | collective-permute-start | bytes 584 | tf_op jit(solution)/shard_map/ppermute | solution.py:47
  29.1 4.9 %collective-permute-start.5 = (f32[1,4,4,1,2,2]{2,5,4,3,1,0:T(2,128)S(1)}, f32[1,4,4,1,2,2]{2,5,4,3,1,0:T(2,128)S(1)}, u32[]{:S(2)}, u32[]{:S(2)}) collective-permute-start(f32[1,4,4,1,2,2]{2,5,4,3,1,0:T(2,128)S(1)} %get-tuple-element.102), channel_id=1, source_target_pairs={{0,32},{32,64},{64,96},{96,128},{128,160},{160,192},{192,224},{224... | collective-permute-start | bytes 776 | tf_op jit(solution)/shard_map/ppermute | solution.py:47
  35.9 6.9 %collective-permute-start.7 = (f32[3,1,4,2,1,2]{2,5,4,3,1,0:T(2,128)S(1)}, f32[3,1,4,2,1,2]{2,5,4,3,1,0:T(2,128)S(1)}, u32[]{:S(2)}, u32[]{:S(2)}) collective-permute-start(f32[3,1,4,2,1,2]{2,5,4,3,1,0:T(2,128)S(1)} %get-tuple-element.108), channel_id=1, source_target_pairs={{0,1},{1,2},{2,3},{3,4},{4,5},{5,6},{6,7},{7,8},{8,9},{9,10},{10,1... | collective-permute-start | bytes 584 | tf_op jit(solution)/shard_map/ppermute | solution.py:47
  44.7 3.2 %collective-permute-start.9 = (f32[3,4,1,2,2,1]{2,5,4,3,1,0:T(1,128)S(1)}, f32[3,4,1,2,2,1]{2,5,4,3,1,0:T(1,128)S(1)}, u32[]{:S(2)}, u32[]{:S(2)}) collective-permute-start(f32[3,4,1,2,2,1]{2,5,4,3,1,0:T(1,128)S(1)} %broadcast_select_fusion.9), channel_id=1, source_target_pairs={{0,512},{512,0},{1,513},{513,1},{2,514},{514,2},{3,515},{515,3},{4... | collective-permute-start | bytes 584 | tf_op jit(solution)/shard_map/ppermute | solution.py:42
  51.5 4.9 %collective-permute-start.10 = (f32[1,4,4,1,2,2]{2,5,4,3,1,0:T(2,128)S(1)}, f32[1,4,4,1,2,2]{2,5,4,3,1,0:T(2,128)S(1)}, u32[]{:S(2)}, u32[]{:S(2)}) collective-permute-start(f32[1,4,4,1,2,2]{2,5,4,3,1,0:T(2,128)S(1)} %get-tuple-element.86), channel_id=1, source_target_pairs={{0,32},{32,64},{64,96},{96,128},{128,160},{160,192},{192,224},{224... | collective-permute-start | bytes 776 | tf_op jit(solution)/shard_map/ppermute | solution.py:47
  58.3 6.9 %collective-permute-start.12 = (f32[3,1,4,2,1,2]{2,5,4,3,1,0:T(2,128)S(1)}, f32[3,1,4,2,1,2]{2,5,4,3,1,0:T(2,128)S(1)}, u32[]{:S(2)}, u32[]{:S(2)}) collective-permute-start(f32[3,1,4,2,1,2]{2,5,4,3,1,0:T(2,128)S(1)} %get-tuple-element.92), channel_id=1, source_target_pairs={{0,1},{1,2},{2,3},{3,4},{4,5},{5,6},{6,7},{7,8},{8,9},{9,10},{10,1... | collective-permute-start | bytes 584 | tf_op jit(solution)/shard_map/ppermute | solution.py:47
  67.1 3.2 %collective-permute-start.14 = (f32[3,4,1,2,2,1]{2,5,4,3,1,0:T(1,128)S(1)}, f32[3,4,1,2,2,1]{2,5,4,3,1,0:T(1,128)S(1)}, u32[]{:S(2)}, u32[]{:S(2)}) collective-permute-start(f32[3,4,1,2,2,1]{2,5,4,3,1,0:T(1,128)S(1)} %broadcast_select_fusion.7), channel_id=1, source_target_pairs={{0,512},{512,0},{1,513},{513,1},{2,514},{514,2},{3,515},{515,3},{4... | collective-permute-start | bytes 584 | tf_op jit(solution)/shard_map/ppermute | solution.py:42
  73.9 2.2 %fusion.24 = f32[3,4,4,6,128]{4,2,3,1,0:T(4,128)S(1)} fusion(s32[6,128]{1,0:T(8,128)S(1)} %get-tuple-element.171, s32[6,128]{1,0:T(8,128)S(1)} %get-tuple-element.174, s32[512]{0:T(512)S(1)} %get-tuple-element.167, s32[512]{0:T(512)S(1)} %get-tuple-element.169, s32[512]{0:T(512)S(1)} %get-tuple-element.166, s32[512]{0:T(512)S(1)} %get-tuple-element.178, ...), kind=kOutput, calls=%fused_computation.60 | convolution fusion | flops 246153216 | bytes 273408 | tf_op jit(solution)/shard_map/dot_general | solution.py:80
  76.2 4.9 %collective-permute-start.15 = (f32[1,4,4,128]{3,2,1,0:T(4,128)S(1)}, f32[1,4,4,128]{3,2,1,0:T(4,128)S(1)}, u32[]{:S(2)}, u32[]{:S(2)}) collective-permute-start(f32[1,4,4,128]{3,2,1,0:T(4,128)S(1)} %get-tuple-element.33), channel_id=1, source_target_pairs={{0,32},{32,64},{64,96},{96,128},{128,160},{160,192},{192,224},{224... | collective-permute-start | bytes 24584 | tf_op jit(solution)/shard_map/ppermute | solution.py:97
  86.8 8.0 %collective-permute-start.17 = (f32[3,1,4,128]{3,2,0,1:T(4,128)S(1)}, f32[3,1,4,128]{3,2,0,1:T(4,128)S(1)}, u32[]{:S(2)}, u32[]{:S(2)}) collective-permute-start(f32[3,1,4,128]{3,2,0,1:T(4,128)S(1)} %slice_bitcast_fusion.9), channel_id=1, source_target_pairs={{0,1},{1,2},{2,3},{3,4},{4,5},{5,6},{6,7},{7,8},{8,9},{9,10},{10,1... | collective-permute-start | bytes 18440 | tf_op jit(solution)/shard_map/ppermute | solution.py:97
  94.9 3.2 %collective-permute-start.19 = (f32[3,4,1,128]{3,1,0,2:T(4,128)S(1)}, f32[3,4,1,128]{3,1,0,2:T(4,128)S(1)}, u32[]{:S(2)}, u32[]{:S(2)}) collective-permute-start(f32[3,4,1,128]{3,1,0,2:T(4,128)S(1)} %slice_select_fusion), channel_id=1, source_target_pairs={{0,512},{512,0},{1,513},{513,1},{2,514},{514,2},{3,515},{515,3},{4... | collective-permute-start | bytes 18440 | tf_op jit(solution)/shard_map/ppermute | solution.py:92
  100.2 5.9 %collective-permute-done.18 = f32[3,1,4,128]{3,2,1,0:T(4,128)S(1)} collective-permute-done((f32[3,1,4,128]{3,2,1,0:T(4,128)S(1)}, f32[3,1,4,128]{3,2,1,0:T(4,128)S(1)}, u32[]{:S(2)}, u32[]{:S(2)}) %collective-permute-start.18) | collective-permute-done | bytes 6176 | tf_op jit(solution)/shard_map/ppermute | solution.py:98
  109.2 3.4 %collective-permute-start.20 = (f32[1,4,4,1,2,2]{2,5,4,3,1,0:T(2,128)S(1)}, f32[1,4,4,1,2,2]{2,5,4,3,1,0:T(2,128)S(1)}, u32[]{:S(2)}, u32[]{:S(2)}) collective-permute-start(f32[1,4,4,1,2,2]{2,5,4,3,1,0:T(2,128)S(1)} %get-tuple-element.70), channel_id=1, source_target_pairs={{0,32},{32,64},{64,96},{96,128},{128,160},{160,192},{192,224},{224... | collective-permute-start | bytes 776 | tf_op jit(solution)/shard_map/ppermute | solution.py:47
  114.6 2.5 %collective-permute-start.22 = (f32[3,1,4,2,1,2]{2,5,4,3,1,0:T(2,128)S(1)}, f32[3,1,4,2,1,2]{2,5,4,3,1,0:T(2,128)S(1)}, u32[]{:S(2)}, u32[]{:S(2)}) collective-permute-start(f32[3,1,4,2,1,2]{2,5,4,3,1,0:T(2,128)S(1)} %get-tuple-element.76), channel_id=1, source_target_pairs={{0,1},{1,2},{2,3},{3,4},{4,5},{5,6},{6,7},{7,8},{8,9},{9,10},{10,1... | collective-permute-start | bytes 584 | tf_op jit(solution)/shard_map/ppermute | solution.py:47
  126.1 4.6 %collective-permute-start.25 = (f32[1,4,4,1,2,2]{2,5,4,3,1,0:T(2,128)S(1)}, f32[1,4,4,1,2,2]{2,5,4,3,1,0:T(2,128)S(1)}, u32[]{:S(2)}, u32[]{:S(2)}) collective-permute-start(f32[1,4,4,1,2,2]{2,5,4,3,1,0:T(2,128)S(1)} %get-tuple-element.54), channel_id=1, source_target_pairs={{0,32},{32,64},{64,96},{96,128},{128,160},{160,192},{192,224},{224... | collective-permute-start | bytes 776 | tf_op jit(solution)/shard_map/ppermute | solution.py:47
  132.6 2.6 %collective-permute-start.29 = (f32[3,4,1,2,2,1]{2,5,4,3,1,0:T(1,128)S(1)}, f32[3,4,1,2,2,1]{2,5,4,3,1,0:T(1,128)S(1)}, u32[]{:S(2)}, u32[]{:S(2)}) collective-permute-start(f32[3,4,1,2,2,1]{2,5,4,3,1,0:T(1,128)S(1)} %broadcast_select_fusion.3), channel_id=1, source_target_pairs={{0,512},{512,0},{1,513},{513,1},{2,514},{514,2},{3,515},{515,3},{4... | collective-permute-start | bytes 584 | tf_op jit(solution)/shard_map/ppermute | solution.py:42
  135.2 7.5 %collective-permute-start.27 = (f32[3,1,4,2,1,2]{2,5,4,3,1,0:T(2,128)S(1)}, f32[3,1,4,2,1,2]{2,5,4,3,1,0:T(2,128)S(1)}, u32[]{:S(2)}, u32[]{:S(2)}) collective-permute-start(f32[3,1,4,2,1,2]{2,5,4,3,1,0:T(2,128)S(1)} %get-tuple-element.60), channel_id=1, source_target_pairs={{0,1},{1,2},{2,3},{3,4},{4,5},{5,6},{6,7},{7,8},{8,9},{9,10},{10,1... | collective-permute-start | bytes 584 | tf_op jit(solution)/shard_map/ppermute | solution.py:47
  144.8 5.8 %collective-permute-done.28 = f32[3,1,4,2,1,2]{2,5,4,3,1,0:T(2,128)S(1)} collective-permute-done((f32[3,1,4,2,1,2]{2,5,4,3,1,0:T(2,128)S(1)}, f32[3,1,4,2,1,2]{2,5,4,3,1,0:T(2,128)S(1)}, u32[]{:S(2)}, u32[]{:S(2)}) %collective-permute-start.28) | collective-permute-done | bytes 224 | tf_op jit(solution)/shard_map/ppermute | solution.py:48
  151.7 4.9 %collective-permute-start.30 = (f32[1,4,4,1,2,2]{2,5,4,3,1,0:T(2,128)S(1)}, f32[1,4,4,1,2,2]{2,5,4,3,1,0:T(2,128)S(1)}, u32[]{:S(2)}, u32[]{:S(2)}) collective-permute-start(f32[1,4,4,1,2,2]{2,5,4,3,1,0:T(2,128)S(1)} %get-tuple-element.38), channel_id=1, source_target_pairs={{0,32},{32,64},{64,96},{96,128},{128,160},{160,192},{192,224},{224... | collective-permute-start | bytes 776 | tf_op jit(solution)/shard_map/ppermute | solution.py:47
  158.4 2.4 %collective-permute-start.34 = (f32[3,4,1,2,2,1]{2,5,4,3,1,0:T(1,128)S(1)}, f32[3,4,1,2,2,1]{2,5,4,3,1,0:T(1,128)S(1)}, u32[]{:S(2)}, u32[]{:S(2)}) collective-permute-start(f32[3,4,1,2,2,1]{2,5,4,3,1,0:T(1,128)S(1)} %broadcast_select_fusion.1), channel_id=1, source_target_pairs={{0,512},{512,0},{1,513},{513,1},{2,514},{514,2},{3,515},{515,3},{4... | collective-permute-start | bytes 584 | tf_op jit(solution)/shard_map/ppermute | solution.py:42
  160.8 2.5 %collective-permute-start.32 = (f32[3,1,4,2,1,2]{2,5,4,3,1,0:T(2,128)S(1)}, f32[3,1,4,2,1,2]{2,5,4,3,1,0:T(2,128)S(1)}, u32[]{:S(2)}, u32[]{:S(2)}) collective-permute-start(f32[3,1,4,2,1,2]{2,5,4,3,1,0:T(2,128)S(1)} %get-tuple-element.44), channel_id=1, source_target_pairs={{0,1},{1,2},{2,3},{3,4},{4,5},{5,6},{6,7},{7,8},{8,9},{9,10},{10,1... | collective-permute-start | bytes 584 | tf_op jit(solution)/shard_map/ppermute | solution.py:47
  165.5 5.8 %collective-permute-done.33 = f32[3,1,4,2,1,2]{2,5,4,3,1,0:T(2,128)S(1)} collective-permute-done((f32[3,1,4,2,1,2]{2,5,4,3,1,0:T(2,128)S(1)}, f32[3,1,4,2,1,2]{2,5,4,3,1,0:T(2,128)S(1)}, u32[]{:S(2)}, u32[]{:S(2)}) %collective-permute-start.33) | collective-permute-done | bytes 224 | tf_op jit(solution)/shard_map/ppermute | solution.py:48
  (221 shorter events, 63.6 us)
Async XLA Ops:
  4.0 24.1 %collective-permute-start.4 = (f32[3,4,1,2,2,1]{2,5,4,3,1,0:T(1,128)S(1)}, f32[3,4,1,2,2,1]{2,5,4,3,1,0:T(1,128)S(1)}, u32[]{:S(2)}, u32[]{:S(2)}) collective-permute-start(f32[3,4,1,2,2,1]{2,5,4,3,1,0:T(1,128)S(1)} %broadcast_select_fusion.11), channel_id=1, source_target_pairs={{0,512},{512,0},{1,513},{513,1},{2,514},{514,2},{3,515},{515,3},{4... | collective-permute-start | bytes 584 | tf_op jit(solution)/shard_map/ppermute | solution.py:42
  7.0 21.4 %collective-permute-start = (f32[1,4,4,1,2,2]{2,5,4,3,1,0:T(2,128)S(1)}, f32[1,4,4,1,2,2]{2,5,4,3,1,0:T(2,128)S(1)}, u32[]{:S(2)}, u32[]{:S(2)}) collective-permute-start(f32[1,4,4,1,2,2]{2,5,4,3,1,0:T(2,128)S(1)} %get-tuple-element.118), channel_id=1, source_target_pairs={{0,32},{32,64},{64,96},{96,128},{128,160},{160,192},{192,224},{224... | collective-permute-start | bytes 776 | tf_op jit(solution)/shard_map/ppermute | solution.py:47
  12.2 16.2 %collective-permute-start.1 = (f32[1,4,4,1,2,2]{2,5,4,3,1,0:T(2,128)S(1)}, f32[1,4,4,1,2,2]{2,5,4,3,1,0:T(2,128)S(1)}, u32[]{:S(2)}, u32[]{:S(2)}) collective-permute-start(f32[1,4,4,1,2,2]{2,5,4,3,1,0:T(2,128)S(1)} %get-tuple-element.119), channel_id=1, source_target_pairs={{32,0},{64,32},{96,64},{128,96},{160,128},{192,160},{224,192},{256... | collective-permute-start | bytes 776 | tf_op jit(solution)/shard_map/ppermute | solution.py:48
  14.1 14.2 %collective-permute-start.2 = (f32[3,1,4,2,1,2]{2,5,4,3,1,0:T(2,128)S(1)}, f32[3,1,4,2,1,2]{2,5,4,3,1,0:T(2,128)S(1)}, u32[]{:S(2)}, u32[]{:S(2)}) collective-permute-start(f32[3,1,4,2,1,2]{2,5,4,3,1,0:T(2,128)S(1)} %get-tuple-element.124), channel_id=1, source_target_pairs={{0,1},{1,2},{2,3},{3,4},{4,5},{5,6},{6,7},{7,8},{8,9},{9,10},{10,1... | collective-permute-start | bytes 584 | tf_op jit(solution)/shard_map/ppermute | solution.py:47
  17.7 10.6 %collective-permute-start.3 = (f32[3,1,4,2,1,2]{2,5,4,3,1,0:T(2,128)S(1)}, f32[3,1,4,2,1,2]{2,5,4,3,1,0:T(2,128)S(1)}, u32[]{:S(2)}, u32[]{:S(2)}) collective-permute-start(f32[3,1,4,2,1,2]{2,5,4,3,1,0:T(2,128)S(1)} %get-tuple-element.125), channel_id=1, source_target_pairs={{1,0},{2,1},{3,2},{4,3},{5,4},{6,5},{7,6},{8,7},{9,8},{10,9},{11,1... | collective-permute-start | bytes 584 | tf_op jit(solution)/shard_map/ppermute | solution.py:48
  29.1 21.7 %collective-permute-start.5 = (f32[1,4,4,1,2,2]{2,5,4,3,1,0:T(2,128)S(1)}, f32[1,4,4,1,2,2]{2,5,4,3,1,0:T(2,128)S(1)}, u32[]{:S(2)}, u32[]{:S(2)}) collective-permute-start(f32[1,4,4,1,2,2]{2,5,4,3,1,0:T(2,128)S(1)} %get-tuple-element.102), channel_id=1, source_target_pairs={{0,32},{32,64},{64,96},{96,128},{128,160},{160,192},{192,224},{224... | collective-permute-start | bytes 776 | tf_op jit(solution)/shard_map/ppermute | solution.py:47
  33.9 16.9 %collective-permute-start.6 = (f32[1,4,4,1,2,2]{2,5,4,3,1,0:T(2,128)S(1)}, f32[1,4,4,1,2,2]{2,5,4,3,1,0:T(2,128)S(1)}, u32[]{:S(2)}, u32[]{:S(2)}) collective-permute-start(f32[1,4,4,1,2,2]{2,5,4,3,1,0:T(2,128)S(1)} %get-tuple-element.103), channel_id=1, source_target_pairs={{32,0},{64,32},{96,64},{128,96},{160,128},{192,160},{224,192},{256... | collective-permute-start | bytes 776 | tf_op jit(solution)/shard_map/ppermute | solution.py:48
  35.9 13.7 %collective-permute-start.7 = (f32[3,1,4,2,1,2]{2,5,4,3,1,0:T(2,128)S(1)}, f32[3,1,4,2,1,2]{2,5,4,3,1,0:T(2,128)S(1)}, u32[]{:S(2)}, u32[]{:S(2)}) collective-permute-start(f32[3,1,4,2,1,2]{2,5,4,3,1,0:T(2,128)S(1)} %get-tuple-element.108), channel_id=1, source_target_pairs={{0,1},{1,2},{2,3},{3,4},{4,5},{5,6},{6,7},{7,8},{8,9},{9,10},{10,1... | collective-permute-start | bytes 584 | tf_op jit(solution)/shard_map/ppermute | solution.py:47
  42.8 8.0 %collective-permute-start.8 = (f32[3,1,4,2,1,2]{2,5,4,3,1,0:T(2,128)S(1)}, f32[3,1,4,2,1,2]{2,5,4,3,1,0:T(2,128)S(1)}, u32[]{:S(2)}, u32[]{:S(2)}) collective-permute-start(f32[3,1,4,2,1,2]{2,5,4,3,1,0:T(2,128)S(1)} %get-tuple-element.109), channel_id=1, source_target_pairs={{1,0},{2,1},{3,2},{4,3},{5,4},{6,5},{7,6},{8,7},{9,8},{10,9},{11,1... | collective-permute-start | bytes 584 | tf_op jit(solution)/shard_map/ppermute | solution.py:48
  51.5 21.7 %collective-permute-start.10 = (f32[1,4,4,1,2,2]{2,5,4,3,1,0:T(2,128)S(1)}, f32[1,4,4,1,2,2]{2,5,4,3,1,0:T(2,128)S(1)}, u32[]{:S(2)}, u32[]{:S(2)}) collective-permute-start(f32[1,4,4,1,2,2]{2,5,4,3,1,0:T(2,128)S(1)} %get-tuple-element.86), channel_id=1, source_target_pairs={{0,32},{32,64},{64,96},{96,128},{128,160},{160,192},{192,224},{224... | collective-permute-start | bytes 776 | tf_op jit(solution)/shard_map/ppermute | solution.py:47
  56.4 16.8 %collective-permute-start.11 = (f32[1,4,4,1,2,2]{2,5,4,3,1,0:T(2,128)S(1)}, f32[1,4,4,1,2,2]{2,5,4,3,1,0:T(2,128)S(1)}, u32[]{:S(2)}, u32[]{:S(2)}) collective-permute-start(f32[1,4,4,1,2,2]{2,5,4,3,1,0:T(2,128)S(1)} %get-tuple-element.87), channel_id=1, source_target_pairs={{32,0},{64,32},{96,64},{128,96},{160,128},{192,160},{224,192},{256... | collective-permute-start | bytes 776 | tf_op jit(solution)/shard_map/ppermute | solution.py:48
  58.3 13.6 %collective-permute-start.12 = (f32[3,1,4,2,1,2]{2,5,4,3,1,0:T(2,128)S(1)}, f32[3,1,4,2,1,2]{2,5,4,3,1,0:T(2,128)S(1)}, u32[]{:S(2)}, u32[]{:S(2)}) collective-permute-start(f32[3,1,4,2,1,2]{2,5,4,3,1,0:T(2,128)S(1)} %get-tuple-element.92), channel_id=1, source_target_pairs={{0,1},{1,2},{2,3},{3,4},{4,5},{5,6},{6,7},{7,8},{8,9},{9,10},{10,1... | collective-permute-start | bytes 584 | tf_op jit(solution)/shard_map/ppermute | solution.py:47
  76.2 10.0 %collective-permute-start.15 = (f32[1,4,4,128]{3,2,1,0:T(4,128)S(1)}, f32[1,4,4,128]{3,2,1,0:T(4,128)S(1)}, u32[]{:S(2)}, u32[]{:S(2)}) collective-permute-start(f32[1,4,4,128]{3,2,1,0:T(4,128)S(1)} %get-tuple-element.33), channel_id=1, source_target_pairs={{0,32},{32,64},{64,96},{96,128},{128,160},{160,192},{192,224},{224... | collective-permute-start | bytes 24584 | tf_op jit(solution)/shard_map/ppermute | solution.py:97
  86.8 13.3 %collective-permute-start.17 = (f32[3,1,4,128]{3,2,0,1:T(4,128)S(1)}, f32[3,1,4,128]{3,2,0,1:T(4,128)S(1)}, u32[]{:S(2)}, u32[]{:S(2)}) collective-permute-start(f32[3,1,4,128]{3,2,0,1:T(4,128)S(1)} %slice_bitcast_fusion.9), channel_id=1, source_target_pairs={{0,1},{1,2},{2,3},{3,4},{4,5},{5,6},{6,7},{7,8},{8,9},{9,10},{10,1... | collective-permute-start | bytes 18440 | tf_op jit(solution)/shard_map/ppermute | solution.py:97
  94.9 11.3 %collective-permute-start.19 = (f32[3,4,1,128]{3,1,0,2:T(4,128)S(1)}, f32[3,4,1,128]{3,1,0,2:T(4,128)S(1)}, u32[]{:S(2)}, u32[]{:S(2)}) collective-permute-start(f32[3,4,1,128]{3,1,0,2:T(4,128)S(1)} %slice_select_fusion), channel_id=1, source_target_pairs={{0,512},{512,0},{1,513},{513,1},{2,514},{514,2},{3,515},{515,3},{4... | collective-permute-start | bytes 18440 | tf_op jit(solution)/shard_map/ppermute | solution.py:92
  109.2 15.8 %collective-permute-start.20 = (f32[1,4,4,1,2,2]{2,5,4,3,1,0:T(2,128)S(1)}, f32[1,4,4,1,2,2]{2,5,4,3,1,0:T(2,128)S(1)}, u32[]{:S(2)}, u32[]{:S(2)}) collective-permute-start(f32[1,4,4,1,2,2]{2,5,4,3,1,0:T(2,128)S(1)} %get-tuple-element.70), channel_id=1, source_target_pairs={{0,32},{32,64},{64,96},{96,128},{128,160},{160,192},{192,224},{224... | collective-permute-start | bytes 776 | tf_op jit(solution)/shard_map/ppermute | solution.py:47
  112.6 12.5 %collective-permute-start.21 = (f32[1,4,4,1,2,2]{2,5,4,3,1,0:T(2,128)S(1)}, f32[1,4,4,1,2,2]{2,5,4,3,1,0:T(2,128)S(1)}, u32[]{:S(2)}, u32[]{:S(2)}) collective-permute-start(f32[1,4,4,1,2,2]{2,5,4,3,1,0:T(2,128)S(1)} %get-tuple-element.71), channel_id=1, source_target_pairs={{32,0},{64,32},{96,64},{128,96},{160,128},{192,160},{224,192},{256... | collective-permute-start | bytes 776 | tf_op jit(solution)/shard_map/ppermute | solution.py:48
  114.6 9.8 %collective-permute-start.22 = (f32[3,1,4,2,1,2]{2,5,4,3,1,0:T(2,128)S(1)}, f32[3,1,4,2,1,2]{2,5,4,3,1,0:T(2,128)S(1)}, u32[]{:S(2)}, u32[]{:S(2)}) collective-permute-start(f32[3,1,4,2,1,2]{2,5,4,3,1,0:T(2,128)S(1)} %get-tuple-element.76), channel_id=1, source_target_pairs={{0,1},{1,2},{2,3},{3,4},{4,5},{5,6},{6,7},{7,8},{8,9},{9,10},{10,1... | collective-permute-start | bytes 584 | tf_op jit(solution)/shard_map/ppermute | solution.py:47
  126.1 24.6 %collective-permute-start.25 = (f32[1,4,4,1,2,2]{2,5,4,3,1,0:T(2,128)S(1)}, f32[1,4,4,1,2,2]{2,5,4,3,1,0:T(2,128)S(1)}, u32[]{:S(2)}, u32[]{:S(2)}) collective-permute-start(f32[1,4,4,1,2,2]{2,5,4,3,1,0:T(2,128)S(1)} %get-tuple-element.54), channel_id=1, source_target_pairs={{0,32},{32,64},{64,96},{96,128},{128,160},{160,192},{192,224},{224... | collective-permute-start | bytes 776 | tf_op jit(solution)/shard_map/ppermute | solution.py:47
  130.7 20.0 %collective-permute-start.26 = (f32[1,4,4,1,2,2]{2,5,4,3,1,0:T(2,128)S(1)}, f32[1,4,4,1,2,2]{2,5,4,3,1,0:T(2,128)S(1)}, u32[]{:S(2)}, u32[]{:S(2)}) collective-permute-start(f32[1,4,4,1,2,2]{2,5,4,3,1,0:T(2,128)S(1)} %get-tuple-element.55), channel_id=1, source_target_pairs={{32,0},{64,32},{96,64},{128,96},{160,128},{192,160},{224,192},{256... | collective-permute-start | bytes 776 | tf_op jit(solution)/shard_map/ppermute | solution.py:48
  132.6 12.0 %collective-permute-start.29 = (f32[3,4,1,2,2,1]{2,5,4,3,1,0:T(1,128)S(1)}, f32[3,4,1,2,2,1]{2,5,4,3,1,0:T(1,128)S(1)}, u32[]{:S(2)}, u32[]{:S(2)}) collective-permute-start(f32[3,4,1,2,2,1]{2,5,4,3,1,0:T(1,128)S(1)} %broadcast_select_fusion.3), channel_id=1, source_target_pairs={{0,512},{512,0},{1,513},{513,1},{2,514},{514,2},{3,515},{515,3},{4... | collective-permute-start | bytes 584 | tf_op jit(solution)/shard_map/ppermute | solution.py:42
  135.2 9.7 %collective-permute-start.27 = (f32[3,1,4,2,1,2]{2,5,4,3,1,0:T(2,128)S(1)}, f32[3,1,4,2,1,2]{2,5,4,3,1,0:T(2,128)S(1)}, u32[]{:S(2)}, u32[]{:S(2)}) collective-permute-start(f32[3,1,4,2,1,2]{2,5,4,3,1,0:T(2,128)S(1)} %get-tuple-element.60), channel_id=1, source_target_pairs={{0,1},{1,2},{2,3},{3,4},{4,5},{5,6},{6,7},{7,8},{8,9},{9,10},{10,1... | collective-permute-start | bytes 584 | tf_op jit(solution)/shard_map/ppermute | solution.py:47
  151.7 19.7 %collective-permute-start.30 = (f32[1,4,4,1,2,2]{2,5,4,3,1,0:T(2,128)S(1)}, f32[1,4,4,1,2,2]{2,5,4,3,1,0:T(2,128)S(1)}, u32[]{:S(2)}, u32[]{:S(2)}) collective-permute-start(f32[1,4,4,1,2,2]{2,5,4,3,1,0:T(2,128)S(1)} %get-tuple-element.38), channel_id=1, source_target_pairs={{0,32},{32,64},{64,96},{96,128},{128,160},{160,192},{192,224},{224... | collective-permute-start | bytes 776 | tf_op jit(solution)/shard_map/ppermute | solution.py:47
  156.5 14.8 %collective-permute-start.31 = (f32[1,4,4,1,2,2]{2,5,4,3,1,0:T(2,128)S(1)}, f32[1,4,4,1,2,2]{2,5,4,3,1,0:T(2,128)S(1)}, u32[]{:S(2)}, u32[]{:S(2)}) collective-permute-start(f32[1,4,4,1,2,2]{2,5,4,3,1,0:T(2,128)S(1)} %get-tuple-element.39), channel_id=1, source_target_pairs={{32,0},{64,32},{96,64},{128,96},{160,128},{192,160},{224,192},{256... | collective-permute-start | bytes 776 | tf_op jit(solution)/shard_map/ppermute | solution.py:48
  (19 other events, 159.0 us)

commit v3 on v2

--- a/solution.py
+++ b/solution.py
@@ -54,6 +54,106 @@
         )
     return (lower_list, upper_list)
 
+
+def shift(v, axis, s):
+    size = v.shape[axis]
+    zshape = list(v.shape)
+    zshape[axis] = abs(s)
+    zeros = jnp.zeros(zshape, v.dtype)
+    if s > 0:
+        return jnp.concatenate([lax.slice_in_dim(v, s, size, axis=axis), zeros], axis=axis)
+    return jnp.concatenate([zeros, lax.slice_in_dim(v, 0, size + s, axis=axis)], axis=axis)
+
+
+def halo_box(packet, width):
+    for dim, axis in ((1, "gx"), (2, "yz"), (3, "grp")):
+        count = lax.axis_size(axis)
+        block = packet.shape[dim]
+        lo_piece = lax.slice_in_dim(packet, block - width, block, axis=dim)
+        hi_piece = lax.slice_in_dim(packet, 0, width, axis=dim)
+        if count == 2:
+            me = lax.axis_index(axis)
+            got = lax.ppermute(jnp.where(me == 0, lo_piece, hi_piece), axis, [(0, 1), (1, 0)])
+            zero = jnp.zeros_like(got)
+            from_below = jnp.where(me == 1, got, zero)
+            from_above = jnp.where(me == 0, got, zero)
+        else:
+            from_below = lax.ppermute(lo_piece, axis, [(i, i + 1) for i in range(count - 1)])
+            from_above = lax.ppermute(hi_piece, axis, [(i + 1, i) for i in range(count - 1)])
+        packet = jnp.concatenate([from_below, packet, from_above], axis=dim)
+    return packet
+
+
+def box_solver(coeff, flag_values, starts, totals, width):
+    bx, by, bz = coeff.shape
+    nx, ny, nz = bx + 2 * width, by + 2 * width, bz + 2 * width
+    flat = nx * ny
+    state = {}
+
+    def to_box(chans):
+        c = chans.shape[0]
+        return chans.transpose(0, 3, 1, 2).reshape(c, nz, flat)
+
+    def setup(coeffb, flagb):
+        pos = [starts[d] - width + jnp.arange(n, dtype=jnp.int32) for d, n in enumerate((nx, ny, nz))]
+        px = jnp.broadcast_to(pos[0][None, :, None], (nz, nx, ny)).reshape(nz, flat)
+        py = jnp.broadcast_to(pos[1][None, None, :], (nz, nx, ny)).reshape(nz, flat)
+        pz = jnp.broadcast_to(pos[2][:, None], (nz, flat))
+        pvals = (px, py, pz)
+        in_domain = (
+            (px >= 0) & (px < totals[0]) & (py >= 0) & (py < totals[1]) & (pz >= 0) & (pz < totals[2])
+        )
+        state["coeff"] = coeffb
+        state["g_lo"] = [jnp.where(pvals[d] > 0, 1.0, flagb) for d in range(3)]
+        state["g_hi"] = [jnp.where(pvals[d] < totals[d] - 1, 1.0, flagb) for d in range(3)]
+        state["inverse_diag"] = jnp.where(
+            in_domain, 1.0 / (coeffb * 3.5 + 3.0 * COARSE_PENALTY), 0.0
+        )
+
+    moves = ((4, ny), (4, 1), (3, 1))
+
+    def face_dim(v, d):
+        ax, st = moves[d]
+        low = lax.slice_in_dim(v, 0, 1, axis=d)
+        high = lax.slice_in_dim(v, 1, 2, axis=d)
+        tau = COARSE_PENALTY
+        low_term = tau * state["g_lo"][d] * low - tau * shift(high, ax, -st)
+        high_term = tau * state["g_hi"][d] * high - tau * shift(low, ax, st)
+        return jnp.concatenate([low_term, high_term], axis=d)
+
+    def apply_coarse(v):
+        block = state["coeff"] * (3.5 * v - jnp.flip(v, 0) - jnp.flip(v, 1) - jnp.flip(v, 2))
+        faces = face_dim(v, 0) + face_dim(v, 1) + face_dim(v, 2)
+        return block + faces
+
+    def solve(coarse_rhs):
+        chans = coarse_rhs.transpose(3, 0, 1, 2)
+        first = not state
+        if first:
+            chans = jnp.concatenate([chans, jnp.stack([coeff, flag_values])], axis=0)
+        box = to_box(halo_box(chans, width))
+        if first:
+            setup(box[8], box[9])
+            box = box[:8]
+        box = box.reshape(2, 2, 2, nz, flat)
+        inverse_diag = state["inverse_diag"]
+        center = 0.5 * (CHEB_HIGH + CHEB_LOW)
+        half_width = 0.5 * (CHEB_HIGH - CHEB_LOW)
+        sigma_value = center / half_width
+        rho_now = 1.0 / sigma_value
+        remain = box
+        update = inverse_diag * remain / center
+        result = update
+        for sweep_num in range(CHEB - 1):
+            remain = remain - apply_coarse(update)
+            rho_next = 1.0 / (2.0 * sigma_value - rho_now)
+            update = rho_next * rho_now * update + 2.0 * rho_next / half_width * (inverse_diag * remain)
+            result = result + update
+            rho_now = rho_next
+        own = result.reshape(8, nz, nx, ny)[:, width : width + bz, width : width + bx, width : width + by]
+        return own.transpose(2, 3, 1, 0)
+
+    return solve
 
 def _onehot_tables():
     idx = np.arange(DEG1**3)
@@ -226,6 +326,7 @@
         )
         return eigen_apply(solution, eigen_table, block_scale) + faces
 
+    solve_coarse = box_solver(coeff, flag_values, starts, totals, CHEB - 1)
     solution = jnp.zeros_like(rhs)
     for iteration in range(ITERS):
         residual = rhs if iteration == 0 else rhs - apply_fine(solution)
@@ -236,15 +337,7 @@
             precision=HIGHEST,
             preferred_element_type=jnp.float32,
         ).reshape(shape_three + (8,))
-        own_coefs = boundary_coefs(flag_values, starts, totals, COARSE_PENALTY)
-
-        def apply_own(values):
-            corners = values.reshape(values.shape[:3] + (2, 2, 2))
-            lower_list, upper_list = face_traces(corners, 2)
-            faces = face_term(corners, lower_list, upper_list, own_coefs, COARSE_PENALTY)
-            return (coarse_block(corners, coeff) + faces).reshape(values.shape)
-
-        coarse_sol = chebyshev(coarse_rhs, coeff, apply_own)
+        coarse_sol = solve_coarse(coarse_rhs)
         lifted = lax.dot_general(
             coarse_sol.reshape(-1, 8),
             restrict_table,

time: 174 us -> 110 us (0.63)
  the two profiles are of different devices: /device:TPU:249 before, /device:TPU:827 now
where the time goes in v3:
time: 110 us; the launch traced here: 109 us
  starting transfers between devices  47.5 us (43%)
  waiting for transfers between devices  25.7 us (23%)
  matrix products  18.9 us (17%)
  local copies, waits for them, and re-layouts  9.08 us (8%)
  other arithmetic  7.25 us (7%)
    ppermute x4, starting transfers between devices, halo_box(): lax.ppermute(lo_piece, axis, [(i, i + 1) for i in range(count - 1)])  16.1 us
    ppermute x4, waiting for transfers between devices, halo_box(): lax.ppermute(hi_piece, axis, [(i + 1, i) for i in range(count - 1)])  11.8 us
    ppermute x4, starting transfers between devices, halo_box(): lax.ppermute(hi_piece, axis, [(i + 1, i) for i in range(count - 1)])  10.3 us
    ppermute x2, starting transfers between devices, fine_face_term(): from_below = lax.ppermute(top, axis, [(i, i + 1) for i in range(count - 1)])  8.01 us
    ppermute x2, starting transfers between devices, fine_face_term(): lax.ppermute(bottom, axis, [(i + 1, i) for i in range(count - 1)])  6.52 us
    ppermute x2, waiting for transfers between devices, halo_box(): lax.ppermute(jnp.where(me == 0, lo_piece, hi_piece), axis, [(0, 1), (1, 0)])  5.99 us
    dot_general x3, matrix products, eigen_apply(): jnp.dot(flat, eigen_table, precision=HIGHEST, preferred_element_type=jnp....  5.47 us
    ppermute x2, starting transfers between devices, halo_box(): lax.ppermute(jnp.where(me == 0, lo_piece, hi_piece), axis, [(0, 1), (1, 0)])  4.4 us
  transfers between devices with their start and end apart: 15, of which 7 were waited for; matrix products, arithmetic and copies ran while one was open for 14% of the time, Pallas kernels for 0%

profile of v3, /device:TPU:827, one launch (start us, length us, event | category | flops | bytes accessed | tf_op | source)
XLA Modules:
  0.0 109.4 jit_solution(7753033535164311755)
XLA Ops:
  4.9 3.4 %collective-permute-start.1 = (f32[10,3,4,4]{0,3,2,1:T(4,128)S(1)}, f32[10,3,4,4]{0,3,2,1:T(4,128)S(1)}, u32[]{:S(2)}, u32[]{:S(2)}) collective-permute-start(f32[10,3,4,4]{0,3,2,1:T(4,128)S(1)} %pad_maximum_fusion.4), channel_id=1, source_target_pairs={{32,0},{64,32},{96,64},{128,96},{160,128},{192,160},{224,192},{256... | collective-permute-start | bytes 5768 | tf_op jit(solution)/shard_map/ppermute | solution.py:82
  8.3 1.9 %collective-permute-start = (f32[10,3,4,4]{0,3,2,1:T(4,128)S(1)}, f32[10,3,4,4]{0,3,2,1:T(4,128)S(1)}, u32[]{:S(2)}, u32[]{:S(2)}) collective-permute-start(f32[10,3,4,4]{0,3,2,1:T(4,128)S(1)} %pad_maximum_fusion.4), channel_id=1, source_target_pairs={{0,32},{32,64},{64,96},{96,128},{128,160},{160,192},{192,224},{224... | collective-permute-start | bytes 5768 | tf_op jit(solution)/shard_map/ppermute | solution.py:81
  18.3 4.4 %collective-permute-start.2 = (f32[10,9,3,4]{0,3,2,1:T(4,128)S(1)}, f32[10,9,3,4]{0,3,2,1:T(4,128)S(1)}, u32[]{:S(2)}, u32[]{:S(2)}) collective-permute-start(f32[10,9,3,4]{0,3,2,1:T(4,128)S(1)} %get-tuple-element.34), channel_id=1, source_target_pairs={{0,1},{1,2},{2,3},{3,4},{4,5},{5,6},{6,7},{7,8},{8,9},{9,10},{10,1... | collective-permute-start | bytes 12968 | tf_op jit(solution)/shard_map/ppermute | solution.py:81
  22.7 1.9 %collective-permute-start.3 = (f32[10,9,3,4]{0,3,2,1:T(4,128)S(1)}, f32[10,9,3,4]{0,3,2,1:T(4,128)S(1)}, u32[]{:S(2)}, u32[]{:S(2)}) collective-permute-start(f32[10,9,3,4]{0,3,2,1:T(4,128)S(1)} %get-tuple-element.35), channel_id=1, source_target_pairs={{1,0},{2,1},{3,2},{4,3},{5,4},{6,5},{7,6},{8,7},{9,8},{10,9},{11,1... | collective-permute-start | bytes 12968 | tf_op jit(solution)/shard_map/ppermute | solution.py:82
  24.7 6.5 %collective-permute-done.3 = f32[10,9,3,4]{0,3,2,1:T(4,128)S(1)} collective-permute-done((f32[10,9,3,4]{0,3,2,1:T(4,128)S(1)}, f32[10,9,3,4]{0,3,2,1:T(4,128)S(1)}, u32[]{:S(2)}, u32[]{:S(2)}) %collective-permute-start.3) | collective-permute-done | bytes 4352 | tf_op jit(solution)/shard_map/ppermute | solution.py:82
  31.4 2.3 %collective-permute-start.4 = (f32[10,9,10,3]{0,3,2,1:T(4,128)S(1)}, f32[10,9,10,3]{0,3,2,1:T(4,128)S(1)}, u32[]{:S(2)}, u32[]{:S(2)}) collective-permute-start(f32[10,9,10,3]{0,3,2,1:T(4,128)S(1)} %slice_select_fusion.1), channel_id=1, source_target_pairs={{0,512},{512,0},{1,513},{513,1},{2,514},{514,2},{3,515},{515,3},{4... | collective-permute-start | bytes 32408 | tf_op jit(solution)/shard_map/ppermute | solution.py:76
  34.6 3.1 %collective-permute-done.4 = f32[10,9,10,3]{0,3,2,1:T(4,128)S(1)} collective-permute-done((f32[10,9,10,3]{0,3,2,1:T(4,128)S(1)}, f32[10,9,10,3]{0,3,2,1:T(4,128)S(1)}, u32[]{:S(2)}, u32[]{:S(2)}) %collective-permute-start.4) | collective-permute-done | bytes 10832 | tf_op jit(solution)/shard_map/ppermute | solution.py:76
  43.2 2.2 %fusion.24 = f32[3,4,4,6,128]{4,2,3,1,0:T(4,128)S(1)} fusion(s32[6,128]{1,0:T(8,128)S(1)} %get-tuple-element.145, s32[6,128]{1,0:T(8,128)S(1)} %get-tuple-element.148, s32[512]{0:T(512)S(1)} %get-tuple-element.141, s32[512]{0:T(512)S(1)} %get-tuple-element.143, s32[512]{0:T(512)S(1)} %get-tuple-element.140, s32[512]{0:T(512)S(1)} %get-tuple-element.152, ...), kind=kOutput, calls=%fused_computation.60 | convolution fusion | flops 246153216 | bytes 273408 | tf_op jit(solution)/shard_map/dot_general | solution.py:180
  45.4 4.6 %collective-permute-start.6 = (f32[1,4,4,128]{3,2,1,0:T(4,128)S(1)}, f32[1,4,4,128]{3,2,1,0:T(4,128)S(1)}, u32[]{:S(2)}, u32[]{:S(2)}) collective-permute-start(f32[1,4,4,128]{3,2,1,0:T(4,128)S(1)} %get-tuple-element.30), channel_id=1, source_target_pairs={{32,0},{64,32},{96,64},{128,96},{160,128},{192,160},{224,192},{256... | collective-permute-start | bytes 24584 | tf_op jit(solution)/shard_map/ppermute | solution.py:198
  50.0 1.9 %collective-permute-start.5 = (f32[1,4,4,128]{3,2,1,0:T(4,128)S(1)}, f32[1,4,4,128]{3,2,1,0:T(4,128)S(1)}, u32[]{:S(2)}, u32[]{:S(2)}) collective-permute-start(f32[1,4,4,128]{3,2,1,0:T(4,128)S(1)} %get-tuple-element.31), channel_id=1, source_target_pairs={{0,32},{32,64},{64,96},{96,128},{128,160},{160,192},{192,224},{224... | collective-permute-start | bytes 24584 | tf_op jit(solution)/shard_map/ppermute | solution.py:197
  55.9 6.1 %collective-permute-start.7 = (f32[3,1,4,128]{3,2,0,1:T(4,128)S(1)}, f32[3,1,4,128]{3,2,0,1:T(4,128)S(1)}, u32[]{:S(2)}, u32[]{:S(2)}) collective-permute-start(f32[3,1,4,128]{3,2,0,1:T(4,128)S(1)} %slice_bitcast_fusion.9), channel_id=1, source_target_pairs={{0,1},{1,2},{2,3},{3,4},{4,5},{5,6},{6,7},{7,8},{8,9},{9,10},{10,1... | collective-permute-start | bytes 18440 | tf_op jit(solution)/shard_map/ppermute | solution.py:197
  62.0 1.9 %collective-permute-start.8 = (f32[3,1,4,128]{3,2,1,0:T(4,128)S(1)}, f32[3,1,4,128]{3,2,1,0:T(4,128)S(1)}, u32[]{:S(2)}, u32[]{:S(2)}) collective-permute-start(f32[3,1,4,128]{3,2,1,0:T(4,128)S(1)} %slice.520), channel_id=1, source_target_pairs={{1,0},{2,1},{3,2},{4,3},{5,4},{6,5},{7,6},{8,7},{9,8},{10,9},{11,1... | collective-permute-start | bytes 18440 | tf_op jit(solution)/shard_map/ppermute | solution.py:198
  64.0 2.1 %collective-permute-start.9 = (f32[3,4,1,128]{3,1,0,2:T(4,128)S(1)}, f32[3,4,1,128]{3,1,0,2:T(4,128)S(1)}, u32[]{:S(2)}, u32[]{:S(2)}) collective-permute-start(f32[3,4,1,128]{3,1,0,2:T(4,128)S(1)} %slice_select_fusion.2), channel_id=1, source_target_pairs={{0,512},{512,0},{1,513},{513,1},{2,514},{514,2},{3,515},{515,3},{4... | collective-permute-start | bytes 18440 | tf_op jit(solution)/shard_map/ppermute | solution.py:192
  66.2 3.7 %collective-permute-done.8 = f32[3,1,4,128]{3,2,1,0:T(4,128)S(1)} collective-permute-done((f32[3,1,4,128]{3,2,1,0:T(4,128)S(1)}, f32[3,1,4,128]{3,2,1,0:T(4,128)S(1)}, u32[]{:S(2)}, u32[]{:S(2)}) %collective-permute-start.8) | collective-permute-done | bytes 6176 | tf_op jit(solution)/shard_map/ppermute | solution.py:198
  70.2 2.0 %fusion.45 = f32[3,4,4,512]{3,2,1,0:T(4,128)S(1)} fusion(f32[3,4,4,512]{3,2,1,0:T(4,128)S(1)} %copy-done.4, f32[3,4,4,512]{3,2,1,0:T(4,128)S(1)} %reshape.569, s32[768]{0:T(1024)S(1)} %get-tuple-element.155, s32[768]{0:T(1024)S(1)} %get-tuple-element.156, s32[512]{0:T(512)S(1)} %get-tuple-element.141, s32[512]{0:T(512)S(1)} %get-tuple-element.143, ...), kind=kOutput, calls=%fused_computation.82 | convolution fusion | flops 246202368 | bytes 470016 | tf_op jit(solution)/shard_map/dot_general | solution.py:207
  72.5 3.1 %collective-permute-start.11 = (f32[8,3,4,4]{0,3,2,1:T(4,128)S(1)}, f32[8,3,4,4]{0,3,2,1:T(4,128)S(1)}, u32[]{:S(2)}, u32[]{:S(2)}) collective-permute-start(f32[8,3,4,4]{0,3,2,1:T(4,128)S(1)} %fusion.163), channel_id=1, source_target_pairs={{32,0},{64,32},{96,64},{128,96},{160,128},{192,160},{224,192},{256... | collective-permute-start | bytes 4616 | tf_op jit(solution)/shard_map/ppermute | solution.py:82
  75.7 2.2 %collective-permute-start.10 = (f32[8,3,4,4]{0,3,2,1:T(4,128)S(1)}, f32[8,3,4,4]{0,3,2,1:T(4,128)S(1)}, u32[]{:S(2)}, u32[]{:S(2)}) collective-permute-start(f32[8,3,4,4]{0,3,2,1:T(4,128)S(1)} %fusion.163), channel_id=1, source_target_pairs={{0,32},{32,64},{64,96},{96,128},{128,160},{160,192},{192,224},{224... | collective-permute-start | bytes 4616 | tf_op jit(solution)/shard_map/ppermute | solution.py:81
  77.9 3.5 %collective-permute-done.10 = f32[8,3,4,4]{0,3,2,1:T(4,128)S(1)} collective-permute-done((f32[8,3,4,4]{0,3,2,1:T(4,128)S(1)}, f32[8,3,4,4]{0,3,2,1:T(4,128)S(1)}, u32[]{:S(2)}, u32[]{:S(2)}) %collective-permute-start.10) | collective-permute-done | bytes 1568 | tf_op jit(solution)/shard_map/ppermute | solution.py:81
  81.5 7.6 %collective-permute-start.12 = (f32[8,9,3,4]{0,3,2,1:T(4,128)S(1)}, f32[8,9,3,4]{0,3,2,1:T(4,128)S(1)}, u32[]{:S(2)}, u32[]{:S(2)}) collective-permute-start(f32[8,9,3,4]{0,3,2,1:T(4,128)S(1)} %get-tuple-element.32), channel_id=1, source_target_pairs={{0,1},{1,2},{2,3},{3,4},{4,5},{5,6},{6,7},{7,8},{8,9},{9,10},{10,1... | collective-permute-start | bytes 10376 | tf_op jit(solution)/shard_map/ppermute | solution.py:81
  89.1 1.9 %collective-permute-start.13 = (f32[8,9,3,4]{0,3,2,1:T(4,128)S(1)}, f32[8,9,3,4]{0,3,2,1:T(4,128)S(1)}, u32[]{:S(2)}, u32[]{:S(2)}) collective-permute-start(f32[8,9,3,4]{0,3,2,1:T(4,128)S(1)} %get-tuple-element.33), channel_id=1, source_target_pairs={{1,0},{2,1},{3,2},{4,3},{5,4},{6,5},{7,6},{8,7},{9,8},{10,9},{11,1... | collective-permute-start | bytes 10376 | tf_op jit(solution)/shard_map/ppermute | solution.py:82
  91.0 1.8 %convolution_multiply_fusion.2 = f32[48,512]{0,1:T(8,128)S(1)} fusion(f32[48,512]{1,0:T(8,128)S(1)} %reshape.570, f32[512,512]{1,0:T(8,128)S(1)} %convolution_multiply_fusion, f32[512]{0:T(512)S(1)} %add.356, f32[48]{0:T(128)S(1)} %mul.639), kind=kOutput, calls=%fused_computation.74 | convolution fusion | flops 151068672 | bytes 1247424 | tf_op jit(solution)/shard_map/dot_general | solution.py:239
  92.8 5.3 %collective-permute-done.13 = f32[8,9,3,4]{0,3,2,1:T(4,128)S(1)} collective-permute-done((f32[8,9,3,4]{0,3,2,1:T(4,128)S(1)}, f32[8,9,3,4]{0,3,2,1:T(4,128)S(1)}, u32[]{:S(2)}, u32[]{:S(2)}) %collective-permute-start.13) | collective-permute-done | bytes 3488 | tf_op jit(solution)/shard_map/ppermute | solution.py:82
  98.3 2.1 %collective-permute-start.14 = (f32[8,9,10,3]{0,3,2,1:T(4,128)S(1)}, f32[8,9,10,3]{0,3,2,1:T(4,128)S(1)}, u32[]{:S(2)}, u32[]{:S(2)}) collective-permute-start(f32[8,9,10,3]{0,3,2,1:T(4,128)S(1)} %slice_select_fusion), channel_id=1, source_target_pairs={{0,512},{512,0},{1,513},{513,1},{2,514},{514,2},{3,515},{515,3},{4... | collective-permute-start | bytes 25928 | tf_op jit(solution)/shard_map/ppermute | solution.py:76
  101.6 2.9 %collective-permute-done.14 = f32[8,9,10,3]{0,3,2,1:T(4,128)S(1)} collective-permute-done((f32[8,9,10,3]{0,3,2,1:T(4,128)S(1)}, f32[8,9,10,3]{0,3,2,1:T(4,128)S(1)}, u32[]{:S(2)}, u32[]{:S(2)}) %collective-permute-start.14) | collective-permute-done | bytes 8672 | tf_op jit(solution)/shard_map/ppermute | solution.py:76
  (189 shorter events, 29.7 us)
Async XLA Ops:
  0.0 10.9 %copy-start = (f32[8,8]{1,0:T(8,128)S(1)}, f32[8,8]{1,0:T(8,128)}, u32[]{:S(2)}) copy-start(f32[8,8]{1,0:T(8,128)} %param.12) | copy-start | bytes 772
  0.0 10.9 %copy-start.3 = (f32[512,8]{1,0:T(8,128)S(1)}, f32[512,8]{1,0:T(8,128)}, u32[]{:S(2)}) copy-start(f32[512,8]{1,0:T(8,128)} %constant.194.clone) | copy-start | bytes 49156
  0.0 11.2 %copy-start.2 = (f32[512,8]{1,0:T(8,128)S(1)}, f32[512,8]{1,0:T(8,128)}, u32[]{:S(2)}) copy-start(f32[512,8]{1,0:T(8,128)} %constant.195.clone) | copy-start | bytes 49156
  0.0 10.2 %copy-start.6 = (f32[3,4,4]{2,1,0:T(4,128)S(1)}, f32[3,4,4]{2,1,0:T(4,128)}, u32[]{:S(2)}) copy-start(f32[3,4,4]{2,1,0:T(4,128)} %param.10) | copy-start | bytes 580
  0.0 10.6 %copy-start.7 = (f32[8]{0:T(128)S(1)}, f32[8]{0:T(128)}, u32[]{:S(2)}) copy-start(f32[8]{0:T(128)} %param.13) | copy-start | bytes 100
  3.5 8.0 %copy-start.1 = (f32[512,8]{1,0:T(8,128)S(1)}, f32[512,8]{1,0:T(8,128)}, u32[]{:S(2)}) copy-start(f32[512,8]{1,0:T(8,128)} %constant.196.clone) | copy-start | bytes 49156
  4.9 13.2 %collective-permute-start.1 = (f32[10,3,4,4]{0,3,2,1:T(4,128)S(1)}, f32[10,3,4,4]{0,3,2,1:T(4,128)S(1)}, u32[]{:S(2)}, u32[]{:S(2)}) collective-permute-start(f32[10,3,4,4]{0,3,2,1:T(4,128)S(1)} %pad_maximum_fusion.4), channel_id=1, source_target_pairs={{32,0},{64,32},{96,64},{128,96},{160,128},{192,160},{224,192},{256... | collective-permute-start | bytes 5768 | tf_op jit(solution)/shard_map/ppermute | solution.py:82
  8.3 9.8 %collective-permute-start = (f32[10,3,4,4]{0,3,2,1:T(4,128)S(1)}, f32[10,3,4,4]{0,3,2,1:T(4,128)S(1)}, u32[]{:S(2)}, u32[]{:S(2)}) collective-permute-start(f32[10,3,4,4]{0,3,2,1:T(4,128)S(1)} %pad_maximum_fusion.4), channel_id=1, source_target_pairs={{0,32},{32,64},{64,96},{96,128},{128,160},{160,192},{192,224},{224... | collective-permute-start | bytes 5768 | tf_op jit(solution)/shard_map/ppermute | solution.py:81
  16.8 1.3 %copy-start.5 = (s32[3,4,4]{2,1,0:T(4,128)S(1)}, s32[3,4,4]{2,1,0:T(4,128)}, u32[]{:S(2)}) copy-start(s32[3,4,4]{2,1,0:T(4,128)} %param.11) | copy-start | bytes 580
  18.3 6.4 %collective-permute-start.2 = (f32[10,9,3,4]{0,3,2,1:T(4,128)S(1)}, f32[10,9,3,4]{0,3,2,1:T(4,128)S(1)}, u32[]{:S(2)}, u32[]{:S(2)}) collective-permute-start(f32[10,9,3,4]{0,3,2,1:T(4,128)S(1)} %get-tuple-element.34), channel_id=1, source_target_pairs={{0,1},{1,2},{2,3},{3,4},{4,5},{5,6},{6,7},{7,8},{8,9},{9,10},{10,1... | collective-permute-start | bytes 12968 | tf_op jit(solution)/shard_map/ppermute | solution.py:81
  22.7 8.5 %collective-permute-start.3 = (f32[10,9,3,4]{0,3,2,1:T(4,128)S(1)}, f32[10,9,3,4]{0,3,2,1:T(4,128)S(1)}, u32[]{:S(2)}, u32[]{:S(2)}) collective-permute-start(f32[10,9,3,4]{0,3,2,1:T(4,128)S(1)} %get-tuple-element.35), channel_id=1, source_target_pairs={{1,0},{2,1},{3,2},{4,3},{5,4},{6,5},{7,6},{8,7},{9,8},{10,9},{11,1... | collective-permute-start | bytes 12968 | tf_op jit(solution)/shard_map/ppermute | solution.py:82
  31.4 6.3 %collective-permute-start.4 = (f32[10,9,10,3]{0,3,2,1:T(4,128)S(1)}, f32[10,9,10,3]{0,3,2,1:T(4,128)S(1)}, u32[]{:S(2)}, u32[]{:S(2)}) collective-permute-start(f32[10,9,10,3]{0,3,2,1:T(4,128)S(1)} %slice_select_fusion.1), channel_id=1, source_target_pairs={{0,512},{512,0},{1,513},{513,1},{2,514},{514,2},{3,515},{515,3},{4... | collective-permute-start | bytes 32408 | tf_op jit(solution)/shard_map/ppermute | solution.py:76
  45.4 10.3 %collective-permute-start.6 = (f32[1,4,4,128]{3,2,1,0:T(4,128)S(1)}, f32[1,4,4,128]{3,2,1,0:T(4,128)S(1)}, u32[]{:S(2)}, u32[]{:S(2)}) collective-permute-start(f32[1,4,4,128]{3,2,1,0:T(4,128)S(1)} %get-tuple-element.30), channel_id=1, source_target_pairs={{32,0},{64,32},{96,64},{128,96},{160,128},{192,160},{224,192},{256... | collective-permute-start | bytes 24584 | tf_op jit(solution)/shard_map/ppermute | solution.py:198
  50.0 5.6 %collective-permute-start.5 = (f32[1,4,4,128]{3,2,1,0:T(4,128)S(1)}, f32[1,4,4,128]{3,2,1,0:T(4,128)S(1)}, u32[]{:S(2)}, u32[]{:S(2)}) collective-permute-start(f32[1,4,4,128]{3,2,1,0:T(4,128)S(1)} %get-tuple-element.31), channel_id=1, source_target_pairs={{0,32},{32,64},{64,96},{96,128},{128,160},{160,192},{192,224},{224... | collective-permute-start | bytes 24584 | tf_op jit(solution)/shard_map/ppermute | solution.py:197
  53.8 16.4 %copy-start.4 = (f32[3,4,4,512]{3,2,1,0:T(4,128)S(1)}, f32[3,4,4,512]{3,2,1,0:T(4,128)}, u32[]{:S(2)}) copy-start(f32[3,4,4,512]{3,2,1,0:T(4,128)} %param.9) | copy-start | bytes 294916
  55.9 10.2 %collective-permute-start.7 = (f32[3,1,4,128]{3,2,0,1:T(4,128)S(1)}, f32[3,1,4,128]{3,2,0,1:T(4,128)S(1)}, u32[]{:S(2)}, u32[]{:S(2)}) collective-permute-start(f32[3,1,4,128]{3,2,0,1:T(4,128)S(1)} %slice_bitcast_fusion.9), channel_id=1, source_target_pairs={{0,1},{1,2},{2,3},{3,4},{4,5},{5,6},{6,7},{7,8},{8,9},{9,10},{10,1... | collective-permute-start | bytes 18440 | tf_op jit(solution)/shard_map/ppermute | solution.py:197
  62.0 8.0 %collective-permute-start.8 = (f32[3,1,4,128]{3,2,1,0:T(4,128)S(1)}, f32[3,1,4,128]{3,2,1,0:T(4,128)S(1)}, u32[]{:S(2)}, u32[]{:S(2)}) collective-permute-start(f32[3,1,4,128]{3,2,1,0:T(4,128)S(1)} %slice.520), channel_id=1, source_target_pairs={{1,0},{2,1},{3,2},{4,3},{5,4},{6,5},{7,6},{8,7},{9,8},{10,9},{11,1... | collective-permute-start | bytes 18440 | tf_op jit(solution)/shard_map/ppermute | solution.py:198
  64.0 6.0 %collective-permute-start.9 = (f32[3,4,1,128]{3,1,0,2:T(4,128)S(1)}, f32[3,4,1,128]{3,1,0,2:T(4,128)S(1)}, u32[]{:S(2)}, u32[]{:S(2)}) collective-permute-start(f32[3,4,1,128]{3,1,0,2:T(4,128)S(1)} %slice_select_fusion.2), channel_id=1, source_target_pairs={{0,512},{512,0},{1,513},{513,1},{2,514},{514,2},{3,515},{515,3},{4... | collective-permute-start | bytes 18440 | tf_op jit(solution)/shard_map/ppermute | solution.py:192
  72.5 5.3 %collective-permute-start.11 = (f32[8,3,4,4]{0,3,2,1:T(4,128)S(1)}, f32[8,3,4,4]{0,3,2,1:T(4,128)S(1)}, u32[]{:S(2)}, u32[]{:S(2)}) collective-permute-start(f32[8,3,4,4]{0,3,2,1:T(4,128)S(1)} %fusion.163), channel_id=1, source_target_pairs={{32,0},{64,32},{96,64},{128,96},{160,128},{192,160},{224,192},{256... | collective-permute-start | bytes 4616 | tf_op jit(solution)/shard_map/ppermute | solution.py:82
  75.7 5.8 %collective-permute-start.10 = (f32[8,3,4,4]{0,3,2,1:T(4,128)S(1)}, f32[8,3,4,4]{0,3,2,1:T(4,128)S(1)}, u32[]{:S(2)}, u32[]{:S(2)}) collective-permute-start(f32[8,3,4,4]{0,3,2,1:T(4,128)S(1)} %fusion.163), channel_id=1, source_target_pairs={{0,32},{32,64},{64,96},{96,128},{128,160},{160,192},{192,224},{224... | collective-permute-start | bytes 4616 | tf_op jit(solution)/shard_map/ppermute | solution.py:81
  81.5 11.3 %collective-permute-start.12 = (f32[8,9,3,4]{0,3,2,1:T(4,128)S(1)}, f32[8,9,3,4]{0,3,2,1:T(4,128)S(1)}, u32[]{:S(2)}, u32[]{:S(2)}) collective-permute-start(f32[8,9,3,4]{0,3,2,1:T(4,128)S(1)} %get-tuple-element.32), channel_id=1, source_target_pairs={{0,1},{1,2},{2,3},{3,4},{4,5},{5,6},{6,7},{7,8},{8,9},{9,10},{10,1... | collective-permute-start | bytes 10376 | tf_op jit(solution)/shard_map/ppermute | solution.py:81
  89.1 9.1 %collective-permute-start.13 = (f32[8,9,3,4]{0,3,2,1:T(4,128)S(1)}, f32[8,9,3,4]{0,3,2,1:T(4,128)S(1)}, u32[]{:S(2)}, u32[]{:S(2)}) collective-permute-start(f32[8,9,3,4]{0,3,2,1:T(4,128)S(1)} %get-tuple-element.33), channel_id=1, source_target_pairs={{1,0},{2,1},{3,2},{4,3},{5,4},{6,5},{7,6},{8,7},{9,8},{10,9},{11,1... | collective-permute-start | bytes 10376 | tf_op jit(solution)/shard_map/ppermute | solution.py:82
  98.3 6.3 %collective-permute-start.14 = (f32[8,9,10,3]{0,3,2,1:T(4,128)S(1)}, f32[8,9,10,3]{0,3,2,1:T(4,128)S(1)}, u32[]{:S(2)}, u32[]{:S(2)}) collective-permute-start(f32[8,9,10,3]{0,3,2,1:T(4,128)S(1)} %slice_select_fusion), channel_id=1, source_target_pairs={{0,512},{512,0},{1,513},{513,1},{2,514},{514,2},{3,515},{515,3},{4... | collective-permute-start | bytes 25928 | tf_op jit(solution)/shard_map/ppermute | solution.py:76

commit v4 on v1

v4 whole, which is shorter than its diff:
```python
import jax
import jax.numpy as jnp
import numpy as np
from jax import lax
from jax.sharding import PartitionSpec as P

DEG1 = 8
ITERS = 2
CHEB = 4


PENALTY = 2.0
COARSE_PENALTY = 1.0
DAMPING = 0.5
CHEB_LOW = 0.1
CHEB_HIGH = 2.0
GLL_POINTS = (
    -1.0,
    -0.8717401485096066,
    -0.5917001814331423,
    -0.2092992179024789,
    0.2092992179024789,
    0.5917001814331423,
    0.8717401485096066,
    1.0,
)
HIGHEST = lax.Precision.HIGHEST


def face_traces(field, points):
    lower_list, upper_list = ([], [])
    for dimension, axis in enumerate(("gx", "yz", "grp")):
        count = lax.axis_size(axis)
        block = field.shape[dimension]
        node_axis = 3 + dimension
        high = lax.slice_in_dim(field, points - 1, points, axis=node_axis)
        low = lax.slice_in_dim(field, 0, 1, axis=node_axis)
        top = lax.slice_in_dim(high, block - 1, block, axis=dimension)
        bottom = lax.slice_in_dim(low, 0, 1, axis=dimension)
        if count == 2:
            me = lax.axis_index(axis)
            got = lax.ppermute(jnp.where(me == 0, top, bottom), axis, [(0, 1), (1, 0)])
            zero = jnp.zeros_like(got)
            from_below = jnp.where(me == 1, got, zero)
            from_above = jnp.where(me == 0, got, zero)
        else:
            from_below = lax.ppermute(top, axis, [(i, i + 1) for i in range(count - 1)])
            from_above = lax.ppermute(bottom, axis, [(i + 1, i) for i in range(count - 1)])
        lower_list.append(
            jnp.concatenate([from_below, lax.slice_in_dim(high, 0, block - 1, axis=dimension)], axis=dimension)
        )
        upper_list.append(
            jnp.concatenate([lax.slice_in_dim(low, 1, block, axis=dimension), from_above], axis=dimension)
        )
    return (lower_list, upper_list)


def shift(v, axis, s):
    size = v.shape[axis]
    zshape = list(v.shape)
    zshape[axis] = abs(s)
    zeros = jnp.zeros(zshape, v.dtype)
    if s > 0:
        return jnp.concatenate([lax.slice_in_dim(v, s, size, axis=axis), zeros], axis=axis)
    return jnp.concatenate([zeros, lax.slice_in_dim(v, 0, size + s, axis=axis)], axis=axis)


def pack(parts):
    return jnp.concatenate([p.reshape(-1) for p in parts])


def unpack(flat, likes):
    out, at = [], 0
    for like in likes:
        size = like.size
        out.append(flat[at : at + size].reshape(like.shape))
        at += size
    return out


def halo_box(packet, width, extras=None):
    extras = extras or {}
    received = {}
    for dim, axis in ((3, "grp"), (2, "yz"), (1, "gx")):
        count = lax.axis_size(axis)
        block = packet.shape[dim]
        reach = -(-width // block)
        lows, highs = [], []
        for k in range(1, reach + 1):
            take = min(block, width - (k - 1) * block)
            lo_piece = lax.slice_in_dim(packet, block - take, block, axis=dim)
            hi_piece = lax.slice_in_dim(packet, 0, take, axis=dim)
            lo_send, hi_send = [lo_piece], [hi_piece]
            if k == 1 and axis in extras:
                lo_send.append(extras[axis][0])
                hi_send.append(extras[axis][1])
            if count == 2:
                me = lax.axis_index(axis)
                got = lax.ppermute(jnp.where(me == 0, pack(lo_send), pack(hi_send)), axis, [(0, 1), (1, 0)])
                got = unpack(got, lo_send)
                lo_got = [jnp.where(me == 1, g, jnp.zeros_like(g)) for g in got]
                hi_got = [jnp.where(me == 0, g, jnp.zeros_like(g)) for g in got]
            else:
                up = [(i, i + k) for i in range(count - k)]
                down = [(i + k, i) for i in range(count - k)]
                lo_got = unpack(lax.ppermute(pack(lo_send), axis, up), lo_send)
                hi_got = unpack(lax.ppermute(pack(hi_send), axis, down), hi_send)
            lows.append(lo_got[0])
            highs.append(hi_got[0])
            if len(lo_got) > 1:
                received[axis] = (lo_got[1], hi_got[1])
        packet = jnp.concatenate(lows[::-1] + [packet] + highs, axis=dim)
    return packet, received


def box_geometry(statics, starts, totals, width, block):
    nx, ny, nz = (b + 2 * width for b in block)
    flat = nx * ny

    def to_box(chans):
        c = chans.shape[0]
        return chans.transpose(0, 3, 1, 2).reshape(c, nz, flat)

    st = to_box(statics)
    coeffb, flagb = st[0], st[1]
    pos = [starts[d] - width + jnp.arange(n, dtype=jnp.int32) for d, n in enumerate((nx, ny, nz))]
    px = jnp.broadcast_to(pos[0][None, :, None], (nz, nx, ny)).reshape(nz, flat)
    py = jnp.broadcast_to(pos[1][None, None, :], (nz, nx, ny)).reshape(nz, flat)
    pz = jnp.broadcast_to(pos[2][:, None], (nz, flat))
    pvals = (px, py, pz)
    in_domain = (
        (px >= 0) & (px < totals[0]) & (py >= 0) & (py < totals[1]) & (pz >= 0) & (pz < totals[2])
    )
    g_lo = [jnp.where(pvals[d] > 0, 1.0, flagb) for d in range(3)]
    g_hi = [jnp.where(pvals[d] < totals[d] - 1, 1.0, flagb) for d in range(3)]
    inverse_diag = jnp.where(in_domain, 1.0 / (coeffb * 3.5 + 3.0 * COARSE_PENALTY), 0.0)
    moves = ((4, ny), (4, 1), (3, 1))

    def face_dim(v, d):
        ax, stp = moves[d]
        low = lax.slice_in_dim(v, 0, 1, axis=d)
        high = lax.slice_in_dim(v, 1, 2, axis=d)
        tau = COARSE_PENALTY
        low_term = tau * g_lo[d] * low - tau * shift(high, ax, -stp)
        high_term = tau * g_hi[d] * high - tau * shift(low, ax, stp)
        return jnp.concatenate([low_term, high_term], axis=d)

    def apply_coarse(v):
        blk = coeffb * (3.5 * v - jnp.flip(v, 0) - jnp.flip(v, 1) - jnp.flip(v, 2))
        faces = face_dim(v, 0) + face_dim(v, 1) + face_dim(v, 2)
        return blk + faces

    def solve(chans):
        box = to_box(chans).reshape(2, 2, 2, nz, flat)
        center = 0.5 * (CHEB_HIGH + CHEB_LOW)
        half_width = 0.5 * (CHEB_HIGH - CHEB_LOW)
        sigma_value = center / half_width
        rho_now = 1.0 / sigma_value
        remain = box
        update = inverse_diag * remain / center
        result = update
        for sweep_num in range(CHEB - 1):
            remain = remain - apply_coarse(update)
            rho_next = 1.0 / (2.0 * sigma_value - rho_now)
            update = rho_next * rho_now * update + 2.0 * rho_next / half_width * (inverse_diag * remain)
            result = result + update
            rho_now = rho_next
        result = result.reshape(8, nz, nx, ny)

        def take(ranges):
            (x0, x1), (y0, y1), (z0, z1) = ranges
            return result[:, z0:z1, x0:x1, y0:y1].transpose(2, 3, 1, 0)

        return take

    return solve


def _onehot_tables():
    idx = np.arange(DEG1**3)
    picks = [idx // (DEG1 * DEG1), (idx // DEG1) % DEG1, idx % DEG1]
    return np.stack([(p[:, None] == np.arange(DEG1)[None, :]) for p in picks]).astype(np.float32)


ONEHOT = _onehot_tables()


def face_select():
    n = lax.broadcasted_iota(jnp.int32, (DEG1**3, 6 * 128), 0)
    c = lax.broadcasted_iota(jnp.int32, (DEG1**3, 6 * 128), 1)
    face, spot = c // 128, c % 128
    dim, side = face // 2, face % 2
    n0, n1, n2 = n // (DEG1 * DEG1), (n // DEG1) % DEG1, n % DEG1
    along = jnp.where(dim == 0, n0, jnp.where(dim == 1, n1, n2))
    rest = jnp.where(dim == 0, n1 * DEG1 + n2, jnp.where(dim == 1, n0 * DEG1 + n2, n0 * DEG1 + n1))
    return ((along == side * (DEG1 - 1)) & (spot == rest)).astype(jnp.float32)


def build_tables(basis, eigenvalues):
    eigen_table = None
    for pick in ONEHOT:
        pick = jnp.asarray(pick)
        part = lax.dot_general(
            jnp.dot(pick, basis, precision=HIGHEST, preferred_element_type=jnp.float32),
            pick,
            (((1,), (1,)), ((), ())),
            precision=HIGHEST,
            preferred_element_type=jnp.float32,
        )
        eigen_table = part if eigen_table is None else eigen_table * part
    spectrum = (
        eigenvalues[:, None, None] + eigenvalues[None, :, None] + eigenvalues[None, None, :]
    ).reshape(-1)
    points = jnp.array(np.array(GLL_POINTS), jnp.float32)
    linear = jnp.stack([(1.0 - points) * 0.5, (1.0 + points) * 0.5])
    restrict_table = (
        linear.T[:, None, None, :, None, None]
        * linear.T[None, :, None, None, :, None]
        * linear.T[None, None, :, None, None, :]
    ).reshape(DEG1**3, 8)
    return (eigen_table, spectrum, restrict_table)


def boundary_coefs(flag_values, starts, totals, penalty):
    result_list = []
    for dimension in range(3):
        position = starts[dimension] + lax.broadcasted_iota(jnp.int32, flag_values.shape, dimension)
        lower_coef = penalty * jnp.where(position > 0, 1.0, flag_values)
        upper_coef = penalty * jnp.where(position < totals[dimension] - 1, 1.0, flag_values)
        result_list.append((lower_coef[..., None, None, None], upper_coef[..., None, None, None]))
    return result_list


def eigen_apply(flat, eigen_table, scale):
    inside = jnp.dot(flat, eigen_table, precision=HIGHEST, preferred_element_type=jnp.float32)
    return lax.dot_general(
        inside * scale, eigen_table, (((1,), (1,)), ((), ())), precision=HIGHEST,
        preferred_element_type=jnp.float32,
    )


def mm(a, b):
    return jnp.dot(a, b, precision=HIGHEST, preferred_element_type=jnp.float32)


def mm_t(a, b):
    return lax.dot_general(
        a, b, (((1,), (1,)), ((), ())), precision=HIGHEST, preferred_element_type=jnp.float32
    )


def body(rhs, coeff, flags, basis, eigenvalues):
    eigen_table, spectrum, restrict_table = build_tables(basis, eigenvalues)
    shape_three = rhs.shape[:3]
    node_count = rhs.shape[3]
    count = rhs.size // node_count
    axes = ("gx", "yz", "grp")
    flag_values = flags.astype(jnp.float32)
    starts = tuple(lax.axis_index(a) * shape_three[d] for d, a in enumerate(axes))
    totals = tuple(shape_three[d] * lax.axis_size(a) for d, a in enumerate(axes))
    fine_coefs = boundary_coefs(flag_values, starts, totals, PENALTY)
    coeff2 = coeff.reshape(count, 1)
    block_scale = coeff2 * spectrum[None, :]
    inverse_scale = 1.0 / block_scale
    select = face_select()
    restrict_faces = lax.dot_general(
        restrict_table, select, (((0,), (0,)), ((), ())), precision=HIGHEST,
        preferred_element_type=jnp.float32,
    )
    wide = CHEB
    narrow = CHEB - 1

    rhs2 = rhs.reshape(count, node_count)
    smoothed0 = eigen_apply(rhs2, eigen_table, inverse_scale)
    q0 = mm(rhs2, restrict_table)
    s_faces = mm(smoothed0, select).reshape(shape_three + (6, 128))

    def face_of(faces, d, side, lo, hi):
        return lax.slice_in_dim(faces[..., 2 * d + side, :], lo, hi, axis=d)

    bx, by, bz = shape_three
    extras = {
        "gx": (face_of(s_faces, 0, 1, bx - 1, bx), face_of(s_faces, 0, 0, 0, 1)),
        "yz": (face_of(s_faces, 1, 1, by - 1, by), face_of(s_faces, 1, 0, 0, 1)),
    }
    z_count = lax.axis_size("grp")
    z_top, z_bottom = face_of(s_faces, 2, 1, bz - 1, bz), face_of(s_faces, 2, 0, 0, 1)
    if z_count == 2:
        me = lax.axis_index("grp")
        got = lax.ppermute(jnp.where(me == 0, z_top, z_bottom), "grp", [(0, 1), (1, 0)])
        z_recv = (jnp.where(me == 1, got, jnp.zeros_like(got)), jnp.where(me == 0, got, jnp.zeros_like(got)))
    else:
        z_recv = (
            lax.ppermute(z_top, "grp", [(i, i + 1) for i in range(z_count - 1)]),
            lax.ppermute(z_bottom, "grp", [(i + 1, i) for i in range(z_count - 1)]),
        )

    packet0 = jnp.concatenate(
        [q0.T.reshape((8,) + shape_three), jnp.stack([coeff, flag_values])], axis=0
    )
    box0, received = halo_box(packet0, wide, extras)
    received["grp"] = z_recv
    statics = box0[8:10]
    take0 = box_geometry(statics, starts, totals, wide, shape_three)(box0[:8])
    own = [(wide, wide + b) for b in shape_three]
    c0_own = take0(own).reshape(count, 8)
    u1 = DAMPING * (smoothed0 + mm_t(c0_own, restrict_table))

    u_faces = mm(u1, select).reshape(shape_three + (6, 128))
    terms = []
    for d, axis in enumerate(axes):
        block = shape_three[d]
        below = list(own)
        below[d] = (wide - 1, wide)
        above = list(own)
        above[d] = (wide + block, wide + block + 1)
        planes = []
        for rng, side, got in ((below, 1, received[axis][0]), (above, 0, received[axis][1])):
            c = take0(rng)
            lifted = mm(c.reshape(-1, 8), restrict_faces).reshape(c.shape[:3] + (6, 128))
            planes.append(DAMPING * (got + lifted[..., 2 * d + side, :]))
        low = u_faces[..., 2 * d, :]
        high = u_faces[..., 2 * d + 1, :]
        lower = jnp.concatenate([planes[0], lax.slice_in_dim(high, 0, block - 1, axis=d)], axis=d)
        upper = jnp.concatenate([lax.slice_in_dim(low, 1, block, axis=d), planes[1]], axis=d)
        lower_coef, upper_coef = fine_coefs[d]
        lower_coef = lower_coef.reshape(shape_three + (1,))
        upper_coef = upper_coef.reshape(shape_three + (1,))
        terms.append(lower_coef * low - PENALTY * lower)
        terms.append(upper_coef * high - PENALTY * upper)
    terms = jnp.stack(terms, axis=3).reshape(count, 6 * 128)
    faces = mm_t(terms, select)
    residual = rhs2 - (eigen_apply(u1, eigen_table, block_scale) + faces)
    smoothed1 = eigen_apply(residual, eigen_table, inverse_scale)
    q1 = mm(residual, restrict_table)
    box1, _ = halo_box(q1.T.reshape((8,) + shape_three), narrow)
    cut = wide - narrow
    statics1 = statics[:, cut:-cut, cut:-cut, cut:-cut]
    take1 = box_geometry(statics1, starts, totals, narrow, shape_three)(box1)
    c1_own = take1([(narrow, narrow + b) for b in shape_three]).reshape(count, 8)
    u2 = u1 + DAMPING * (smoothed1 + mm_t(c1_own, restrict_table))
    return u2.reshape(rhs.shape)


def solution(mesh):
    in_specs = (P("gx", "yz", "grp", None), P("gx", "yz", "grp"), P("gx", "yz", "grp"), P(), P())
    out_specs = P("gx", "yz", "grp", None)
    return jax.shard_map(body, mesh=mesh, in_specs=in_specs, out_specs=out_specs, check_vma=False)
```

time: 233 us -> 132 us (0.57)
  the two profiles are of different devices: /device:TPU:4 before, /device:TPU:791 now
where the time goes in v4:
time: 132 us; the launch traced here: 131 us
  starting transfers between devices  45.2 us (34%)
  local copies, waits for them, and re-layouts  41 us (31%)
  matrix products  17 us (13%)
  other arithmetic  15.2 us (12%)
  waiting for transfers between devices  10.3 us (8%)
  between operations  1.94 us (1%)
    ppermute x5, starting transfers between devices, halo_box(): lo_got = unpack(lax.ppermute(pack(lo_send), axis, up), lo_send)  23.7 us
    ppermute x5, starting transfers between devices, halo_box(): hi_got = unpack(lax.ppermute(pack(hi_send), axis, down), hi_send)  14 us
    reshape x22, local copies, waits for them, and re-layouts, unpack(): out.append(flat[at:at + size].reshape(like.shape))  6.88 us
    ppermute x2, starting transfers between devices, halo_box(): lax.ppermute(jnp.where(me == 0, pack(lo_send), pack(hi_send)), axis, [(0,...  5.51 us
    transpose x4, local copies, waits for them, and re-layouts, to_box(): return chans.transpose(0, 3, 1, 2).reshape(c, nz, flat)  5.46 us
    ppermute x5, waiting for transfers between devices, halo_box(): lo_got = unpack(lax.ppermute(pack(lo_send), axis, up), lo_send)  4.71 us
    ppermute x5, waiting for transfers between devices, halo_box(): hi_got = unpack(lax.ppermute(pack(hi_send), axis, down), hi_send)  4.37 us
    dot_general x10, matrix products, mm(): return jnp.dot(a, b, precision=HIGHEST, preferred_element_type=jnp.float32)  3.81 us
  transfers between devices with their start and end apart: 13, of which 4 were waited for; matrix products, arithmetic and copies ran while one was open for 39% of the time, Pallas kernels for 0%

profile of v4, /device:TPU:791, one launch (start us, length us, event | category | flops | bytes accessed | tf_op | source)
XLA Modules:
  0.0 130.7 jit_solution(14393018774607307187)
XLA Ops:
  3.6 1.2 fusion.127
  5.2 3.2 %collective-permute-start = (f32[480]{0:T(512)S(1)}, f32[480]{0:T(512)S(1)}, u32[]{:S(2)}, u32[]{:S(2)}) collective-permute-start(f32[480]{0:T(512)S(1)} %reshape.978), channel_id=1, source_target_pairs={{0,512},{512,0},{1,513},{513,1},{2,514},{514,2},{3,515},{515,3},{4... | collective-permute-start | bytes 5768 | tf_op jit(solution)/shard_map/ppermute | solution.py:99
  15.7 1.3 fusion.25
  18.4 2.1 %collective-permute-start.7 = (f32[3,4,1,128]{3,1,0,2:T(4,128)}, f32[3,4,1,128]{3,1,0,2:T(4,128)}, u32[]{:S(2)}, u32[]{:S(2)}) collective-permute-start(f32[3,4,1,128]{3,1,0,2:T(4,128)} %slice_select_fusion.1), channel_id=1, source_target_pairs={{0,512},{512,0},{1,513},{513,1},{2,514},{514,2},{3,515},{515,3},{4... | collective-permute-start | bytes 18440 | tf_op jit(solution)/shard_map/ppermute | solution.py:290
  25.0 1.6 %fusion.22 = f32[6,128,8]{1,2,0:T(8,128)S(1)} fusion(f32[512,8,1]{0,1,2:T(8,128)S(1)} %reshape.1017, s32[6,128]{1,0:T(8,128)S(1)} %get-tuple-element.179, s32[6,128]{1,0:T(8,128)S(1)} %get-tuple-element.182, s32[512]{0:T(512)S(1)} %get-tuple-element.151, s32[512]{0:T(512)S(1)} %get-tuple-element.153, s32[512]{0:T(512)S(1)} %get-tuple-element.150, ...), kind=kOutput, calls=%fused_computation.58 | convolution fusion | flops 57409536 | bytes 68608 | tf_op jit(solution)/shard_map/dot_general | solution.py:266
  27.8 6.5 %collective-permute-start.1 = (f32[2976]{0:T(1024)S(1)}, f32[2976]{0:T(1024)S(1)}, u32[]{:S(2)}, u32[]{:S(2)}) collective-permute-start(f32[2976]{0:T(1024)S(1)} %get-tuple-element.134), channel_id=1, source_target_pairs={{0,1},{1,2},{2,3},{3,4},{4,5},{5,6},{6,7},{7,8},{8,9},{9,10},{10,1... | collective-permute-start | bytes 35720 | tf_op jit(solution)/shard_map/ppermute | solution.py:106
  34.4 1.9 %collective-permute-start.2 = (f32[2976]{0:T(1024)S(1)}, f32[2976]{0:T(1024)S(1)}, u32[]{:S(2)}, u32[]{:S(2)}) collective-permute-start(f32[2976]{0:T(1024)S(1)} %get-tuple-element.135), channel_id=1, source_target_pairs={{1,0},{2,1},{3,2},{4,3},{5,4},{6,5},{7,6},{8,7},{9,8},{10,9},{11,1... | collective-permute-start | bytes 35720 | tf_op jit(solution)/shard_map/ppermute | solution.py:107
  46.7 3.4 %collective-permute-start.6 = (f32[1440]{0:T(1024)S(1)}, f32[1440]{0:T(1024)S(1)}, u32[]{:S(2)}, u32[]{:S(2)}) collective-permute-start(f32[1440]{0:T(1024)S(1)} %reshape.992), channel_id=1, source_target_pairs={{64,0},{96,32},{128,64},{160,96},{192,128},{224,160},{256,192},{28... | collective-permute-start | bytes 17288 | tf_op jit(solution)/shard_map/ppermute | solution.py:107
  50.4 2.8 %collective-permute-start.3 = (f32[1440]{0:T(1024)S(1)}, f32[1440]{0:T(1024)S(1)}, u32[]{:S(2)}, u32[]{:S(2)}) collective-permute-start(f32[1440]{0:T(1024)S(1)} %reshape.985), channel_id=1, source_target_pairs={{0,64},{32,96},{64,128},{96,160},{128,192},{160,224},{192,256},{22... | collective-permute-start | bytes 17288 | tf_op jit(solution)/shard_map/ppermute | solution.py:106
  53.3 4.6 %collective-permute-start.5 = (f32[6368]{0:T(1024)S(1)}, f32[6368]{0:T(1024)S(1)}, u32[]{:S(2)}, u32[]{:S(2)}) collective-permute-start(f32[6368]{0:T(1024)S(1)} %get-tuple-element.120), channel_id=1, source_target_pairs={{32,0},{64,32},{96,64},{128,96},{160,128},{192,160},{224,192},{256... | collective-permute-start | bytes 76424 | tf_op jit(solution)/shard_map/ppermute | solution.py:107
  57.9 2.1 %collective-permute-start.4 = (f32[6368]{0:T(1024)S(1)}, f32[6368]{0:T(1024)S(1)}, u32[]{:S(2)}, u32[]{:S(2)}) collective-permute-start(f32[6368]{0:T(1024)S(1)} %get-tuple-element.121), channel_id=1, source_target_pairs={{0,32},{32,64},{64,96},{96,128},{128,160},{160,192},{192,224},{224... | collective-permute-start | bytes 76424 | tf_op jit(solution)/shard_map/ppermute | solution.py:106
  61.2 2.5 %collective-permute-done.4 = f32[6368]{0:T(1024)S(1)} collective-permute-done((f32[6368]{0:T(1024)S(1)}, f32[6368]{0:T(1024)S(1)}, u32[]{:S(2)}, u32[]{:S(2)}) %collective-permute-start.4) | collective-permute-done | bytes 25504 | tf_op jit(solution)/shard_map/ppermute | solution.py:106
  65.8 1.3 copy.102
  70.2 1.6 %slice_bitcast_fusion.1 = f32[2,12,11,12]{0,1,3,2:T(8,128)S(1)} fusion(f32[10,11,12,12]{0,3,2,1:T(8,128)} %copy-done.1), kind=kLoop, calls=%fused_computation.86 | loop fusion | bytes 25344 | tf_op jit(solution)/shard_map/transpose | solution.py:122
  71.8 2.1 %copy.105 = f32[8,12,11,12]{3,2,0,1:T(8,128)S(1)} copy(f32[8,12,11,12]{0,1,3,2:T(8,128)} %slice_bitcast_fusion) | data formatting | bytes 101376 | tf_op jit(solution)/shard_map/transpose | solution.py:122
  90.4 1.4 %convolution_multiply_fusion.2 = f32[48,512]{1,0:T(8,128)} fusion(f32[48,512]{1,0:T(8,128)S(1)} %fusion.34, f32[512,512]{1,0:T(8,128)S(1)} %convolution_multiply_fusion, f32[512]{0:T(512)S(1)} %add.489, f32[48]{0:T(128)S(1)} %copy-done.40), kind=kOutput, calls=%fused_computation.69 | convolution fusion | flops 151068672 | bytes 1247424 | tf_op jit(solution)/shard_map/dot_general | solution.py:235
  95.2 2.3 %collective-permute-start.8 = (f32[288]{0:T(512)S(1)}, f32[288]{0:T(512)S(1)}, u32[]{:S(2)}, u32[]{:S(2)}) collective-permute-start(f32[288]{0:T(512)S(1)} %select_n.435), channel_id=1, source_target_pairs={{0,512},{512,0},{1,513},{513,1},{2,514},{514,2},{3,515},{515,3},{4... | collective-permute-start | bytes 3464 | tf_op jit(solution)/shard_map/ppermute | solution.py:99
  98.3 1.2 collective-permute-done.8
  100.6 8.9 %collective-permute-start.9 = (f32[720]{0:T(1024)S(1)}, f32[720]{0:T(1024)S(1)}, u32[]{:S(2)}, u32[]{:S(2)}) collective-permute-start(f32[720]{0:T(1024)S(1)} %reshape.1006), channel_id=1, source_target_pairs={{0,1},{1,2},{2,3},{3,4},{4,5},{5,6},{6,7},{7,8},{8,9},{9,10},{10,1... | collective-permute-start | bytes 8648 | tf_op jit(solution)/shard_map/ppermute | solution.py:106
  109.8 2.1 %collective-permute-start.10 = (f32[720]{0:T(1024)S(1)}, f32[720]{0:T(1024)S(1)}, u32[]{:S(2)}, u32[]{:S(2)}) collective-permute-start(f32[720]{0:T(1024)S(1)} %reshape.1008), channel_id=1, source_target_pairs={{1,0},{2,1},{3,2},{4,3},{5,4},{6,5},{7,6},{8,7},{9,8},{10,9},{11,1... | collective-permute-start | bytes 8648 | tf_op jit(solution)/shard_map/ppermute | solution.py:107
  112.5 4.4 %collective-permute-done.10 = f32[720]{0:T(1024)S(1)} collective-permute-done((f32[720]{0:T(1024)S(1)}, f32[720]{0:T(1024)S(1)}, u32[]{:S(2)}, u32[]{:S(2)}) %collective-permute-start.10) | collective-permute-done | bytes 2912 | tf_op jit(solution)/shard_map/ppermute | solution.py:107
  117.6 1.9 %collective-permute-start.12 = (f32[2400]{0:T(1024)S(1)}, f32[2400]{0:T(1024)S(1)}, u32[]{:S(2)}, u32[]{:S(2)}) collective-permute-start(f32[2400]{0:T(1024)S(1)} %reshape.1010), channel_id=1, source_target_pairs={{32,0},{64,32},{96,64},{128,96},{160,128},{192,160},{224,192},{256... | collective-permute-start | bytes 28808 | tf_op jit(solution)/shard_map/ppermute | solution.py:107
  119.5 3.4 %collective-permute-start.11 = (f32[2400]{0:T(1024)S(1)}, f32[2400]{0:T(1024)S(1)}, u32[]{:S(2)}, u32[]{:S(2)}) collective-permute-start(f32[2400]{0:T(1024)S(1)} %reshape.1010), channel_id=1, source_target_pairs={{0,32},{32,64},{64,96},{96,128},{128,160},{160,192},{192,224},{224... | collective-permute-start | bytes 28808 | tf_op jit(solution)/shard_map/ppermute | solution.py:106
  123.0 2.2 %collective-permute-done.11 = f32[2400]{0:T(1024)S(1)} collective-permute-done((f32[2400]{0:T(1024)S(1)}, f32[2400]{0:T(1024)S(1)}, u32[]{:S(2)}, u32[]{:S(2)}) %collective-permute-start.11) | collective-permute-done | bytes 9632 | tf_op jit(solution)/shard_map/ppermute | solution.py:106
  (401 shorter events, 62.8 us)
Async XLA Ops:
  5.2 21.5 %collective-permute-start = (f32[480]{0:T(512)S(1)}, f32[480]{0:T(512)S(1)}, u32[]{:S(2)}, u32[]{:S(2)}) collective-permute-start(f32[480]{0:T(512)S(1)} %reshape.978), channel_id=1, source_target_pairs={{0,512},{512,0},{1,513},{513,1},{2,514},{514,2},{3,515},{515,3},{4... | collective-permute-start | bytes 5768 | tf_op jit(solution)/shard_map/ppermute | solution.py:99
  18.4 68.6 %collective-permute-start.7 = (f32[3,4,1,128]{3,1,0,2:T(4,128)}, f32[3,4,1,128]{3,1,0,2:T(4,128)}, u32[]{:S(2)}, u32[]{:S(2)}) collective-permute-start(f32[3,4,1,128]{3,1,0,2:T(4,128)} %slice_select_fusion.1), channel_id=1, source_target_pairs={{0,512},{512,0},{1,513},{513,1},{2,514},{514,2},{3,515},{515,3},{4... | collective-permute-start | bytes 18440 | tf_op jit(solution)/shard_map/ppermute | solution.py:290
  27.0 40.1 %copy-start.17 = (f32[10,3,4,4]{0,3,2,1:T(4,128)}, f32[10,3,4,4]{0,3,2,1:T(4,128)S(1)}, u32[]{:S(2)}) copy-start(f32[10,3,4,4]{0,3,2,1:T(4,128)S(1)} %copy.92) | copy-start | bytes 5764
  27.3 39.8 %copy-start.19 = (f32[10,3,4,4]{0,3,2,1:T(4,128)}, f32[10,3,4,4]{0,3,2,1:T(4,128)S(1)}, u32[]{:S(2)}) copy-start(f32[10,3,4,4]{0,3,2,1:T(4,128)S(1)} %copy.93) | copy-start | bytes 5764
  27.8 16.3 %collective-permute-start.1 = (f32[2976]{0:T(1024)S(1)}, f32[2976]{0:T(1024)S(1)}, u32[]{:S(2)}, u32[]{:S(2)}) collective-permute-start(f32[2976]{0:T(1024)S(1)} %get-tuple-element.134), channel_id=1, source_target_pairs={{0,1},{1,2},{2,3},{3,4},{4,5},{5,6},{6,7},{7,8},{8,9},{9,10},{10,1... | collective-permute-start | bytes 35720 | tf_op jit(solution)/shard_map/ppermute | solution.py:106
  34.4 9.4 %collective-permute-start.2 = (f32[2976]{0:T(1024)S(1)}, f32[2976]{0:T(1024)S(1)}, u32[]{:S(2)}, u32[]{:S(2)}) collective-permute-start(f32[2976]{0:T(1024)S(1)} %get-tuple-element.135), channel_id=1, source_target_pairs={{1,0},{2,1},{3,2},{4,3},{5,4},{6,5},{7,6},{8,7},{9,8},{10,9},{11,1... | collective-permute-start | bytes 35720 | tf_op jit(solution)/shard_map/ppermute | solution.py:107
  46.7 13.6 %collective-permute-start.6 = (f32[1440]{0:T(1024)S(1)}, f32[1440]{0:T(1024)S(1)}, u32[]{:S(2)}, u32[]{:S(2)}) collective-permute-start(f32[1440]{0:T(1024)S(1)} %reshape.992), channel_id=1, source_target_pairs={{64,0},{96,32},{128,64},{160,96},{192,128},{224,160},{256,192},{28... | collective-permute-start | bytes 17288 | tf_op jit(solution)/shard_map/ppermute | solution.py:107
  50.4 9.6 %collective-permute-start.3 = (f32[1440]{0:T(1024)S(1)}, f32[1440]{0:T(1024)S(1)}, u32[]{:S(2)}, u32[]{:S(2)}) collective-permute-start(f32[1440]{0:T(1024)S(1)} %reshape.985), channel_id=1, source_target_pairs={{0,64},{32,96},{64,128},{96,160},{128,192},{160,224},{192,256},{22... | collective-permute-start | bytes 17288 | tf_op jit(solution)/shard_map/ppermute | solution.py:106
  53.3 11.1 %collective-permute-start.5 = (f32[6368]{0:T(1024)S(1)}, f32[6368]{0:T(1024)S(1)}, u32[]{:S(2)}, u32[]{:S(2)}) collective-permute-start(f32[6368]{0:T(1024)S(1)} %get-tuple-element.120), channel_id=1, source_target_pairs={{32,0},{64,32},{96,64},{128,96},{160,128},{192,160},{224,192},{256... | collective-permute-start | bytes 76424 | tf_op jit(solution)/shard_map/ppermute | solution.py:107
  57.9 5.8 %collective-permute-start.4 = (f32[6368]{0:T(1024)S(1)}, f32[6368]{0:T(1024)S(1)}, u32[]{:S(2)}, u32[]{:S(2)}) collective-permute-start(f32[6368]{0:T(1024)S(1)} %get-tuple-element.121), channel_id=1, source_target_pairs={{0,32},{32,64},{64,96},{96,128},{128,160},{160,192},{192,224},{224... | collective-permute-start | bytes 76424 | tf_op jit(solution)/shard_map/ppermute | solution.py:106
  95.1 16.8 %copy-start.42 = (pred[90]{0:T(512)(128)(4,1)S(1)}, pred[90]{0:T(512)(128)(4,1)}, u32[]{:S(2)}) copy-start(pred[90]{0:T(512)(128)(4,1)} %lt.220) | copy-start | bytes 274
  95.1 16.8 %copy-start.43 = (pred[90]{0:T(512)(128)(4,1)S(1)}, pred[90]{0:T(512)(128)(4,1)}, u32[]{:S(2)}) copy-start(pred[90]{0:T(512)(128)(4,1)} %lt.217) | copy-start | bytes 274
  95.1 16.8 %copy-start.44 = (pred[90]{0:T(512)(128)(4,1)S(1)}, pred[90]{0:T(512)(128)(4,1)}, u32[]{:S(2)}) copy-start(pred[90]{0:T(512)(128)(4,1)} %gt.67) | copy-start | bytes 274
  95.1 16.8 %copy-start.45 = (pred[90]{0:T(512)(128)(4,1)S(1)}, pred[90]{0:T(512)(128)(4,1)}, u32[]{:S(2)}) copy-start(pred[90]{0:T(512)(128)(4,1)} %gt.65) | copy-start | bytes 274
  95.1 16.8 %copy-start.52 = (pred[10]{0:T(512)(128)(4,1)S(1)}, pred[10]{0:T(512)(128)(4,1)}, u32[]{:S(2)}) copy-start(pred[10]{0:T(512)(128)(4,1)} %get-tuple-element.184) | copy-start | bytes 34
  95.1 16.8 %copy-start.53 = (pred[10]{0:T(512)(128)(4,1)S(1)}, pred[10]{0:T(512)(128)(4,1)}, u32[]{:S(2)}) copy-start(pred[10]{0:T(512)(128)(4,1)} %get-tuple-element.185) | copy-start | bytes 34
  95.2 4.3 %collective-permute-start.8 = (f32[288]{0:T(512)S(1)}, f32[288]{0:T(512)S(1)}, u32[]{:S(2)}, u32[]{:S(2)}) collective-permute-start(f32[288]{0:T(512)S(1)} %select_n.435), channel_id=1, source_target_pairs={{0,512},{512,0},{1,513},{513,1},{2,514},{514,2},{3,515},{515,3},{4... | collective-permute-start | bytes 3464 | tf_op jit(solution)/shard_map/ppermute | solution.py:99
  100.3 22.6 %copy-start.51 = (pred[90]{0:T(512)(128)(4,1)S(1)}, pred[90]{0:T(512)(128)(4,1)}, u32[]{:S(2)}) copy-start(pred[90]{0:T(512)(128)(4,1)} %and.235) | copy-start | bytes 274
  100.3 22.6 %copy-start.58 = (pred[10]{0:T(512)(128)(4,1)S(1)}, pred[10]{0:T(512)(128)(4,1)}, u32[]{:S(2)}) copy-start(pred[10]{0:T(512)(128)(4,1)} %get-tuple-element.186) | copy-start | bytes 34
  100.3 22.6 %copy-start.59 = (pred[10]{0:T(512)(128)(4,1)S(1)}, pred[10]{0:T(512)(128)(4,1)}, u32[]{:S(2)}) copy-start(pred[10]{0:T(512)(128)(4,1)} %get-tuple-element.187) | copy-start | bytes 34
  100.6 11.6 %collective-permute-start.9 = (f32[720]{0:T(1024)S(1)}, f32[720]{0:T(1024)S(1)}, u32[]{:S(2)}, u32[]{:S(2)}) collective-permute-start(f32[720]{0:T(1024)S(1)} %reshape.1006), channel_id=1, source_target_pairs={{0,1},{1,2},{2,3},{3,4},{4,5},{5,6},{6,7},{7,8},{8,9},{9,10},{10,1... | collective-permute-start | bytes 8648 | tf_op jit(solution)/shard_map/ppermute | solution.py:106
  109.8 7.0 %collective-permute-start.10 = (f32[720]{0:T(1024)S(1)}, f32[720]{0:T(1024)S(1)}, u32[]{:S(2)}, u32[]{:S(2)}) collective-permute-start(f32[720]{0:T(1024)S(1)} %reshape.1008), channel_id=1, source_target_pairs={{1,0},{2,1},{3,2},{4,3},{5,4},{6,5},{7,6},{8,7},{9,8},{10,9},{11,1... | collective-permute-start | bytes 8648 | tf_op jit(solution)/shard_map/ppermute | solution.py:107
  117.6 8.0 %collective-permute-start.12 = (f32[2400]{0:T(1024)S(1)}, f32[2400]{0:T(1024)S(1)}, u32[]{:S(2)}, u32[]{:S(2)}) collective-permute-start(f32[2400]{0:T(1024)S(1)} %reshape.1010), channel_id=1, source_target_pairs={{32,0},{64,32},{96,64},{128,96},{160,128},{192,160},{224,192},{256... | collective-permute-start | bytes 28808 | tf_op jit(solution)/shard_map/ppermute | solution.py:107
  119.5 5.7 %collective-permute-start.11 = (f32[2400]{0:T(1024)S(1)}, f32[2400]{0:T(1024)S(1)}, u32[]{:S(2)}, u32[]{:S(2)}) collective-permute-start(f32[2400]{0:T(1024)S(1)} %reshape.1010), channel_id=1, source_target_pairs={{0,32},{32,64},{64,96},{96,128},{128,160},{160,192},{192,224},{224... | collective-permute-start | bytes 28808 | tf_op jit(solution)/shard_map/ppermute | solution.py:106
  (49 other events, 160.2 us)

commit v5 on v3

--- a/solution.py
+++ b/solution.py
@@ -162,6 +162,19 @@
 
 
 ONEHOT = _onehot_tables()
+
+
+def _restrict_table():
+    points = np.array(GLL_POINTS, np.float32)
+    linear = np.stack([(1.0 - points) * 0.5, (1.0 + points) * 0.5]).astype(np.float32)
+    return (
+        linear.T[:, None, None, :, None, None]
+        * linear.T[None, :, None, None, :, None]
+        * linear.T[None, None, :, None, None, :]
+    ).reshape(DEG1**3, 8)
+
+
+RESTRICT = _restrict_table()
 
 
 def face_select():
@@ -224,13 +237,7 @@
     spectrum = (
         eigenvalues[:, None, None] + eigenvalues[None, :, None] + eigenvalues[None, None, :]
     ).reshape(-1)
-    points = jnp.array(np.array(GLL_POINTS), jnp.float32)
-    linear = jnp.stack([(1.0 - points) * 0.5, (1.0 + points) * 0.5])
-    restrict_table = (
-        linear.T[:, None, None, :, None, None]
-        * linear.T[None, :, None, None, :, None]
-        * linear.T[None, None, :, None, None, :]
-    ).reshape(DEG1**3, 8)
+    restrict_table = jnp.asarray(RESTRICT)
     return (eigen_table, spectrum, restrict_table)
 
 

time: 110 us -> 112 us (1.018)
  matrix products: 18.9 us -> 20.8 us
    mul x2 -> x0, other arithmetic: 1.64 us -> none  [build_tables(): linear.T[:, None, None, :, None, None]]
    add x2, other arithmetic: 0.15 us -> 1.53 us  [build_tables(): eigenvalues[:, None, None] + eigenvalues[None, :, None]]
  transfers between devices with their start and end apart: 15 -> 15, of which waited for: 7 -> 7; matrix products, arithmetic and copies ran while one was open for 14% -> 17% of each run, Pallas kernels for 0% -> 0%
where the time goes in v5:
time: 112 us
  starting transfers between devices  47.5 us (42%)
  waiting for transfers between devices  25.9 us (23%)
  matrix products  20.8 us (19%)
  local copies, waits for them, and re-layouts  9.37 us (8%)
  other arithmetic  6.95 us (6%)
    ppermute x4, starting transfers between devices, halo_box(): lax.ppermute(lo_piece, axis, [(i, i + 1) for i in range(count - 1)])  16.1 us
    ppermute x4, waiting for transfers between devices, halo_box(): lax.ppermute(hi_piece, axis, [(i + 1, i) for i in range(count - 1)])  11.8 us
    ppermute x4, starting transfers between devices, halo_box(): lax.ppermute(hi_piece, axis, [(i + 1, i) for i in range(count - 1)])  10.3 us
    ppermute x2, starting transfers between devices, fine_face_term(): from_below = lax.ppermute(top, axis, [(i, i + 1) for i in range(count - 1)])  8.02 us
    ppermute x2, starting transfers between devices, fine_face_term(): lax.ppermute(bottom, axis, [(i + 1, i) for i in range(count - 1)])  6.52 us
    ppermute x2, waiting for transfers between devices, halo_box(): lax.ppermute(jnp.where(me == 0, lo_piece, hi_piece), axis, [(0, 1), (1, 0)])  6.14 us
    dot_general x3, matrix products, eigen_apply(): jnp.dot(flat, eigen_table, precision=HIGHEST, preferred_element_type=jnp....  5.47 us
    ppermute x2, starting transfers between devices, halo_box(): lax.ppermute(jnp.where(me == 0, lo_piece, hi_piece), axis, [(0, 1), (1, 0)])  4.4 us
  transfers between devices with their start and end apart: 15, of which 7 were waited for; matrix products, arithmetic and copies ran while one was open for 17% of the time, Pallas kernels for 0%

profile of v5, /device:TPU:827, one launch (start us, length us, event | category | flops | bytes accessed | tf_op | source)
XLA Modules:
  0.0 111.5 jit_solution(10799489087879206932)
XLA Ops:
  3.1 3.4 %collective-permute-start.1 = (f32[10,3,4,4]{0,3,2,1:T(4,128)S(1)}, f32[10,3,4,4]{0,3,2,1:T(4,128)S(1)}, u32[]{:S(2)}, u32[]{:S(2)}) collective-permute-start(f32[10,3,4,4]{0,3,2,1:T(4,128)S(1)} %pad_maximum_fusion.4), channel_id=1, source_target_pairs={{32,0},{64,32},{96,64},{128,96},{160,128},{192,160},{224,192},{256... | collective-permute-start | bytes 5768 | tf_op jit(solution)/shard_map/ppermute | solution.py:82
  6.5 1.9 %collective-permute-start = (f32[10,3,4,4]{0,3,2,1:T(4,128)S(1)}, f32[10,3,4,4]{0,3,2,1:T(4,128)S(1)}, u32[]{:S(2)}, u32[]{:S(2)}) collective-permute-start(f32[10,3,4,4]{0,3,2,1:T(4,128)S(1)} %pad_maximum_fusion.4), channel_id=1, source_target_pairs={{0,32},{32,64},{64,96},{96,128},{128,160},{160,192},{192,224},{224... | collective-permute-start | bytes 5768 | tf_op jit(solution)/shard_map/ppermute | solution.py:81
  20.4 4.4 %collective-permute-start.2 = (f32[10,9,3,4]{0,3,2,1:T(4,128)S(1)}, f32[10,9,3,4]{0,3,2,1:T(4,128)S(1)}, u32[]{:S(2)}, u32[]{:S(2)}) collective-permute-start(f32[10,9,3,4]{0,3,2,1:T(4,128)S(1)} %get-tuple-element.34), channel_id=1, source_target_pairs={{0,1},{1,2},{2,3},{3,4},{4,5},{5,6},{6,7},{7,8},{8,9},{9,10},{10,1... | collective-permute-start | bytes 12968 | tf_op jit(solution)/shard_map/ppermute | solution.py:81
  24.8 1.9 %collective-permute-start.3 = (f32[10,9,3,4]{0,3,2,1:T(4,128)S(1)}, f32[10,9,3,4]{0,3,2,1:T(4,128)S(1)}, u32[]{:S(2)}, u32[]{:S(2)}) collective-permute-start(f32[10,9,3,4]{0,3,2,1:T(4,128)S(1)} %get-tuple-element.35), channel_id=1, source_target_pairs={{1,0},{2,1},{3,2},{4,3},{5,4},{6,5},{7,6},{8,7},{9,8},{10,9},{11,1... | collective-permute-start | bytes 12968 | tf_op jit(solution)/shard_map/ppermute | solution.py:82
  26.8 6.5 %collective-permute-done.3 = f32[10,9,3,4]{0,3,2,1:T(4,128)S(1)} collective-permute-done((f32[10,9,3,4]{0,3,2,1:T(4,128)S(1)}, f32[10,9,3,4]{0,3,2,1:T(4,128)S(1)}, u32[]{:S(2)}, u32[]{:S(2)}) %collective-permute-start.3) | collective-permute-done | bytes 4352 | tf_op jit(solution)/shard_map/ppermute | solution.py:82
  33.5 2.3 %collective-permute-start.4 = (f32[10,9,10,3]{0,3,2,1:T(4,128)S(1)}, f32[10,9,10,3]{0,3,2,1:T(4,128)S(1)}, u32[]{:S(2)}, u32[]{:S(2)}) collective-permute-start(f32[10,9,10,3]{0,3,2,1:T(4,128)S(1)} %slice_select_fusion.1), channel_id=1, source_target_pairs={{0,512},{512,0},{1,513},{513,1},{2,514},{514,2},{3,515},{515,3},{4... | collective-permute-start | bytes 32408 | tf_op jit(solution)/shard_map/ppermute | solution.py:76
  36.5 3.2 %collective-permute-done.4 = f32[10,9,10,3]{0,3,2,1:T(4,128)S(1)} collective-permute-done((f32[10,9,10,3]{0,3,2,1:T(4,128)S(1)}, f32[10,9,10,3]{0,3,2,1:T(4,128)S(1)}, u32[]{:S(2)}, u32[]{:S(2)}) %collective-permute-start.4) | collective-permute-done | bytes 10832 | tf_op jit(solution)/shard_map/ppermute | solution.py:76
  45.3 2.2 %fusion.24 = f32[3,4,4,6,128]{4,2,3,1,0:T(4,128)S(1)} fusion(s32[6,128]{1,0:T(8,128)S(1)} %get-tuple-element.145, s32[6,128]{1,0:T(8,128)S(1)} %get-tuple-element.148, s32[512]{0:T(512)S(1)} %get-tuple-element.141, s32[512]{0:T(512)S(1)} %get-tuple-element.143, s32[512]{0:T(512)S(1)} %get-tuple-element.140, s32[512]{0:T(512)S(1)} %get-tuple-element.152, ...), kind=kOutput, calls=%fused_computation.60 | convolution fusion | flops 246153216 | bytes 273408 | tf_op jit(solution)/shard_map/dot_general | solution.py:193
  47.5 4.6 %collective-permute-start.6 = (f32[1,4,4,128]{3,2,1,0:T(4,128)S(1)}, f32[1,4,4,128]{3,2,1,0:T(4,128)S(1)}, u32[]{:S(2)}, u32[]{:S(2)}) collective-permute-start(f32[1,4,4,128]{3,2,1,0:T(4,128)S(1)} %get-tuple-element.30), channel_id=1, source_target_pairs={{32,0},{64,32},{96,64},{128,96},{160,128},{192,160},{224,192},{256... | collective-permute-start | bytes 24584 | tf_op jit(solution)/shard_map/ppermute | solution.py:211
  52.1 1.9 %collective-permute-start.5 = (f32[1,4,4,128]{3,2,1,0:T(4,128)S(1)}, f32[1,4,4,128]{3,2,1,0:T(4,128)S(1)}, u32[]{:S(2)}, u32[]{:S(2)}) collective-permute-start(f32[1,4,4,128]{3,2,1,0:T(4,128)S(1)} %get-tuple-element.31), channel_id=1, source_target_pairs={{0,32},{32,64},{64,96},{96,128},{128,160},{160,192},{192,224},{224... | collective-permute-start | bytes 24584 | tf_op jit(solution)/shard_map/ppermute | solution.py:210
  58.0 6.1 %collective-permute-start.7 = (f32[3,1,4,128]{3,2,0,1:T(4,128)S(1)}, f32[3,1,4,128]{3,2,0,1:T(4,128)S(1)}, u32[]{:S(2)}, u32[]{:S(2)}) collective-permute-start(f32[3,1,4,128]{3,2,0,1:T(4,128)S(1)} %slice_bitcast_fusion.9), channel_id=1, source_target_pairs={{0,1},{1,2},{2,3},{3,4},{4,5},{5,6},{6,7},{7,8},{8,9},{9,10},{10,1... | collective-permute-start | bytes 18440 | tf_op jit(solution)/shard_map/ppermute | solution.py:210
  64.1 1.9 %collective-permute-start.8 = (f32[3,1,4,128]{3,2,1,0:T(4,128)S(1)}, f32[3,1,4,128]{3,2,1,0:T(4,128)S(1)}, u32[]{:S(2)}, u32[]{:S(2)}) collective-permute-start(f32[3,1,4,128]{3,2,1,0:T(4,128)S(1)} %slice.520), channel_id=1, source_target_pairs={{1,0},{2,1},{3,2},{4,3},{5,4},{6,5},{7,6},{8,7},{9,8},{10,9},{11,1... | collective-permute-start | bytes 18440 | tf_op jit(solution)/shard_map/ppermute | solution.py:211
  66.2 2.1 %collective-permute-start.9 = (f32[3,4,1,128]{3,1,0,2:T(4,128)S(1)}, f32[3,4,1,128]{3,1,0,2:T(4,128)S(1)}, u32[]{:S(2)}, u32[]{:S(2)}) collective-permute-start(f32[3,4,1,128]{3,1,0,2:T(4,128)S(1)} %slice_select_fusion.2), channel_id=1, source_target_pairs={{0,512},{512,0},{1,513},{513,1},{2,514},{514,2},{3,515},{515,3},{4... | collective-permute-start | bytes 18440 | tf_op jit(solution)/shard_map/ppermute | solution.py:205
  68.3 3.7 %collective-permute-done.8 = f32[3,1,4,128]{3,2,1,0:T(4,128)S(1)} collective-permute-done((f32[3,1,4,128]{3,2,1,0:T(4,128)S(1)}, f32[3,1,4,128]{3,2,1,0:T(4,128)S(1)}, u32[]{:S(2)}, u32[]{:S(2)}) %collective-permute-start.8) | collective-permute-done | bytes 6176 | tf_op jit(solution)/shard_map/ppermute | solution.py:211
  72.3 2.0 %fusion.45 = f32[3,4,4,512]{3,2,1,0:T(4,128)S(1)} fusion(f32[3,4,4,512]{3,2,1,0:T(4,128)S(1)} %copy-done.4, f32[3,4,4,512]{3,2,1,0:T(4,128)S(1)} %reshape.540, s32[768]{0:T(1024)S(1)} %get-tuple-element.155, s32[768]{0:T(1024)S(1)} %get-tuple-element.156, s32[512]{0:T(512)S(1)} %get-tuple-element.141, s32[512]{0:T(512)S(1)} %get-tuple-element.143, ...), kind=kOutput, calls=%fused_computation.82 | convolution fusion | flops 246202368 | bytes 470016 | tf_op jit(solution)/shard_map/dot_general | solution.py:220
  74.7 3.1 %collective-permute-start.11 = (f32[8,3,4,4]{0,3,2,1:T(4,128)S(1)}, f32[8,3,4,4]{0,3,2,1:T(4,128)S(1)}, u32[]{:S(2)}, u32[]{:S(2)}) collective-permute-start(f32[8,3,4,4]{0,3,2,1:T(4,128)S(1)} %fusion.243), channel_id=1, source_target_pairs={{32,0},{64,32},{96,64},{128,96},{160,128},{192,160},{224,192},{256... | collective-permute-start | bytes 4616 | tf_op jit(solution)/shard_map/ppermute | solution.py:82
  77.8 2.2 %collective-permute-start.10 = (f32[8,3,4,4]{0,3,2,1:T(4,128)S(1)}, f32[8,3,4,4]{0,3,2,1:T(4,128)S(1)}, u32[]{:S(2)}, u32[]{:S(2)}) collective-permute-start(f32[8,3,4,4]{0,3,2,1:T(4,128)S(1)} %fusion.243), channel_id=1, source_target_pairs={{0,32},{32,64},{64,96},{96,128},{128,160},{160,192},{192,224},{224... | collective-permute-start | bytes 4616 | tf_op jit(solution)/shard_map/ppermute | solution.py:81
  80.0 3.5 %collective-permute-done.10 = f32[8,3,4,4]{0,3,2,1:T(4,128)S(1)} collective-permute-done((f32[8,3,4,4]{0,3,2,1:T(4,128)S(1)}, f32[8,3,4,4]{0,3,2,1:T(4,128)S(1)}, u32[]{:S(2)}, u32[]{:S(2)}) %collective-permute-start.10) | collective-permute-done | bytes 1568 | tf_op jit(solution)/shard_map/ppermute | solution.py:81
  83.6 7.6 %collective-permute-start.12 = (f32[8,9,3,4]{0,3,2,1:T(4,128)S(1)}, f32[8,9,3,4]{0,3,2,1:T(4,128)S(1)}, u32[]{:S(2)}, u32[]{:S(2)}) collective-permute-start(f32[8,9,3,4]{0,3,2,1:T(4,128)S(1)} %get-tuple-element.32), channel_id=1, source_target_pairs={{0,1},{1,2},{2,3},{3,4},{4,5},{5,6},{6,7},{7,8},{8,9},{9,10},{10,1... | collective-permute-start | bytes 10376 | tf_op jit(solution)/shard_map/ppermute | solution.py:81
  91.2 1.9 %collective-permute-start.13 = (f32[8,9,3,4]{0,3,2,1:T(4,128)S(1)}, f32[8,9,3,4]{0,3,2,1:T(4,128)S(1)}, u32[]{:S(2)}, u32[]{:S(2)}) collective-permute-start(f32[8,9,3,4]{0,3,2,1:T(4,128)S(1)} %get-tuple-element.33), channel_id=1, source_target_pairs={{1,0},{2,1},{3,2},{4,3},{5,4},{6,5},{7,6},{8,7},{9,8},{10,9},{11,1... | collective-permute-start | bytes 10376 | tf_op jit(solution)/shard_map/ppermute | solution.py:82
  93.1 1.8 %convolution_multiply_fusion.2 = f32[48,512]{0,1:T(8,128)S(1)} fusion(f32[48,512]{1,0:T(8,128)S(1)} %reshape.541, f32[512,512]{1,0:T(8,128)S(1)} %convolution_multiply_fusion, f32[512]{0:T(512)S(1)} %add.353, f32[48]{0:T(128)S(1)} %mul.588), kind=kOutput, calls=%fused_computation.74 | convolution fusion | flops 151068672 | bytes 1247424 | tf_op jit(solution)/shard_map/dot_general | solution.py:246
  95.0 5.3 %collective-permute-done.13 = f32[8,9,3,4]{0,3,2,1:T(4,128)S(1)} collective-permute-done((f32[8,9,3,4]{0,3,2,1:T(4,128)S(1)}, f32[8,9,3,4]{0,3,2,1:T(4,128)S(1)}, u32[]{:S(2)}, u32[]{:S(2)}) %collective-permute-start.13) | collective-permute-done | bytes 3488 | tf_op jit(solution)/shard_map/ppermute | solution.py:82
  100.4 2.1 %collective-permute-start.14 = (f32[8,9,10,3]{0,3,2,1:T(4,128)S(1)}, f32[8,9,10,3]{0,3,2,1:T(4,128)S(1)}, u32[]{:S(2)}, u32[]{:S(2)}) collective-permute-start(f32[8,9,10,3]{0,3,2,1:T(4,128)S(1)} %slice_select_fusion), channel_id=1, source_target_pairs={{0,512},{512,0},{1,513},{513,1},{2,514},{514,2},{3,515},{515,3},{4... | collective-permute-start | bytes 25928 | tf_op jit(solution)/shard_map/ppermute | solution.py:76
  103.7 2.9 %collective-permute-done.14 = f32[8,9,10,3]{0,3,2,1:T(4,128)S(1)} collective-permute-done((f32[8,9,10,3]{0,3,2,1:T(4,128)S(1)}, f32[8,9,10,3]{0,3,2,1:T(4,128)S(1)}, u32[]{:S(2)}, u32[]{:S(2)}) %collective-permute-start.14) | collective-permute-done | bytes 8672 | tf_op jit(solution)/shard_map/ppermute | solution.py:76
  (182 shorter events, 31.7 us)
Async XLA Ops:
  0.0 12.0 %copy-start = (f32[8,8]{1,0:T(8,128)S(1)}, f32[8,8]{1,0:T(8,128)}, u32[]{:S(2)}) copy-start(f32[8,8]{1,0:T(8,128)} %param.12) | copy-start | bytes 772
  0.0 13.3 %copy-start.2 = (f32[512,8]{1,0:T(8,128)S(1)}, f32[512,8]{1,0:T(8,128)}, u32[]{:S(2)}) copy-start(f32[512,8]{1,0:T(8,128)} %constant.193.clone) | copy-start | bytes 49156
  0.0 13.7 %copy-start.1 = (f32[512,8]{1,0:T(8,128)S(1)}, f32[512,8]{1,0:T(8,128)}, u32[]{:S(2)}) copy-start(f32[512,8]{1,0:T(8,128)} %constant.194.clone) | copy-start | bytes 49156
  3.0 11.1 %copy-start.3 = (f32[512,8]{1,0:T(8,128)S(1)}, f32[512,8]{1,0:T(8,128)}, u32[]{:S(2)}) copy-start(f32[512,8]{1,0:T(8,128)} %constant.192.clone) | copy-start | bytes 49156
  3.1 17.1 %collective-permute-start.1 = (f32[10,3,4,4]{0,3,2,1:T(4,128)S(1)}, f32[10,3,4,4]{0,3,2,1:T(4,128)S(1)}, u32[]{:S(2)}, u32[]{:S(2)}) collective-permute-start(f32[10,3,4,4]{0,3,2,1:T(4,128)S(1)} %pad_maximum_fusion.4), channel_id=1, source_target_pairs={{32,0},{64,32},{96,64},{128,96},{160,128},{192,160},{224,192},{256... | collective-permute-start | bytes 5768 | tf_op jit(solution)/shard_map/ppermute | solution.py:82
  6.5 13.8 %collective-permute-start = (f32[10,3,4,4]{0,3,2,1:T(4,128)S(1)}, f32[10,3,4,4]{0,3,2,1:T(4,128)S(1)}, u32[]{:S(2)}, u32[]{:S(2)}) collective-permute-start(f32[10,3,4,4]{0,3,2,1:T(4,128)S(1)} %pad_maximum_fusion.4), channel_id=1, source_target_pairs={{0,32},{32,64},{64,96},{96,128},{128,160},{160,192},{192,224},{224... | collective-permute-start | bytes 5768 | tf_op jit(solution)/shard_map/ppermute | solution.py:81
  18.9 1.3 %copy-start.6 = (s32[3,4,4]{2,1,0:T(4,128)S(1)}, s32[3,4,4]{2,1,0:T(4,128)}, u32[]{:S(2)}) copy-start(s32[3,4,4]{2,1,0:T(4,128)} %param.11) | copy-start | bytes 580
  20.4 6.4 %collective-permute-start.2 = (f32[10,9,3,4]{0,3,2,1:T(4,128)S(1)}, f32[10,9,3,4]{0,3,2,1:T(4,128)S(1)}, u32[]{:S(2)}, u32[]{:S(2)}) collective-permute-start(f32[10,9,3,4]{0,3,2,1:T(4,128)S(1)} %get-tuple-element.34), channel_id=1, source_target_pairs={{0,1},{1,2},{2,3},{3,4},{4,5},{5,6},{6,7},{7,8},{8,9},{9,10},{10,1... | collective-permute-start | bytes 12968 | tf_op jit(solution)/shard_map/ppermute | solution.py:81
  24.8 8.5 %collective-permute-start.3 = (f32[10,9,3,4]{0,3,2,1:T(4,128)S(1)}, f32[10,9,3,4]{0,3,2,1:T(4,128)S(1)}, u32[]{:S(2)}, u32[]{:S(2)}) collective-permute-start(f32[10,9,3,4]{0,3,2,1:T(4,128)S(1)} %get-tuple-element.35), channel_id=1, source_target_pairs={{1,0},{2,1},{3,2},{4,3},{5,4},{6,5},{7,6},{8,7},{9,8},{10,9},{11,1... | collective-permute-start | bytes 12968 | tf_op jit(solution)/shard_map/ppermute | solution.py:82
  33.5 6.3 %collective-permute-start.4 = (f32[10,9,10,3]{0,3,2,1:T(4,128)S(1)}, f32[10,9,10,3]{0,3,2,1:T(4,128)S(1)}, u32[]{:S(2)}, u32[]{:S(2)}) collective-permute-start(f32[10,9,10,3]{0,3,2,1:T(4,128)S(1)} %slice_select_fusion.1), channel_id=1, source_target_pairs={{0,512},{512,0},{1,513},{513,1},{2,514},{514,2},{3,515},{515,3},{4... | collective-permute-start | bytes 32408 | tf_op jit(solution)/shard_map/ppermute | solution.py:76
  43.7 1.3 %copy-start.5 = (f32[512,8,1,1]{0,1,3,2:T(8,128)S(1)}, f32[512,8,1,1]{0,1,3,2:T(8,128)}, u32[]{:S(2)}) copy-start(f32[512,8,1,1]{0,1,3,2:T(8,128)} %constant.271) | copy-start | bytes 49156
  47.5 10.3 %collective-permute-start.6 = (f32[1,4,4,128]{3,2,1,0:T(4,128)S(1)}, f32[1,4,4,128]{3,2,1,0:T(4,128)S(1)}, u32[]{:S(2)}, u32[]{:S(2)}) collective-permute-start(f32[1,4,4,128]{3,2,1,0:T(4,128)S(1)} %get-tuple-element.30), channel_id=1, source_target_pairs={{32,0},{64,32},{96,64},{128,96},{160,128},{192,160},{224,192},{256... | collective-permute-start | bytes 24584 | tf_op jit(solution)/shard_map/ppermute | solution.py:211
  52.1 5.6 %collective-permute-start.5 = (f32[1,4,4,128]{3,2,1,0:T(4,128)S(1)}, f32[1,4,4,128]{3,2,1,0:T(4,128)S(1)}, u32[]{:S(2)}, u32[]{:S(2)}) collective-permute-start(f32[1,4,4,128]{3,2,1,0:T(4,128)S(1)} %get-tuple-element.31), channel_id=1, source_target_pairs={{0,32},{32,64},{64,96},{96,128},{128,160},{160,192},{192,224},{224... | collective-permute-start | bytes 24584 | tf_op jit(solution)/shard_map/ppermute | solution.py:210
  55.9 16.4 %copy-start.4 = (f32[3,4,4,512]{3,2,1,0:T(4,128)S(1)}, f32[3,4,4,512]{3,2,1,0:T(4,128)}, u32[]{:S(2)}) copy-start(f32[3,4,4,512]{3,2,1,0:T(4,128)} %param.9) | copy-start | bytes 294916
  58.0 10.2 %collective-permute-start.7 = (f32[3,1,4,128]{3,2,0,1:T(4,128)S(1)}, f32[3,1,4,128]{3,2,0,1:T(4,128)S(1)}, u32[]{:S(2)}, u32[]{:S(2)}) collective-permute-start(f32[3,1,4,128]{3,2,0,1:T(4,128)S(1)} %slice_bitcast_fusion.9), channel_id=1, source_target_pairs={{0,1},{1,2},{2,3},{3,4},{4,5},{5,6},{6,7},{7,8},{8,9},{9,10},{10,1... | collective-permute-start | bytes 18440 | tf_op jit(solution)/shard_map/ppermute | solution.py:210
  64.1 8.0 %collective-permute-start.8 = (f32[3,1,4,128]{3,2,1,0:T(4,128)S(1)}, f32[3,1,4,128]{3,2,1,0:T(4,128)S(1)}, u32[]{:S(2)}, u32[]{:S(2)}) collective-permute-start(f32[3,1,4,128]{3,2,1,0:T(4,128)S(1)} %slice.520), channel_id=1, source_target_pairs={{1,0},{2,1},{3,2},{4,3},{5,4},{6,5},{7,6},{8,7},{9,8},{10,9},{11,1... | collective-permute-start | bytes 18440 | tf_op jit(solution)/shard_map/ppermute | solution.py:211
  66.2 6.0 %collective-permute-start.9 = (f32[3,4,1,128]{3,1,0,2:T(4,128)S(1)}, f32[3,4,1,128]{3,1,0,2:T(4,128)S(1)}, u32[]{:S(2)}, u32[]{:S(2)}) collective-permute-start(f32[3,4,1,128]{3,1,0,2:T(4,128)S(1)} %slice_select_fusion.2), channel_id=1, source_target_pairs={{0,512},{512,0},{1,513},{513,1},{2,514},{514,2},{3,515},{515,3},{4... | collective-permute-start | bytes 18440 | tf_op jit(solution)/shard_map/ppermute | solution.py:205
  74.7 5.3 %collective-permute-start.11 = (f32[8,3,4,4]{0,3,2,1:T(4,128)S(1)}, f32[8,3,4,4]{0,3,2,1:T(4,128)S(1)}, u32[]{:S(2)}, u32[]{:S(2)}) collective-permute-start(f32[8,3,4,4]{0,3,2,1:T(4,128)S(1)} %fusion.243), channel_id=1, source_target_pairs={{32,0},{64,32},{96,64},{128,96},{160,128},{192,160},{224,192},{256... | collective-permute-start | bytes 4616 | tf_op jit(solution)/shard_map/ppermute | solution.py:82
  77.8 5.8 %collective-permute-start.10 = (f32[8,3,4,4]{0,3,2,1:T(4,128)S(1)}, f32[8,3,4,4]{0,3,2,1:T(4,128)S(1)}, u32[]{:S(2)}, u32[]{:S(2)}) collective-permute-start(f32[8,3,4,4]{0,3,2,1:T(4,128)S(1)} %fusion.243), channel_id=1, source_target_pairs={{0,32},{32,64},{64,96},{96,128},{128,160},{160,192},{192,224},{224... | collective-permute-start | bytes 4616 | tf_op jit(solution)/shard_map/ppermute | solution.py:81
  83.6 11.3 %collective-permute-start.12 = (f32[8,9,3,4]{0,3,2,1:T(4,128)S(1)}, f32[8,9,3,4]{0,3,2,1:T(4,128)S(1)}, u32[]{:S(2)}, u32[]{:S(2)}) collective-permute-start(f32[8,9,3,4]{0,3,2,1:T(4,128)S(1)} %get-tuple-element.32), channel_id=1, source_target_pairs={{0,1},{1,2},{2,3},{3,4},{4,5},{5,6},{6,7},{7,8},{8,9},{9,10},{10,1... | collective-permute-start | bytes 10376 | tf_op jit(solution)/shard_map/ppermute | solution.py:81
  91.2 9.1 %collective-permute-start.13 = (f32[8,9,3,4]{0,3,2,1:T(4,128)S(1)}, f32[8,9,3,4]{0,3,2,1:T(4,128)S(1)}, u32[]{:S(2)}, u32[]{:S(2)}) collective-permute-start(f32[8,9,3,4]{0,3,2,1:T(4,128)S(1)} %get-tuple-element.33), channel_id=1, source_target_pairs={{1,0},{2,1},{3,2},{4,3},{5,4},{6,5},{7,6},{8,7},{9,8},{10,9},{11,1... | collective-permute-start | bytes 10376 | tf_op jit(solution)/shard_map/ppermute | solution.py:82
  100.4 6.3 %collective-permute-start.14 = (f32[8,9,10,3]{0,3,2,1:T(4,128)S(1)}, f32[8,9,10,3]{0,3,2,1:T(4,128)S(1)}, u32[]{:S(2)}, u32[]{:S(2)}) collective-permute-start(f32[8,9,10,3]{0,3,2,1:T(4,128)S(1)} %slice_select_fusion), channel_id=1, source_target_pairs={{0,512},{512,0},{1,513},{513,1},{2,514},{514,2},{3,515},{515,3},{4... | collective-permute-start | bytes 25928 | tf_op jit(solution)/shard_map/ppermute | solution.py:76
